TPU v7x, 32 devices: a whole 2x2x4 slice. The times are simulated.
32 devices in a mesh: swath: 2 (over y), sub: 4 (over z), beam: 2 (over x), half: 2 (over core).
Axes of the slice: x: 2, y: 2, z: 4, core: 2. Of those that a mesh axis runs over, the one named last changes fastest.
Arguments:
- images: bfloat16 [4, 2, 2048, 1024], P('sub', None, ('swath', 'half'), 'beam'), parts along dimension 2, may hold values from -6 to 6
- offsets: float32 [4], replicated, may hold values from 3840 to 4505
- owners: int32 [2, 4], replicated, may hold values from 0 to 3, each once within a row
Outputs:
- sectors: bfloat16 [8, 1, 2, 512, 2048], P(('sub', 'beam'), None, None, None, ('swath', 'half')), parts along dimension 4
There are 2 independent parts, one for each index of `swath`. A program takes and returns all parts, laid end to end along the dimension named above; an argument that names none is the same for every part. Nothing has to cross between parts.
Inputs may be any that keep to these rules, and one draw needn't show every extreme that they name: Each row of owners names every one of the 4 sectors of its beam shard exactly once.
All inputs are finite; a program needn't handle non-finite values.
Results may differ from a plain program's by a relative error of at most 0.0052.
Values may be sent and summed in bfloat16 or wider, within the bound.
No kernel may reach another device: no remote copies, remote signals or barrier semaphores. Data moves between devices by JAX's collectives and lax.ppermute only.
A program may use at most 64 MiB of HBM per device.

v0:
```python
import math

import jax
import jax.numpy as jnp
from jax import lax
from jax.sharding import PartitionSpec as P

B = 1024
NR = 1024


def swapped(value, axis, distance):
    return lax.ppermute(value, axis, [(i, i ^ 1 << distance) for i in range(lax.axis_size(axis))])


def odd_kernel(beam_total, columns):
    source_ix = lax.broadcasted_iota(jnp.int32, (beam_total, columns), 0)
    target_ix = lax.broadcasted_iota(jnp.int32, (beam_total, columns), 1)
    spacing = target_ix - source_ix
    parity = jnp.where(spacing % 2 == 0, 1.0, -1.0).astype(jnp.float32)
    angles = (2.0 * spacing.astype(jnp.float32) + 1.0) * (math.pi / (2.0 * beam_total))
    return (parity * jnp.cos(angles) / (beam_total * jnp.sin(angles))).astype(jnp.bfloat16)


def steer_phase(upsampled, shifts, rows_at, beams_at, beams_out):
    ratios = NR / (NR + rows_at.astype(jnp.float32))
    tilts = (2.0 * beams_at.astype(jnp.float32) + 1.0) / beams_out - 1.0
    phases = ratios[:, None] * tilts[None, :] * shifts[..., None, None]
    cosine = jnp.cos(phases)
    sines = jnp.sin(phases)
    real_part = upsampled[..., 0, :, :]
    imag_part = upsampled[..., 1, :, :]
    return jnp.stack(
        [real_part * cosine - imag_part * sines, real_part * sines + imag_part * cosine], -3
    )


def rotate_sum(children, odd_beams, shifts, rows_at, beams_out):
    count = children.shape[-1]
    even_at = 2 * jnp.arange(count, dtype=jnp.int32)
    even_sum = jnp.sum(
        steer_phase(children.astype(jnp.float32), shifts, rows_at, even_at, beams_out), axis=0
    )
    odd_sum = jnp.sum(steer_phase(odd_beams, shifts, rows_at, even_at + 1, beams_out), axis=0)
    joined = jnp.stack([even_sum, odd_sum], -1)
    return joined.reshape(even_sum.shape[:-1] + (2 * count,)).astype(jnp.bfloat16)


def odd_local(children, kernel):
    product = jnp.dot(
        children.reshape(-1, children.shape[-1]), kernel, preferred_element_type=jnp.float32
    )
    return product.reshape(children.shape[:-1] + (kernel.shape[1],))


def swap_first(pieces):
    return swapped(pieces, "sub", 0)


def swap_second(pieces):
    return swapped(pieces, "sub", 1)


def keep_and_trade(field, which_bit, swapper):
    length = field.shape[2] // 2
    kept = lax.dynamic_slice_in_dim(field, which_bit * length, length, 2)
    given = lax.dynamic_slice_in_dim(field, (1 - which_bit) * length, length, 2)
    return (jnp.stack([kept, swapper(given)]), length)


def shift_block(offsets, index, per_device):
    return lax.dynamic_slice_in_dim(offsets, index * per_device, per_device, 0)


def body(images, offsets, owners):
    sub_count = lax.axis_size("sub")
    beam_count = lax.axis_size("beam")
    sub_place = lax.axis_index("sub")
    beam_lane = lax.axis_index("beam")
    half_side = lax.axis_index("half")
    low_bit = sub_place % 2
    high_bit = sub_place // 2 % 2
    per_device = images.shape[0]
    half_rows = images.shape[2]
    own_shift = shift_block(offsets, sub_place, per_device)
    mate_shift = shift_block(offsets, jnp.bitwise_xor(sub_place, 1), per_device)
    shifts_one = jnp.stack([own_shift, mate_shift])
    pair_base = sub_place - low_bit
    mate_base = jnp.bitwise_xor(sub_place, 2) - low_bit
    center_own = (
        shift_block(offsets, pair_base, per_device)
        + shift_block(offsets, pair_base + 1, per_device)
    ) * 0.5
    center_mate = (
        shift_block(offsets, mate_base, per_device)
        + shift_block(offsets, mate_base + 1, per_device)
    ) * 0.5
    shifts_two = jnp.stack([center_own, center_mate])
    all_beams = lax.all_to_all(images, "beam", split_axis=2, concat_axis=3, tiled=True)
    block_rows = all_beams.shape[2]
    start_row = half_side * half_rows + beam_lane * block_rows
    children, length = keep_and_trade(all_beams, low_bit, swap_first)
    rows_at = start_row + low_bit * length + jnp.arange(length, dtype=jnp.int32)
    odd_beams = odd_local(children, odd_kernel(B, B))
    first_merge = rotate_sum(children, odd_beams, shifts_one, rows_at, 2 * B)
    children, quarter = keep_and_trade(first_merge, high_bit, swap_second)
    rows_at = (
        start_row + low_bit * length + high_bit * quarter + jnp.arange(quarter, dtype=jnp.int32)
    )
    odd_beams = odd_local(children, odd_kernel(2 * B, 2 * B))
    merged = rotate_sum(children, odd_beams, shifts_two, rows_at, 4 * B)
    sector_tiles = merged.reshape(per_device, 2, quarter, beam_count, sub_count, -1)
    beam_ids = jnp.arange(beam_count, dtype=jnp.int32)[:, None]
    picked = sector_tiles[:, :, :, beam_ids, owners, :]
    outgoing = picked.transpose(4, 3, 0, 1, 5, 2)
    received = lax.all_to_all(
        lax.all_to_all(outgoing, "sub", split_axis=0, concat_axis=0, tiled=True),
        "beam",
        split_axis=1,
        concat_axis=1,
        tiled=True,
    )
    sector_width = received.shape[4]
    received = received.reshape(
        sub_count // 4, 2, 2, beam_count, per_device, 2, sector_width, quarter
    )
    received = received.transpose(0, 4, 5, 6, 3, 2, 1, 7)
    return received.reshape(1, sub_count // 4 * per_device, 2, sector_width, half_rows)


def solution(mesh):
    placed = (P("sub", None, ("swath", "half"), "beam"), P(), P())
    return jax.shard_map(
        body,
        mesh=mesh,
        in_specs=placed,
        out_specs=P(("sub", "beam"), None, None, None, ("swath", "half")),
        check_vma=False,
    )
```

profile of v0, /device:TPU:0, one launch (start us, length us, event | category | flops | bytes accessed | tf_op | source)
XLA Modules:
  0.0 222.4 jit_solution(12710477142224495665)
XLA Ops:
  0.0 3.3 %copy.32 = bf16[1,2,512,512]{3,1,0,2:T(2,128)(2,1)} copy(bf16[1,2,512,512]{3,2,1,0:T(8,128)(2,1)} %param.3) | data formatting | bytes 2097152 | tf_op args[0]
  3.3 4.2 %all-to-all-start = ((bf16[1,2,512,512]{3,1,0,2:T(2,128)(2,1)}), bf16[1,2,512,512]{3,1,0,2:T(2,128)(2,1)S(1)}, u32[]{:S(2)}, u32[]{:S(2)}) async-start(bf16[1,2,512,512]{3,1,0,2:T(2,128)(2,1)} %copy.32), calls=%async_computation | async-start | bytes 2097152 | tf_op jit(solution)/shard_map/all_to_all | solution.py:99
  7.5 0.7 fusion.82
  8.2 13.7 %all-to-all-done = bf16[1,2,512,512]{3,1,0,2:T(2,128)(2,1)S(1)} async-done(((bf16[1,2,512,512]{3,1,0,2:T(2,128)(2,1)}), bf16[1,2,512,512]{3,1,0,2:T(2,128)(2,1)S(1)}, u32[]{:S(2)}, u32[]{:S(2)}) %all-to-all-start) | async-done | bytes 1048608 | tf_op jit(solution)/shard_map/all_to_all | solution.py:99
  22.0 1.1 copy.50
  23.1 0.9 all_to_all.22
  24.1 1.9 collective-permute-start
  26.0 1.3 maximum_bitcast_fusion
  29.9 7.3 %collective-permute-done = bf16[1,2,128,1024]{3,2,1,0:T(8,128)(2,1)S(1)} collective-permute-done((bf16[1,2,128,1024]{3,2,1,0:T(8,128)(2,1)S(1)}, bf16[1,2,128,1024]{3,2,1,0:T(8,128)(2,1)S(1)}, u32[]{:S(2)}, u32[]{:S(2)}) %collective-permute-start) | collective-permute-done | bytes 524320 | tf_op jit(solution)/shard_map/ppermute | solution.py:13
  37.2 17.9 %fusion.29 = f32[2,1,2,128,1024]{4,3,2,0,1:T(8,128)S(1)} fusion(bf16[1,1,2,128,1024]{4,3,2,0,1:T(8,128)(2,1)S(1)} %bitcast.99, bf16[1,1,2,128,1024]{4,3,2,0,1:T(8,128)(2,1)S(1)} %get-tuple-element.15), kind=kOutput, calls=%fused_computation.40 | convolution fusion | flops 1097334784 | bytes 3145728 | tf_op jit(solution)/shard_map/dot_general | solution.py:50
  55.3 8.0 %fusion.54 = (f32[2,1,1,128,1024]{4,3,2,0,1:T(8,128)S(1)}, f32[2,1,1,128,1024]{4,3,2,0,1:T(8,128)S(1)}, f32[2,1,1,128,1024]{4,3,2,0,1:T(8,128)S(1)}, f32[2,1,1,128,1024]{4,3,2,0,1:T(8,128)S(1)}) fusion(f32[2,1,2,128,1024]{4,3,2,0,1:T(8,128)S(1)} %fusion.59, f32[2]{0:T(128)S(1)} %maximum_bitcast_fusion, f32[128,1024]{1,0:T(8,128)S(1)} %get-tuple-element.29, ...), kind=kLoop, calls=%fused_computation.71 | loop fusion | flops 3670016 | bytes 9437192 | tf_op jit(solution)/shard_map/sub | solution.py:34
  63.7 0.8 copy.34
  64.5 0.6 constant_dynamic-slice_fusion.1
  65.1 1.1 copy.46
  66.2 2.6 %collective-permute-start.1 = (bf16[1,2,64,2048]{3,2,1,0:T(8,128)(2,1)}, bf16[1,2,64,2048]{3,2,1,0:T(8,128)(2,1)S(1)}, u32[]{:S(2)}, u32[]{:S(2)}) collective-permute-start(bf16[1,2,64,2048]{3,2,1,0:T(8,128)(2,1)} %copy.46), channel_id=1, source_target_pairs={{0,8},{4,12},{8,0},{12,4},{1,9},{5,13},{9,1},{13,5},{2,10},{6,14},... | collective-permute-start | bytes 1572872 | tf_op jit(solution)/shard_map/ppermute | solution.py:13
  69.5 21.4 %collective-permute-done.1 = bf16[1,2,64,2048]{3,2,1,0:T(8,128)(2,1)S(1)} collective-permute-done((bf16[1,2,64,2048]{3,2,1,0:T(8,128)(2,1)}, bf16[1,2,64,2048]{3,2,1,0:T(8,128)(2,1)S(1)}, u32[]{:S(2)}, u32[]{:S(2)}) %collective-permute-start.1) | collective-permute-done | bytes 524320 | tf_op jit(solution)/shard_map/ppermute | solution.py:13
  91.1 72.4 %fusion.15 = f32[2,1,2,64,2048]{4,3,2,0,1:T(8,128)S(1)} fusion(bf16[2,2,64,2048]{3,2,1,0:T(8,128)(2,1)S(1)} %fusion.89), kind=kOutput, calls=%fused_computation.25 | convolution fusion | flops 2239758336 | bytes 3145728 | tf_op jit(solution)/shard_map/dot_general | solution.py:50
  163.5 8.0 %fusion.50 = (f32[2,1,1,64,2048]{4,3,2,0,1:T(8,128)S(1)}, f32[2,1,1,64,2048]{4,3,2,0,1:T(8,128)S(1)}, f32[2,1,1,64,2048]{4,3,2,0,1:T(8,128)S(1)}, f32[2,1,1,64,2048]{4,3,2,0,1:T(8,128)S(1)}) fusion(f32[2,1,2,64,2048]{4,3,2,0,1:T(8,128)S(1)} %fusion.58, f32[2]{0:T(128)S(1)} %maximum_bitcast_fusion.1, f32[64,2048]{1,0:T(8,128)S(1)} %get-tuple-element.19, ...), kind=kLoop, calls=%fused_computation.67 | loop fusion | flops 3670016 | bytes 9437192 | tf_op jit(solution)/shard_map/sub | solution.py:34
  171.8 1.5 copy.37
  173.3 0.8 copy.38
  174.2 0.6 gather_fusion
  174.9 30.2 %all_to_all.28 = bf16[4,2,1,2,512,64]{4,5,3,2,1,0:T(8,128)(2,1)S(1)} all-to-all(bf16[4,2,1,2,512,64]{4,5,3,2,1,0:T(8,128)(2,1)S(1)} %bitcast.90), channel_id=1, replica_groups=mesh['swath'=2,'sub'=4,'beam'=2,'half'=2] {'sub'}, dimensions={0} | all-to-all | bytes 2097152 | tf_op jit(solution)/shard_map/all_to_all | solution.py:117
  205.2 15.6 %all_to_all.29 = bf16[4,2,1,2,512,64]{4,5,3,2,0,1:T(8,128)(2,1)S(1)} all-to-all(bf16[4,2,1,2,512,64]{4,5,3,2,0,1:T(8,128)(2,1)S(1)} %copy.40), channel_id=1, replica_groups=mesh['swath'=2,'sub'=4,'beam'=2,'half'=2] {'beam'}, dimensions={1} | all-to-all | bytes 2097152 | tf_op jit(solution)/shard_map/all_to_all | solution.py:116
  221.0 1.3 copy.43
  (28 shorter events, 2.4 us)
Async XLA Ops:
  0.0 7.5 %copy-start = (f32[4]{0:T(128)S(1)}, f32[4]{0:T(128)}, u32[]{:S(2)}) copy-start(f32[4]{0:T(128)} %param.4) | copy-start | bytes 52
  3.3 18.7 %all-to-all-start = ((bf16[1,2,512,512]{3,1,0,2:T(2,128)(2,1)}), bf16[1,2,512,512]{3,1,0,2:T(2,128)(2,1)S(1)}, u32[]{:S(2)}, u32[]{:S(2)}) async-start(bf16[1,2,512,512]{3,1,0,2:T(2,128)(2,1)} %copy.32), calls=%async_computation | async-start | bytes 2097152 | tf_op jit(solution)/shard_map/all_to_all | solution.py:99
  23.0 6.7 %copy-start.1 = (s32[2,4]{1,0:T(2,128)S(1)}, s32[2,4]{1,0:T(2,128)}, u32[]{:S(2)}) copy-start(s32[2,4]{1,0:T(2,128)} %param.5) | copy-start | bytes 100
  24.1 13.2 %collective-permute-start = (bf16[1,2,128,1024]{3,2,1,0:T(8,128)(2,1)S(1)}, bf16[1,2,128,1024]{3,2,1,0:T(8,128)(2,1)S(1)}, u32[]{:S(2)}, u32[]{:S(2)}) collective-permute-start(bf16[1,2,128,1024]{3,2,1,0:T(8,128)(2,1)S(1)} %get-tuple-element.16), channel_id=1, source_target_pairs={{0,4},{4,0},{8,12},{12,8},{1,5},{5,1},{9,13},{13,9},{2,6},{6,2},{1... | collective-permute-start | bytes 1572872 | tf_op jit(solution)/shard_map/ppermute | solution.py:13
  66.2 24.6 %collective-permute-start.1 = (bf16[1,2,64,2048]{3,2,1,0:T(8,128)(2,1)}, bf16[1,2,64,2048]{3,2,1,0:T(8,128)(2,1)S(1)}, u32[]{:S(2)}, u32[]{:S(2)}) collective-permute-start(bf16[1,2,64,2048]{3,2,1,0:T(8,128)(2,1)} %copy.46), channel_id=1, source_target_pairs={{0,8},{4,12},{8,0},{12,4},{1,9},{5,13},{9,1},{13,5},{2,10},{6,14},... | collective-permute-start | bytes 1572872 | tf_op jit(solution)/shard_map/ppermute | solution.py:13
where the time goes:
time: 226 us; the launch traced here: 222 us
  matrix products  90.3 us (40%)
  blocking collectives  45.8 us (20%)
  waiting for transfers between devices  42.4 us (19%)
  other arithmetic  18.8 us (8%)
  local copies, waits for them, and re-layouts  13.7 us (6%)
  starting transfers between devices  8.68 us (4%)
  between operations  2.88 us (1%)
    dot_general x2, matrix products, odd_local(): jnp.dot(children.reshape(-1, children.shape[-1]), kernel, preferred_eleme...  90.3 us
    all_to_all x1, blocking collectives, body(): lax.all_to_all(outgoing, 'sub', split_axis=0, concat_axis=0, tiled=True)  30.2 us
    ppermute x2, waiting for transfers between devices, swapped(): lax.ppermute(value, axis, [(i, i ^ 1 << distance) for i in range(lax.axis...  28.7 us
    sub x2, other arithmetic, steer_phase(): real_part * cosine - imag_part * sines  16 us
    all_to_all x1, blocking collectives, body(): lax.all_to_all(lax.all_to_all(outgoing, 'sub', split_axis=0, concat_axis=...  15.6 us
    all_to_all x1, waiting for transfers between devices, body(): lax.all_to_all(images, 'beam', split_axis=2, concat_axis=3, tiled=True)  13.7 us
  transfers between devices with their start and end apart: 3, of which 3 were waited for; matrix products, arithmetic and copies ran while one was open for 1% of the time, Pallas kernels for 0%

commit v1 on v0

--- a/solution.py
+++ b/solution.py
@@ -1,6 +1,7 @@
 import math
 
 import jax
+import numpy as np
 import jax.numpy as jnp
 from jax import lax
 from jax.sharding import PartitionSpec as P
@@ -14,12 +15,11 @@
 
 
 def odd_kernel(beam_total, columns):
-    source_ix = lax.broadcasted_iota(jnp.int32, (beam_total, columns), 0)
-    target_ix = lax.broadcasted_iota(jnp.int32, (beam_total, columns), 1)
-    spacing = target_ix - source_ix
-    parity = jnp.where(spacing % 2 == 0, 1.0, -1.0).astype(jnp.float32)
-    angles = (2.0 * spacing.astype(jnp.float32) + 1.0) * (math.pi / (2.0 * beam_total))
-    return (parity * jnp.cos(angles) / (beam_total * jnp.sin(angles))).astype(jnp.bfloat16)
+    spacing = np.arange(columns, dtype=np.int64)[None, :] - np.arange(beam_total, dtype=np.int64)[:, None]
+    parity = np.where(spacing % 2 == 0, 1.0, -1.0).astype(np.float32)
+    angles = (2.0 * spacing.astype(np.float32) + np.float32(1.0)) * np.float32(math.pi / (2.0 * beam_total))
+    values = parity * np.cos(angles) / (np.float32(beam_total) * np.sin(angles))
+    return jnp.asarray(values.astype(np.float32).astype(jnp.bfloat16))
 
 
 def steer_phase(upsampled, shifts, rows_at, beams_at, beams_out):

time: 226 us -> 139 us (0.62); the launches traced: 222 us -> 139 us
  matrix products: 90.3 us -> 7.03 us
    dot_general x2, matrix products: 90.3 us -> 7.03 us  [odd_local(): jnp.dot(children.reshape(-1, children.shape[-1]), kernel, preferred_eleme...]
  transfers between devices with their start and end apart: 3 -> 3, of which waited for: 3 -> 3; matrix products, arithmetic and copies ran while one was open for 1% -> 2% of each run, Pallas kernels for 0% -> 0%
where the time goes in v1:
time: 139 us
  blocking collectives  45.8 us (33%)
  waiting for transfers between devices  42.3 us (30%)
  other arithmetic  18.8 us (14%)
  local copies, waits for them, and re-layouts  13.5 us (10%)
  starting transfers between devices  8.68 us (6%)
  matrix products  7.03 us (5%)
  between operations  2.69 us (2%)
    all_to_all x1, blocking collectives, body(): lax.all_to_all(outgoing, 'sub', split_axis=0, concat_axis=0, tiled=True)  30.2 us
    ppermute x2, waiting for transfers between devices, swapped(): lax.ppermute(value, axis, [(i, i ^ 1 << distance) for i in range(lax.axis...  28.6 us
    sub x2, other arithmetic, steer_phase(): real_part * cosine - imag_part * sines  16 us
    all_to_all x1, blocking collectives, body(): lax.all_to_all(lax.all_to_all(outgoing, 'sub', split_axis=0, concat_axis=...  15.6 us
    all_to_all x1, waiting for transfers between devices, body(): lax.all_to_all(images, 'beam', split_axis=2, concat_axis=3, tiled=True)  13.7 us
    dot_general x2, matrix products, odd_local(): jnp.dot(children.reshape(-1, children.shape[-1]), kernel, preferred_eleme...  7.03 us
    ppermute x2, starting transfers between devices, swapped(): lax.ppermute(value, axis, [(i, i ^ 1 << distance) for i in range(lax.axis...  4.45 us
    unnamed x8, local copies, waits for them, and re-layouts  4.43 us
  transfers between devices with their start and end apart: 3, of which 3 were waited for; matrix products, arithmetic and copies ran while one was open for 2% of the time, Pallas kernels for 0%

profile of v1, /device:TPU:0, one launch (start us, length us, event | category | flops | bytes accessed | tf_op | source)
XLA Modules:
  0.0 138.8 jit_solution(17803852248841441353)
XLA Ops:
  0.0 3.3 %copy.34 = bf16[1,2,512,512]{3,1,0,2:T(2,128)(2,1)} copy(bf16[1,2,512,512]{3,2,1,0:T(8,128)(2,1)} %param.5) | data formatting | bytes 2097152 | tf_op args[0]
  3.3 4.2 %all-to-all-start = ((bf16[1,2,512,512]{3,1,0,2:T(2,128)(2,1)}), bf16[1,2,512,512]{3,1,0,2:T(2,128)(2,1)S(1)}, u32[]{:S(2)}, u32[]{:S(2)}) async-start(bf16[1,2,512,512]{3,1,0,2:T(2,128)(2,1)} %copy.34), calls=%async_computation | async-start | bytes 2097152 | tf_op jit(solution)/shard_map/all_to_all | solution.py:99
  7.5 0.7 fusion.34
  8.3 13.7 %all-to-all-done = bf16[1,2,512,512]{3,1,0,2:T(2,128)(2,1)S(1)} async-done(((bf16[1,2,512,512]{3,1,0,2:T(2,128)(2,1)}), bf16[1,2,512,512]{3,1,0,2:T(2,128)(2,1)S(1)}, u32[]{:S(2)}, u32[]{:S(2)}) %all-to-all-start) | async-done | bytes 1048608 | tf_op jit(solution)/shard_map/all_to_all | solution.py:99
  22.0 1.1 copy.52
  23.1 0.8 all_to_all.22
  23.9 1.9 %collective-permute-start = (bf16[1,2,128,1024]{3,2,1,0:T(8,128)(2,1)S(1)}, bf16[1,2,128,1024]{3,2,1,0:T(8,128)(2,1)S(1)}, u32[]{:S(2)}, u32[]{:S(2)}) collective-permute-start(bf16[1,2,128,1024]{3,2,1,0:T(8,128)(2,1)S(1)} %get-tuple-element.16), channel_id=1, source_target_pairs={{0,4},{4,0},{8,12},{12,8},{1,5},{5,1},{9,13},{13,9},{2,6},{6,2},{1... | collective-permute-start | bytes 1572872 | tf_op jit(solution)/shard_map/ppermute | solution.py:14
  25.8 1.4 maximum_bitcast_fusion
  29.8 7.3 %collective-permute-done = bf16[1,2,128,1024]{3,2,1,0:T(8,128)(2,1)S(1)} collective-permute-done((bf16[1,2,128,1024]{3,2,1,0:T(8,128)(2,1)S(1)}, bf16[1,2,128,1024]{3,2,1,0:T(8,128)(2,1)S(1)}, u32[]{:S(2)}, u32[]{:S(2)}) %collective-permute-start) | collective-permute-done | bytes 524320 | tf_op jit(solution)/shard_map/ppermute | solution.py:14
  37.2 1.3 convolution_bitcast_fusion.1
  38.5 8.0 %fusion.22 = (f32[2,1,1,128,1024]{4,3,2,0,1:T(8,128)S(1)}, f32[2,1,1,128,1024]{4,3,2,0,1:T(8,128)S(1)}, f32[2,1,1,128,1024]{4,3,2,0,1:T(8,128)S(1)}, f32[2,1,1,128,1024]{4,3,2,0,1:T(8,128)S(1)}) fusion(f32[2,1,2,128,1024]{4,3,2,0,1:T(8,128)S(1)} %fusion.27, f32[2]{0:T(128)S(1)} %maximum_bitcast_fusion, f32[128,1024]{1,0:T(8,128)S(1)} %get-tuple-element.29, ...), kind=kLoop, calls=%fused_computation.37 | loop fusion | flops 3670016 | bytes 9437192 | tf_op jit(solution)/shard_map/sub | solution.py:34
  46.9 0.8 copy.36
  47.7 0.6 constant_dynamic-slice_fusion.1
  48.4 1.1 copy.48
  49.5 2.6 %collective-permute-start.1 = (bf16[1,2,64,2048]{3,2,1,0:T(8,128)(2,1)}, bf16[1,2,64,2048]{3,2,1,0:T(8,128)(2,1)S(1)}, u32[]{:S(2)}, u32[]{:S(2)}) collective-permute-start(bf16[1,2,64,2048]{3,2,1,0:T(8,128)(2,1)} %copy.48), channel_id=1, source_target_pairs={{0,8},{4,12},{8,0},{12,4},{1,9},{5,13},{9,1},{13,5},{2,10},{6,14},... | collective-permute-start | bytes 1572872 | tf_op jit(solution)/shard_map/ppermute | solution.py:14
  52.7 21.4 %collective-permute-done.1 = bf16[1,2,64,2048]{3,2,1,0:T(8,128)(2,1)S(1)} collective-permute-done((bf16[1,2,64,2048]{3,2,1,0:T(8,128)(2,1)}, bf16[1,2,64,2048]{3,2,1,0:T(8,128)(2,1)S(1)}, u32[]{:S(2)}, u32[]{:S(2)}) %collective-permute-start.1) | collective-permute-done | bytes 524320 | tf_op jit(solution)/shard_map/ppermute | solution.py:14
  74.2 5.7 %convolution_bitcast_fusion = f32[2,1,2,64,2048]{4,3,2,0,1:T(8,128)S(1)} fusion(bf16[2048,2048,1,1]{1,0,3,2:T(8,128)(2,1)} %constant.110, bf16[1,1,2,64,2048]{4,3,2,0,1:T(8,128)(2,1)S(1)} %bitcast.84, bf16[1,1,2,64,2048]{4,3,2,0,1:T(8,128)(2,1)S(1)} %bitcast.76), kind=kOutput, calls=%fused_computation.1 | convolution fusion | flops 2148007936 | bytes 11534336 | tf_op jit(solution)/shard_map/dot_general | solution.py:50
  80.0 8.0 %fusion.18 = (f32[2,1,1,64,2048]{4,3,2,0,1:T(8,128)S(1)}, f32[2,1,1,64,2048]{4,3,2,0,1:T(8,128)S(1)}, f32[2,1,1,64,2048]{4,3,2,0,1:T(8,128)S(1)}, f32[2,1,1,64,2048]{4,3,2,0,1:T(8,128)S(1)}) fusion(f32[2,1,2,64,2048]{4,3,2,0,1:T(8,128)S(1)} %fusion.26, f32[2]{0:T(128)S(1)} %maximum_bitcast_fusion.1, f32[64,2048]{1,0:T(8,128)S(1)} %get-tuple-element.19, ...), kind=kLoop, calls=%fused_computation.33 | loop fusion | flops 3670016 | bytes 9437192 | tf_op jit(solution)/shard_map/sub | solution.py:34
  88.3 1.5 %copy.39 = bf16[1,2,64,2048,2]{2,4,3,1,0:T(2,128)(2,1)S(1)} copy(bf16[1,2,64,2048,2]{3,2,1,4,0:T(8,128)(2,1)S(1)} %pad_maximum_fusion.3) | data formatting | bytes 2097152 | tf_op jit(solution)/shard_map/stack | solution.py:45
  89.8 0.8 copy.40
  90.7 0.6 gather_fusion
  91.4 30.2 %all_to_all.28 = bf16[4,2,1,2,512,64]{4,5,3,2,1,0:T(8,128)(2,1)S(1)} all-to-all(bf16[4,2,1,2,512,64]{4,5,3,2,1,0:T(8,128)(2,1)S(1)} %bitcast.72), channel_id=1, replica_groups=mesh['swath'=2,'sub'=4,'beam'=2,'half'=2] {'sub'}, dimensions={0} | all-to-all | bytes 2097152 | tf_op jit(solution)/shard_map/all_to_all | solution.py:117
  121.7 15.6 %all_to_all.29 = bf16[4,2,1,2,512,64]{4,5,3,2,0,1:T(8,128)(2,1)S(1)} all-to-all(bf16[4,2,1,2,512,64]{4,5,3,2,0,1:T(8,128)(2,1)S(1)} %copy.42), channel_id=1, replica_groups=mesh['swath'=2,'sub'=4,'beam'=2,'half'=2] {'beam'}, dimensions={1} | all-to-all | bytes 2097152 | tf_op jit(solution)/shard_map/all_to_all | solution.py:116
  137.5 1.3 copy.45
  (29 shorter events, 2.3 us)
Async XLA Ops:
  0.0 7.5 %copy-start = (f32[4]{0:T(128)S(1)}, f32[4]{0:T(128)}, u32[]{:S(2)}) copy-start(f32[4]{0:T(128)} %param.6) | copy-start | bytes 52
  3.3 18.7 %all-to-all-start = ((bf16[1,2,512,512]{3,1,0,2:T(2,128)(2,1)}), bf16[1,2,512,512]{3,1,0,2:T(2,128)(2,1)S(1)}, u32[]{:S(2)}, u32[]{:S(2)}) async-start(bf16[1,2,512,512]{3,1,0,2:T(2,128)(2,1)} %copy.34), calls=%async_computation | async-start | bytes 2097152 | tf_op jit(solution)/shard_map/all_to_all | solution.py:99
  23.0 6.6 %copy-start.1 = (s32[2,4]{1,0:T(2,128)S(1)}, s32[2,4]{1,0:T(2,128)}, u32[]{:S(2)}) copy-start(s32[2,4]{1,0:T(2,128)} %param.7) | copy-start | bytes 100
  23.9 13.2 %collective-permute-start = (bf16[1,2,128,1024]{3,2,1,0:T(8,128)(2,1)S(1)}, bf16[1,2,128,1024]{3,2,1,0:T(8,128)(2,1)S(1)}, u32[]{:S(2)}, u32[]{:S(2)}) collective-permute-start(bf16[1,2,128,1024]{3,2,1,0:T(8,128)(2,1)S(1)} %get-tuple-element.16), channel_id=1, source_target_pairs={{0,4},{4,0},{8,12},{12,8},{1,5},{5,1},{9,13},{13,9},{2,6},{6,2},{1... | collective-permute-start | bytes 1572872 | tf_op jit(solution)/shard_map/ppermute | solution.py:14
  29.6 7.6 %copy-start.2 = (bf16[1024,1024,1,1]{1,0,3,2:T(8,128)(2,1)S(1)}, bf16[1024,1024,1,1]{1,0,3,2:T(8,128)(2,1)}, u32[]{:S(2)}) copy-start(bf16[1024,1024,1,1]{1,0,3,2:T(8,128)(2,1)} %constant.109) | copy-start | bytes 6291460
  49.5 24.6 %collective-permute-start.1 = (bf16[1,2,64,2048]{3,2,1,0:T(8,128)(2,1)}, bf16[1,2,64,2048]{3,2,1,0:T(8,128)(2,1)S(1)}, u32[]{:S(2)}, u32[]{:S(2)}) collective-permute-start(bf16[1,2,64,2048]{3,2,1,0:T(8,128)(2,1)} %copy.48), channel_id=1, source_target_pairs={{0,8},{4,12},{8,0},{12,4},{1,9},{5,13},{9,1},{13,5},{2,10},{6,14},... | collective-permute-start | bytes 1572872 | tf_op jit(solution)/shard_map/ppermute | solution.py:14

commit v2 on v1

v2 whole, which is shorter than its diff:
```python
import math

import jax
import numpy as np
import jax.numpy as jnp
from jax import lax
from jax.sharding import Mesh
from jax.sharding import PartitionSpec as P

B = 1024
NR = 1024
GROUP_SUBS = 4


def odd_kernel(beam_total, columns):
    spacing = np.arange(columns, dtype=np.int64)[None, :] - np.arange(beam_total, dtype=np.int64)[:, None]
    parity = np.where(spacing % 2 == 0, 1.0, -1.0).astype(np.float32)
    angles = (2.0 * spacing.astype(np.float32) + np.float32(1.0)) * np.float32(math.pi / (2.0 * beam_total))
    values = parity * np.cos(angles) / (np.float32(beam_total) * np.sin(angles))
    return jnp.asarray(values.astype(np.float32).astype(jnp.bfloat16))


def steer_phase(upsampled, shifts, rows_at, beams_at, beams_out):
    ratios = NR / (NR + rows_at.astype(jnp.float32))
    tilts = (2.0 * beams_at.astype(jnp.float32) + 1.0) / beams_out - 1.0
    phases = ratios[:, None] * tilts[None, :] * shifts[..., None, None]
    cosine = jnp.cos(phases)
    sines = jnp.sin(phases)
    real_part = upsampled[..., 0, :, :]
    imag_part = upsampled[..., 1, :, :]
    return jnp.stack(
        [real_part * cosine - imag_part * sines, real_part * sines + imag_part * cosine], -3
    )


def odd_local(children, kernel):
    product = jnp.dot(
        children.reshape(-1, children.shape[-1]), kernel, preferred_element_type=jnp.float32
    )
    return product.reshape(children.shape[:-1] + (kernel.shape[1],))


def merge_pairs(children, shifts, rows_at, kernel):
    count = children.shape[-1]
    beams_out = 2 * count
    even_at = 2 * jnp.arange(count, dtype=jnp.int32)
    odd_beams = odd_local(children, kernel)
    even_sum = jnp.sum(
        steer_phase(children.astype(jnp.float32), shifts, rows_at, even_at, beams_out), axis=1
    )
    odd_sum = jnp.sum(steer_phase(odd_beams, shifts, rows_at, even_at + 1, beams_out), axis=1)
    joined = jnp.stack([even_sum, odd_sum], -1)
    return joined.reshape(even_sum.shape[:-1] + (beams_out,)).astype(jnp.bfloat16)


def body(images, offsets, owners):
    group_count = lax.axis_size("grp")
    sub_count = group_count * GROUP_SUBS
    beam_count = lax.axis_size("beam")
    group_at = lax.axis_index("grp")
    member_at = lax.axis_index("sub4") * beam_count + lax.axis_index("beam")
    half_side = lax.axis_index("half")
    members = GROUP_SUBS * beam_count
    half_rows = images.shape[2]
    own_rows = half_rows // members
    local_beams = images.shape[3]

    pieces = images[0].reshape(2, members, own_rows, local_beams).transpose(1, 0, 2, 3)
    gathered = lax.all_to_all(pieces, ("sub4", "beam"), 0, 0, tiled=True)
    gathered = gathered.reshape(GROUP_SUBS, beam_count, 2, own_rows, local_beams)
    children = gathered.transpose(0, 2, 3, 1, 4).reshape(
        GROUP_SUBS // 2, 2, 2, own_rows, beam_count * local_beams
    )
    rows_at = half_side * half_rows + member_at * own_rows + jnp.arange(own_rows, dtype=jnp.int32)
    shifts = lax.dynamic_slice_in_dim(offsets, group_at * GROUP_SUBS, GROUP_SUBS, 0)
    shifts_one = shifts.reshape(GROUP_SUBS // 2, 2)
    first = merge_pairs(children, shifts_one, rows_at, odd_kernel(B, B))
    centers = (shifts_one[:, 0] + shifts_one[:, 1]) * 0.5
    merged = merge_pairs(first[None], centers[None], rows_at, odd_kernel(2 * B, 2 * B))[0]

    sector_width = merged.shape[-1] // (beam_count * sub_count)
    tiles = merged.reshape(2, own_rows, beam_count, sub_count, sector_width)
    beam_ids = jnp.arange(beam_count, dtype=jnp.int32)[:, None]
    picked = tiles[:, :, beam_ids, owners, :]
    outgoing = picked.transpose(3, 2, 0, 1, 4).reshape(sub_count * beam_count, 2, own_rows, sector_width)
    received = lax.all_to_all(outgoing, ("grp", "sub4", "beam"), 0, 0, tiled=True)
    received = received.reshape(group_count, members, 2, own_rows, sector_width)
    received = received.transpose(0, 2, 4, 1, 3)
    return received.reshape(1, group_count, 2, sector_width, members * own_rows)


def solution(mesh):
    shape = dict(mesh.shape)
    devices = mesh.devices.reshape(
        shape["swath"], shape["sub"] // GROUP_SUBS, GROUP_SUBS, shape["beam"], shape["half"]
    )
    split = Mesh(devices, ("swath", "grp", "sub4", "beam", "half"))
    placed = (P(("grp", "sub4"), None, ("swath", "half"), "beam"), P(), P())
    return jax.shard_map(
        body,
        mesh=split,
        in_specs=placed,
        out_specs=P(("grp", "sub4", "beam"), None, None, None, ("swath", "half")),
        check_vma=False,
    )
```

time: 139 us -> 112 us (0.81)
  waiting for transfers between devices: 42.3 us -> 24 us
  blocking collectives: 45.8 us -> 29.3 us
  local copies, waits for them, and re-layouts: 13.5 us -> 25.5 us
  between operations: 2.69 us -> 0.21 us
  starting transfers between devices: 8.68 us -> 7.28 us
    ppermute x2 -> x0, waiting for transfers between devices: 28.6 us -> none  [swapped(): lax.ppermute(value, axis, [(i, i ^ 1 << distance) for i in range(lax.axis...]
    all_to_all x2 -> x1, blocking collectives: 45.8 us -> 29.3 us  [body(): lax.all_to_all(outgoing, ('grp', 'sub4', 'beam'), 0, 0, tiled=True)]
    all_to_all x1, waiting for transfers between devices: 13.7 us -> 24 us  [body(): gathered = lax.all_to_all(pieces, ('sub4', 'beam'), 0, 0, tiled=True)]
    convert_element_type x1 -> x3, local copies, waits for them, and re-layouts: 0.83 us -> 6.38 us  [the longest x1 4.04 us: merge_pairs(): children.astype(jnp.float32)]
    slice x0 -> x1, local copies, waits for them, and re-layouts: none -> 4.47 us  [steer_phase(): imag_part = upsampled[..., 1, :, :]]
    ppermute x2 -> x0, starting transfers between devices: 4.45 us -> none  [swapped(): lax.ppermute(value, axis, [(i, i ^ 1 << distance) for i in range(lax.axis...]
    transpose x1 -> x4, local copies, waits for them, and re-layouts: 0.09 us -> 3.57 us  [the longest x1 2.31 us: body(): images[0].reshape(2, members, own_rows, local_beams).transpose(1, 0, 2, 3)]
    all_to_all x1, starting transfers between devices: 4.23 us -> 7.28 us  [body(): gathered = lax.all_to_all(pieces, ('sub4', 'beam'), 0, 0, tiled=True)]
  transfers between devices with their start and end apart: 3 -> 1, of which waited for: 3 -> 1; matrix products, arithmetic and copies ran while one was open for 2% -> 2% of each run, Pallas kernels for 0% -> 0%
where the time goes in v2:
time: 112 us
  blocking collectives  29.3 us (26%)
  local copies, waits for them, and re-layouts  25.5 us (23%)
  waiting for transfers between devices  24 us (21%)
  other arithmetic  18.5 us (17%)
  starting transfers between devices  7.28 us (6%)
  matrix products  7.14 us (6%)
    all_to_all x1, blocking collectives, body(): lax.all_to_all(outgoing, ('grp', 'sub4', 'beam'), 0, 0, tiled=True)  29.3 us
    all_to_all x1, waiting for transfers between devices, body(): gathered = lax.all_to_all(pieces, ('sub4', 'beam'), 0, 0, tiled=True)  24 us
    sub x2, other arithmetic, steer_phase(): real_part * cosine - imag_part * sines  16 us
    all_to_all x1, starting transfers between devices, body(): gathered = lax.all_to_all(pieces, ('sub4', 'beam'), 0, 0, tiled=True)  7.28 us
    dot_general x2, matrix products, odd_local(): jnp.dot(children.reshape(-1, children.shape[-1]), kernel, preferred_eleme...  7.14 us
    unnamed x14, local copies, waits for them, and re-layouts  6.67 us
    slice x1, local copies, waits for them, and re-layouts, steer_phase(): imag_part = upsampled[..., 1, :, :]  4.47 us
    convert_element_type x1, local copies, waits for them, and re-layouts, merge_pairs(): children.astype(jnp.float32)  4.04 us
  transfers between devices with their start and end apart: 1, of which 1 were waited for; matrix products, arithmetic and copies ran while one was open for 2% of the time, Pallas kernels for 0%

profile of v2, /device:TPU:0, one launch (start us, length us, event | category | flops | bytes accessed | tf_op | source)
XLA Modules:
  0.0 111.9 jit_solution(17041138042253797647)
XLA Ops:
  0.0 2.3 %copy.26 = bf16[8,2,64,512]{3,2,1,0:T(8,128)(2,1)} copy(bf16[8,2,64,512]{3,2,0,1:T(8,128)(2,1)} %bitcast.57) | data formatting | bytes 2097152 | tf_op jit(solution)/shard_map/transpose | solution.py:68
  2.3 7.3 %all-to-all-start = ((bf16[8,2,64,512]{3,2,1,0:T(8,128)(2,1)}), bf16[8,2,64,512]{3,2,1,0:T(8,128)(2,1)S(1)}, u32[]{:S(2)}, u32[]{:S(2)}) async-start(bf16[8,2,64,512]{3,2,1,0:T(8,128)(2,1)} %copy.26), calls=%async_computation | async-start | bytes 2097152 | tf_op jit(solution)/shard_map/all_to_all | solution.py:69
  9.8 0.2 multiply_reduce_fusion
  10.1 1.2 %broadcast_multiply_fusion.1 = (f32[64,2048]{1,0:T(8,128)}, f32[64,2048]{1,0:T(8,128)}) fusion(f32[2048]{0:T(1024)S(1)} %get-tuple-element.26, f32[64]{0:T(128)S(1)} %add_divide_fusion, f32[2048]{0:T(1024)S(1)} %get-tuple-element.25), kind=kLoop, calls=%fused_computation.44 | loop fusion | flops 262144 | bytes 1065216 | tf_op jit(solution)/shard_map/mul | solution.py:26
  11.3 24.0 %all-to-all-done = bf16[8,2,64,512]{3,2,1,0:T(8,128)(2,1)S(1)} async-done(((bf16[8,2,64,512]{3,2,1,0:T(8,128)(2,1)}), bf16[8,2,64,512]{3,2,1,0:T(8,128)(2,1)S(1)}, u32[]{:S(2)}, u32[]{:S(2)}) %all-to-all-start) | async-done | bytes 1048608 | tf_op jit(solution)/shard_map/all_to_all | solution.py:69
  35.4 1.1 copy.27
  36.5 0.8 reshape.298
  37.2 0.2 convert_element_type.80
  37.5 1.3 %copy-done.5 = bf16[1024,1024,1,1,1]{1,0,4,3,2:T(8,128)(2,1)S(1)} copy-done((bf16[1024,1024,1,1,1]{1,0,4,3,2:T(8,128)(2,1)S(1)}, bf16[1024,1024,1,1,1]{1,0,4,3,2:T(8,128)(2,1)}, u32[]{:S(2)}) %copy-start.5) | copy-done | bytes 2097176
  38.8 1.3 %convolution_bitcast_fusion.1 = f32[2,2,2,64,1024]{4,3,2,1,0:T(8,128)S(1)} fusion(bf16[1024,1024,1,1,1]{1,0,4,3,2:T(8,128)(2,1)S(1)} %copy-done.5, bf16[2,2,2,64,1024]{4,3,2,1,0:T(8,128)(2,1)S(1)} %reshape.298), kind=kOutput, calls=%fused_computation.7 | convolution fusion | flops 1073741824 | bytes 5242880 | tf_op jit(solution)/shard_map/dot_general | solution.py:37
  40.1 8.0 %fusion.22 = (f32[2,2,1,64,1024]{4,3,2,1,0:T(8,128)S(1)}, f32[2,2,1,64,1024]{4,3,2,1,0:T(8,128)S(1)}, f32[2,2,1,64,1024]{4,3,2,1,0:T(8,128)S(1)}, f32[2,2,1,64,1024]{4,3,2,1,0:T(8,128)S(1)}) fusion(f32[2,2,2,64,1024]{4,3,2,1,0:T(8,128)S(1)} %convert_element_type.80, f32[2,2]{1,0:T(2,128)S(1)} %mul.332, f32[64,1024]{1,0:T(8,128)S(1)} %get-tuple-element.21, ...), kind=kLoop, calls=%fused_computation.38 | loop fusion | flops 3670016 | bytes 8912912 | tf_op jit(solution)/shard_map/sub | solution.py:32
  48.1 0.1 maximum_reduce_fusion
  48.5 4.0 %copy.28 = f32[2,2,64,1024,2]{2,4,3,1,0:T(2,128)} copy(bf16[2,2,64,1024,2]{3,2,1,0,4:T(8,128)(2,1)S(1)} %maximum_convert_fusion) | data formatting | bytes 3145728 | tf_op jit(solution)/shard_map/convert_element_type | solution.py:49
  52.5 1.5 %copy.31 = bf16[2,2,64,1024,2]{2,4,3,1,0:T(2,128)(2,1)S(1)} copy(bf16[2,2,64,1024,2]{3,2,1,0,4:T(8,128)(2,1)S(1)} %maximum_convert_fusion) | data formatting | bytes 2097152 | tf_op jit(solution)/shard_map/convert_element_type | solution.py:53
  54.1 4.5 %fusion.28 = (f32[1,2,1,64,2048]{3,4,2,1,0:T(8,128)}, f32[1,2,1,64,2048]{3,4,2,1,0:T(8,128)}) fusion(f32[1,2,2,64,2048]{3,4,2,1,0:T(8,128)} %bitcast.45), kind=kLoop, calls=%fused_computation.60 | loop fusion | bytes 4194304 | tf_op jit(solution)/shard_map/slice | solution.py:30
  58.5 2.2 %copy.41 = f32[1,2,1,64,2048]{4,3,2,1,0:T(8,128)S(1)} copy(f32[1,2,1,64,2048]{3,4,2,1,0:T(8,128)} %get-tuple-element.6) | data formatting | bytes 2097152
  60.7 3.1 %copy.42 = f32[1,2,1,64,2048]{4,3,2,1,0:T(8,128)} copy(f32[1,2,1,64,2048]{3,4,2,1,0:T(8,128)} %get-tuple-element.5) | data formatting | bytes 2097152
  63.9 5.9 %convolution_bitcast_fusion = f32[1,2,2,64,2048]{4,3,2,1,0:T(8,128)S(1)} fusion(bf16[2,2,64,2048]{2,3,1,0:T(8,128)(2,1)S(1)} %bitcast.46, bf16[2048,2048,1,1]{1,0,3,2:T(8,128)(2,1)} %constant.80), kind=kOutput, calls=%fused_computation.1 | convolution fusion | flops 2147483648 | bytes 11534336 | tf_op jit(solution)/shard_map/dot_general | solution.py:37
  69.8 8.0 %fusion.18 = (f32[1,2,1,64,2048]{4,3,2,1,0:T(8,128)S(1)}, f32[1,2,1,64,2048]{4,3,2,1,0:T(8,128)S(1)}, f32[1,2,1,64,2048]{4,3,2,1,0:T(8,128)S(1)}, f32[1,2,1,64,2048]{4,3,2,1,0:T(8,128)S(1)}) fusion(f32[1,2,1,64,2048]{4,3,2,1,0:T(8,128)S(1)} %copy-done, f32[1,2,1,64,2048]{4,3,2,1,0:T(8,128)S(1)} %copy.41, f32[2]{0:T(128)S(1)} %multiply_reduce_fusion, ...), kind=kLoop, calls=%fused_computation.34 | loop fusion | flops 3670016 | bytes 9437192 | tf_op jit(solution)/shard_map/sub | solution.py:32
  78.1 1.5 %copy.33 = bf16[1,2,64,2048,2]{2,4,3,1,0:T(2,128)(2,1)S(1)} copy(bf16[1,2,64,2048,2]{3,2,1,4,0:T(8,128)(2,1)S(1)} %pad_maximum_fusion) | data formatting | bytes 2097152 | tf_op jit(solution)/shard_map/stack | solution.py:52
  79.6 0.8 copy.34
  80.5 0.6 gather_fusion
  81.2 29.3 %all_to_all.10 = bf16[8,2,64,512]{3,2,1,0:T(8,128)(2,1)S(1)} all-to-all(bf16[8,2,64,512]{3,2,1,0:T(8,128)(2,1)S(1)} %bitcast.50), channel_id=1, replica_groups=mesh['swath'=2,'sub'=4,'beam'=2,'half'=2] {'sub','beam'}, dimensions={0} | all-to-all | bytes 2097152 | tf_op jit(solution)/shard_map/all_to_all | solution.py:86
  110.6 1.3 %copy.37 = bf16[1,1,2,512,512]{4,3,2,1,0:T(8,128)(2,1)} copy(bf16[1,1,2,512,512]{3,4,2,1,0:T(8,128)(2,1)S(1)} %bitcast.52) | data formatting | bytes 2097152 | tf_op jit(solution)/shard_map/reshape | solution.py:89
  (25 shorter events, 1.1 us)
Async XLA Ops:
  0.0 9.6 %copy-start.4 = (f32[4]{0:T(128)S(1)}, f32[4]{0:T(128)}, u32[]{:S(2)}) copy-start(f32[4]{0:T(128)} %param.6) | copy-start | bytes 52
  0.0 9.7 %copy-start.3 = (s32[2,4]{1,0:T(2,128)S(1)}, s32[2,4]{1,0:T(2,128)}, u32[]{:S(2)}) copy-start(s32[2,4]{1,0:T(2,128)} %param.7) | copy-start | bytes 100
  2.3 33.0 %all-to-all-start = ((bf16[8,2,64,512]{3,2,1,0:T(8,128)(2,1)}), bf16[8,2,64,512]{3,2,1,0:T(8,128)(2,1)S(1)}, u32[]{:S(2)}, u32[]{:S(2)}) async-start(bf16[8,2,64,512]{3,2,1,0:T(8,128)(2,1)} %copy.26), calls=%async_computation | async-start | bytes 2097152 | tf_op jit(solution)/shard_map/all_to_all | solution.py:69
  37.2 1.6 %copy-start.5 = (bf16[1024,1024,1,1,1]{1,0,4,3,2:T(8,128)(2,1)S(1)}, bf16[1024,1024,1,1,1]{1,0,4,3,2:T(8,128)(2,1)}, u32[]{:S(2)}) copy-start(bf16[1024,1024,1,1,1]{1,0,4,3,2:T(8,128)(2,1)} %constant.79) | copy-start | bytes 6291460
  63.9 5.9 %copy-start = (f32[1,2,1,64,2048]{4,3,2,1,0:T(8,128)S(1)}, f32[1,2,1,64,2048]{4,3,2,1,0:T(8,128)}, u32[]{:S(2)}) copy-start(f32[1,2,1,64,2048]{4,3,2,1,0:T(8,128)} %copy.42) | copy-start | bytes 3145732
  63.9 5.9 %copy-start.1 = (f32[64,2048]{1,0:T(8,128)S(1)}, f32[64,2048]{1,0:T(8,128)}, u32[]{:S(2)}) copy-start(f32[64,2048]{1,0:T(8,128)} %get-tuple-element.19) | copy-start | bytes 1572868
  63.9 5.9 %copy-start.2 = (f32[64,2048]{1,0:T(8,128)S(1)}, f32[64,2048]{1,0:T(8,128)}, u32[]{:S(2)}) copy-start(f32[64,2048]{1,0:T(8,128)} %get-tuple-element.20) | copy-start | bytes 1572868

commit v3 on v2

v3 whole, which is shorter than its diff:
```python
import math

import jax
import numpy as np
import jax.numpy as jnp
from jax import lax
from jax.sharding import Mesh
from jax.sharding import PartitionSpec as P

B = 1024
NR = 1024
GROUP_SUBS = 4


def odd_values(beam_total):
    spacing = np.arange(beam_total, dtype=np.int64)[None, :] - np.arange(beam_total, dtype=np.int64)[:, None]
    parity = np.where(spacing % 2 == 0, 1.0, -1.0).astype(np.float32)
    angles = (2.0 * spacing.astype(np.float32) + np.float32(1.0)) * np.float32(math.pi / (2.0 * beam_total))
    values = parity * np.cos(angles) / (np.float32(beam_total) * np.sin(angles))
    return values.astype(np.float32).astype(jnp.bfloat16)


def split_order(beam_total):
    return np.concatenate([np.arange(0, beam_total, 2), np.arange(1, beam_total, 2)])


def spin(parts, scale, lead, first_at, beams_out):
    count = parts.shape[-1]
    lanes = 128
    coarse = jnp.asarray(
        (2.0 * lead * lanes / beams_out) * np.arange(count // lanes) + ((2 * first_at + 1) / beams_out - 1.0),
        jnp.float32,
    )
    fine = jnp.asarray((2.0 * lead / beams_out) * np.arange(lanes), jnp.float32)
    rough = scale[..., None] * coarse
    small = scale[..., None] * fine
    c1 = jnp.cos(rough)[..., None]
    s1 = jnp.sin(rough)[..., None]
    c2 = jnp.cos(small)[..., None, :]
    s2 = jnp.sin(small)[..., None, :]
    cosine = c1 * c2 - s1 * s2
    sines = s1 * c2 + c1 * s2
    grid = parts.shape[:-3] + (parts.shape[-2], count // lanes, lanes)
    real_part = parts[..., 0, :, :].reshape(grid)
    imag_part = parts[..., 1, :, :].reshape(grid)
    turned = jnp.stack(
        [real_part * cosine - imag_part * sines, real_part * sines + imag_part * cosine], -4
    )
    return turned.reshape(parts.shape)


def odd_local(children, kernel):
    product = jnp.dot(
        children.reshape(-1, children.shape[-1]), kernel, preferred_element_type=jnp.float32
    )
    return product.reshape(children.shape[:-1] + (kernel.shape[1],))


def body(images, offsets, owners):
    group_count = lax.axis_size("grp")
    sub_count = group_count * GROUP_SUBS
    beam_count = lax.axis_size("beam")
    group_at = lax.axis_index("grp")
    member_at = lax.axis_index("sub4") * beam_count + lax.axis_index("beam")
    half_side = lax.axis_index("half")
    members = GROUP_SUBS * beam_count
    half_rows = images.shape[2]
    own_rows = half_rows // members
    local_beams = images.shape[3]

    pieces = images[0].reshape(2, members, own_rows, local_beams).transpose(1, 0, 2, 3)
    gathered = lax.all_to_all(pieces, ("sub4", "beam"), 0, 0, tiled=True)
    gathered = gathered.reshape(GROUP_SUBS, beam_count, 2, own_rows, local_beams)
    children = gathered.transpose(0, 2, 3, 1, 4)
    rows_at = half_side * half_rows + member_at * own_rows + jnp.arange(own_rows, dtype=jnp.int32)
    ratios = NR / (NR + rows_at.astype(jnp.float32))
    shifts = lax.dynamic_slice_in_dim(offsets, group_at * GROUP_SUBS, GROUP_SUBS, 0)
    children = children.reshape(GROUP_SUBS, 2, own_rows, B)
    scale_one = shifts[:, None] * ratios[None, :]
    odd_one = odd_local(children, jnp.asarray(odd_values(B)))
    even_one = spin(children.astype(jnp.float32), scale_one, 2, 0, 2 * B)
    odd_one = spin(odd_one, scale_one, 2, 1, 2 * B)
    pairs = (GROUP_SUBS // 2, 2, 2, own_rows, B)
    first = jnp.concatenate(
        [even_one.reshape(pairs).sum(1), odd_one.reshape(pairs).sum(1)], -1
    ).astype(jnp.bfloat16)
    order = split_order(2 * B)
    kernel_two = jnp.asarray(odd_values(2 * B)[order][:, order])
    centers = (shifts[0::2] + shifts[1::2]) * 0.5
    scale_two = centers[:, None] * ratios[None, :]
    odd_two = odd_local(first, kernel_two)
    first_f = first.astype(jnp.float32)
    merged = jnp.stack(
        [
            spin(first_f[..., :B], scale_two, 4, 0, 4 * B).sum(0),
            spin(odd_two[..., :B], scale_two, 4, 1, 4 * B).sum(0),
            spin(first_f[..., B:], scale_two, 4, 2, 4 * B).sum(0),
            spin(odd_two[..., B:], scale_two, 4, 3, 4 * B).sum(0),
        ]
    ).astype(jnp.bfloat16)

    sector_width = 4 * B // (beam_count * sub_count)
    tiles = merged.reshape(4, 2, own_rows, beam_count, sub_count, sector_width // 4)
    beam_ids = jnp.arange(beam_count, dtype=jnp.int32)[:, None]
    picked = tiles[:, :, :, beam_ids, owners, :]
    outgoing = picked.transpose(4, 3, 1, 5, 0, 2).reshape(
        sub_count * beam_count, 2, sector_width, own_rows
    )
    received = lax.all_to_all(outgoing, ("grp", "sub4", "beam"), 0, 0, tiled=True)
    received = received.reshape(group_count, members, 2, sector_width, own_rows)
    received = received.transpose(0, 2, 3, 1, 4)
    return received.reshape(1, group_count, 2, sector_width, members * own_rows)


def solution(mesh):
    shape = dict(mesh.shape)
    devices = mesh.devices.reshape(
        shape["swath"], shape["sub"] // GROUP_SUBS, GROUP_SUBS, shape["beam"], shape["half"]
    )
    split = Mesh(devices, ("swath", "grp", "sub4", "beam", "half"))
    placed = (P(("grp", "sub4"), None, ("swath", "half"), "beam"), P(), P())
    return jax.shard_map(
        body,
        mesh=split,
        in_specs=placed,
        out_specs=P(("grp", "sub4", "beam"), None, None, None, ("swath", "half")),
        check_vma=False,
    )
```

time: 112 us -> 87.6 us (0.78)
  waiting for transfers between devices: 24 us -> 2.04 us
  other arithmetic: 18.5 us -> 11 us
  local copies, waits for them, and re-layouts: 25.5 us -> 29.8 us
    all_to_all x1, waiting for transfers between devices: 24 us -> 2.04 us  [body(): gathered = lax.all_to_all(pieces, ('sub4', 'beam'), 0, 0, tiled=True)]
    sub x4, other arithmetic: 16 us -> 2.18 us  [spin(): real_part * cosine - imag_part * sines]
    sub x0 -> x6, local copies, waits for them, and re-layouts: none -> 7.99 us  [spin(): cosine = c1 * c2 - s1 * s2]
    add x0 -> x6, local copies, waits for them, and re-layouts: none -> 7.59 us  [spin(): sines = s1 * c2 + c1 * s2]
    convert_element_type x3 -> x0, local copies, waits for them, and re-layouts: 6.38 us -> none  [the longest x1 4.04 us: merge_pairs(): children.astype(jnp.float32)]
    add x0 -> x2, other arithmetic: none -> 4.86 us  [spin(): sines = s1 * c2 + c1 * s2]
    slice x1 -> x4, local copies, waits for them, and re-layouts: 4.47 us -> 0.67 us  [the longest x2 0.49 us: spin(): real_part = parts[..., 0, :, :].reshape(grid)]
    cos x0 -> x4, other arithmetic: none -> 2.81 us  [the longest x2 1.97 us: spin(): c1 = jnp.cos(rough)[..., None]]
  transfers between devices with their start and end apart: 1 -> 1, of which waited for: 1 -> 1; matrix products, arithmetic and copies ran while one was open for 2% -> 27% of each run, Pallas kernels for 0% -> 0%
where the time goes in v3:
time: 87.6 us; the launch traced here: 86.9 us
  local copies, waits for them, and re-layouts  29.8 us (34%)
  blocking collectives  29.3 us (33%)
  other arithmetic  11 us (13%)
  starting transfers between devices  7.28 us (8%)
  matrix products  7.06 us (8%)
  waiting for transfers between devices  2.04 us (2%)
    all_to_all x1, blocking collectives, body(): lax.all_to_all(outgoing, ('grp', 'sub4', 'beam'), 0, 0, tiled=True)  29.3 us
    sub x6, local copies, waits for them, and re-layouts, spin(): cosine = c1 * c2 - s1 * s2  7.99 us
    add x6, local copies, waits for them, and re-layouts, spin(): sines = s1 * c2 + c1 * s2  7.59 us
    all_to_all x1, starting transfers between devices, body(): gathered = lax.all_to_all(pieces, ('sub4', 'beam'), 0, 0, tiled=True)  7.28 us
    dot_general x2, matrix products, odd_local(): jnp.dot(children.reshape(-1, children.shape[-1]), kernel, preferred_eleme...  7.06 us
    add x2, other arithmetic, spin(): sines = s1 * c2 + c1 * s2  4.86 us
    unnamed x40, local copies, waits for them, and re-layouts  4.57 us
    transpose x1, local copies, waits for them, and re-layouts, body(): images[0].reshape(2, members, own_rows, local_beams).transpose(1, 0, 2, 3)  2.34 us
  transfers between devices with their start and end apart: 1, of which 1 were waited for; matrix products, arithmetic and copies ran while one was open for 27% of the time, Pallas kernels for 0%

profile of v3, /device:TPU:0, one launch (start us, length us, event | category | flops | bytes accessed | tf_op | source)
XLA Modules:
  0.0 86.9 jit_solution(11481019598954251960)
XLA Ops:
  0.0 2.3 %copy.29 = bf16[8,2,64,512]{3,2,1,0:T(8,128)(2,1)} copy(bf16[8,2,64,512]{3,2,0,1:T(8,128)(2,1)} %bitcast.71) | data formatting | bytes 2097152 | tf_op jit(solution)/shard_map/transpose | solution.py:71
  2.4 7.3 %all-to-all-start = ((bf16[8,2,64,512]{3,2,1,0:T(8,128)(2,1)}), bf16[8,2,64,512]{3,2,1,0:T(8,128)(2,1)}, u32[]{:S(2)}, u32[]{:S(2)}) async-start(bf16[8,2,64,512]{3,2,1,0:T(8,128)(2,1)} %copy.29), calls=%async_computation | async-start | bytes 2097152 | tf_op jit(solution)/shard_map/all_to_all | solution.py:72
  10.5 1.0 %multiply_cosine_fusion.2 = (f32[4,64,8]{2,1,0:T(8,128)S(1)}, f32[4,64,8]{2,1,0:T(8,128)S(1)}, f32[4,64,8]{2,1,0:T(8,128)S(1)}, f32[4,64,8]{2,1,0:T(8,128)S(1)}) fusion(f32[8]{0:T(128)S(1)} %copy-done.17, f32[4,64]{1,0:T(4,128)S(1)} %broadcast_multiply_fusion, f32[8]{0:T(128)S(1)} %copy-done.18), kind=kLoop, calls=%fused_computation.43 | loop fusion | flops 4096 | bytes 33856 | tf_op jit(solution)/shard_map/cos | solution.py:37
  11.5 2.4 %multiply_add_fusion.3 = (f32[4,64,8,128]{3,2,1,0:T(8,128)S(1)}, f32[4,64,8,128]{3,2,1,0:T(8,128)S(1)}, f32[4,64,8,128]{3,2,1,0:T(8,128)S(1)}, f32[4,64,8,128]{3,2,1,0:T(8,128)}) fusion(f32[4,64,128]{2,1,0:T(8,128)S(1)} %get-tuple-element.48, f32[4,64,8]{2,1,0:T(8,128)S(1)} %get-tuple-element.46, f32[4,64,128]{2,1,0:T(8,128)S(1)} %get-tuple-element.47, ...), kind=kLoop, calls=%fused_computation.18 | loop fusion | flops 3145728 | bytes 4489216 | tf_op jit(solution)/shard_map/add | solution.py:42
  13.9 2.4 %add.184 = f32[2,2,1,64,1024]{4,3,1,0,2:T(8,128)} reshape(f32[4,64,8,128]{3,2,1,0:T(8,128)} %get-tuple-element.36) | data formatting | bytes 2097152 | tf_op jit(solution)/shard_map/add | solution.py:42
  16.3 1.1 %sub.148 = f32[2,2,1,64,1024]{4,3,1,0,2:T(8,128)} reshape(f32[4,64,8,128]{3,2,1,0:T(8,128)S(1)} %get-tuple-element.35) | data formatting | bytes 2097152 | tf_op jit(solution)/shard_map/sub | solution.py:41
  18.2 1.0 %multiply_cosine_fusion.7 = (f32[2,64,8]{2,1,0:T(8,128)S(1)}, f32[2,64,8]{2,1,0:T(8,128)S(1)}, f32[2,64,8]{2,1,0:T(8,128)S(1)}, f32[2,64,8]{2,1,0:T(8,128)S(1)},...) fusion(f32[8]{0:T(128)S(1)} %copy-done.13, ...), kind=kLoop, calls=%fused_computation.53 | loop fusion | flops 4096 | bytes 33408 | tf_op jit(solution)/shard_map/cos | solution.py:37
  19.2 2.4 %multiply_add_fusion.11 = (f32[2,64,8,128]{3,2,1,0:T(8,128)}, f32[2,64,8,128]{3,2,1,0:T(8,128)}, f32[2,64,8,128]{3,2,1,0:T(8,128)}, f32[2,64,8,128]{3,2,1,0:T(8,...) fusion(f32[2,64,128]{2,1,0:T(8,128)S(1)} %get-tuple-element.60,, ...), kind=kLoop, calls=%fused_computation.36 | loop fusion | flops 3145728 | bytes 4358144 | tf_op jit(solution)/shard_map/add | solution.py:42
  21.6 1.9 %add.188 = f32[2,1,64,1024]{3,2,1,0:T(8,128)} reshape(f32[2,64,8,128]{3,2,1,0:T(8,128)} %get-tuple-element.29) | data formatting | bytes 1048576 | tf_op jit(solution)/shard_map/add | solution.py:42
  23.5 1.9 %add.194 = f32[2,1,64,1024]{3,2,1,0:T(8,128)} reshape(f32[2,64,8,128]{3,2,1,0:T(8,128)} %get-tuple-element.42) | data formatting | bytes 1048576 | tf_op jit(solution)/shard_map/add | solution.py:42
  25.4 1.9 %sub.151 = f32[2,1,64,1024]{3,2,1,0:T(8,128)} reshape(f32[2,64,8,128]{3,2,1,0:T(8,128)} %get-tuple-element.30) | data formatting | bytes 1048576 | tf_op jit(solution)/shard_map/sub | solution.py:41
  27.4 0.9 %sub.157 = f32[2,1,64,1024]{3,2,1,0:T(8,128)} reshape(f32[2,64,8,128]{3,2,1,0:T(8,128)S(1)} %get-tuple-element.41) | data formatting | bytes 1048576 | tf_op jit(solution)/shard_map/sub | solution.py:41
  28.4 1.1 %add.197 = f32[2,1,64,1024]{3,2,1,0:T(8,128)S(1)} reshape(f32[2,64,8,128]{3,2,1,0:T(8,128)} %get-tuple-element.44) | data formatting | bytes 1048576 | tf_op jit(solution)/shard_map/add | solution.py:42
  29.5 1.9 %sub.154 = f32[2,1,64,1024]{3,2,1,0:T(8,128)} reshape(f32[2,64,8,128]{3,2,1,0:T(8,128)} %get-tuple-element.39) | data formatting | bytes 1048576 | tf_op jit(solution)/shard_map/sub | solution.py:41
  31.4 1.9 %sub.160 = f32[2,1,64,1024]{3,2,1,0:T(8,128)} reshape(f32[2,64,8,128]{3,2,1,0:T(8,128)} %get-tuple-element.43) | data formatting | bytes 1048576 | tf_op jit(solution)/shard_map/sub | solution.py:41
  33.5 2.0 %all-to-all-done = bf16[8,2,64,512]{3,2,1,0:T(8,128)(2,1)} async-done(((bf16[8,2,64,512]{3,2,1,0:T(8,128)(2,1)}), bf16[8,2,64,512]{3,2,1,0:T(8,128)(2,1)}, u32[]{:S(2)}, u32[]{:S(2)}) %all-to-all-start) | async-done | bytes 1048608 | tf_op jit(solution)/shard_map/all_to_all | solution.py:72
  35.5 1.3 %copy.43 = bf16[4,2,2,8,8,512]{5,4,1,3,2,0:T(8,128)(2,1)S(1)} copy(bf16[4,2,2,8,8,512]{5,4,3,2,1,0:T(8,128)(2,1)} %bitcast.27) | data formatting | bytes 2097152 | tf_op jit(solution)/shard_map/reshape | solution.py:78
  37.1 1.3 %copy-done.19 = bf16[1024,1024,1,1]{1,0,3,2:T(8,128)(2,1)S(1)} copy-done((bf16[1024,1024,1,1]{1,0,3,2:T(8,128)(2,1)S(1)}, bf16[1024,1024,1,1]{1,0,3,2:T(8,128)(2,1)}, u32[]{:S(2)}) %copy-start.19) | copy-done | bytes 2097176
  38.4 1.3 %convolution_bitcast_fusion = f32[4,2,64,1024]{3,2,1,0:T(8,128)S(1)} fusion(bf16[1024,1024,1,1]{1,0,3,2:T(8,128)(2,1)S(1)} %copy-done.19, bf16[4,2,64,1024]{3,2,1,0:T(8,128)(2,1)S(1)} %bitcast.63), kind=kOutput, calls=%fused_computation.3 | convolution fusion | flops 1073741824 | bytes 5242880 | tf_op jit(solution)/shard_map/dot_general | solution.py:53
  40.0 1.0 %copy-done = f32[2,2,1,64,1024]{4,3,1,0,2:T(8,128)S(1)} copy-done((f32[2,2,1,64,1024]{4,3,1,0,2:T(8,128)S(1)}, f32[2,2,1,64,1024]{4,3,1,0,2:T(8,128)}, u32[]{:S(2)}) %copy-start) | copy-done | bytes 1048600
  46.1 5.8 %fusion = f32[2,2,64,2048]{3,2,1,0:T(8,128)S(1)} fusion(bf16[2048,2048,1,1]{1,0,3,2:T(8,128)(2,1)} %constant.77, bf16[2,2,64,1024]{3,2,0,1:T(8,128)(2,1)S(1)} %maximum_reduce_fusion, bf16[2,2,64,1024]{3,2,0,1:T(8,128)(2,1)S(1)} %copy-done.9), kind=kOutput, calls=%fused_computation.20 | convolution fusion | flops 2149580800 | bytes 11534336 | tf_op jit(solution)/shard_map/dot_general | solution.py:53
  53.9 1.4 %copy.37 = bf16[4,2,2,128,4,64]{5,4,3,2,1,0:T(4,128)(2,1)S(1)} copy(bf16[4,2,2,128,4,64]{3,5,2,4,0,1:T(8,128)(2,1)S(1)} %bitcast.65) | data formatting | bytes 2097152 | tf_op jit(solution)/shard_map/transpose | solution.py:106
  56.1 29.3 %all_to_all.10 = bf16[8,2,512,64]{2,3,1,0:T(8,128)(2,1)S(1)} all-to-all(bf16[8,2,512,64]{2,3,1,0:T(8,128)(2,1)S(1)} %copy.38), channel_id=1, replica_groups=mesh['swath'=2,'sub'=4,'beam'=2,'half'=2] {'sub','beam'}, dimensions={0} | all-to-all | bytes 2097152 | tf_op jit(solution)/shard_map/all_to_all | solution.py:109
  85.5 1.3 %copy.40 = bf16[1,1,2,512,512]{4,3,2,1,0:T(8,128)(2,1)} copy(bf16[1,1,2,512,512]{3,4,2,1,0:T(8,128)(2,1)S(1)} %bitcast.66) | data formatting | bytes 2097152 | tf_op jit(solution)/shard_map/reshape | solution.py:112
  (74 shorter events, 10.1 us)
Async XLA Ops:
  0.0 9.6 %copy-start.12 = (f32[4]{0:T(128)S(1)}, f32[4]{0:T(128)}, u32[]{:S(2)}) copy-start(f32[4]{0:T(128)} %param.18) | copy-start | bytes 52
  0.0 9.9 %copy-start.10 = (f32[128]{0:T(128)S(1)}, f32[128]{0:T(128)}, u32[]{:S(2)}) copy-start(f32[128]{0:T(128)} %constant.55.clone) | copy-start | bytes 1540
  0.0 10.4 %copy-start.17 = (f32[8]{0:T(128)S(1)}, f32[8]{0:T(128)}, u32[]{:S(2)}) copy-start(f32[8]{0:T(128)} %constant.54.clone) | copy-start | bytes 100
  0.0 10.5 %copy-start.18 = (f32[8]{0:T(128)S(1)}, f32[8]{0:T(128)}, u32[]{:S(2)}) copy-start(f32[8]{0:T(128)} %constant.56.clone) | copy-start | bytes 100
  2.4 33.2 %all-to-all-start = ((bf16[8,2,64,512]{3,2,1,0:T(8,128)(2,1)}), bf16[8,2,64,512]{3,2,1,0:T(8,128)(2,1)}, u32[]{:S(2)}, u32[]{:S(2)}) async-start(bf16[8,2,64,512]{3,2,1,0:T(8,128)(2,1)} %copy.29), calls=%async_computation | async-start | bytes 2097152 | tf_op jit(solution)/shard_map/all_to_all | solution.py:72
  17.4 0.7 copy-start.13
  17.4 0.8 copy-start.14
  17.4 0.8 copy-start.15
  17.4 0.8 copy-start.16
  28.3 5.1 %copy-start.11 = (s32[2,4]{1,0:T(2,128)S(1)}, s32[2,4]{1,0:T(2,128)}, u32[]{:S(2)}) copy-start(s32[2,4]{1,0:T(2,128)} %param.19) | copy-start | bytes 100
  36.9 1.6 %copy-start.19 = (bf16[1024,1024,1,1]{1,0,3,2:T(8,128)(2,1)S(1)}, bf16[1024,1024,1,1]{1,0,3,2:T(8,128)(2,1)}, u32[]{:S(2)}) copy-start(bf16[1024,1024,1,1]{1,0,3,2:T(8,128)(2,1)} %constant.76) | copy-start | bytes 6291460
  39.7 1.2 %copy-start = (f32[2,2,1,64,1024]{4,3,1,0,2:T(8,128)S(1)}, f32[2,2,1,64,1024]{4,3,1,0,2:T(8,128)}, u32[]{:S(2)}) copy-start(f32[2,2,1,64,1024]{4,3,1,0,2:T(8,128)} %add.184) | copy-start | bytes 3145732
  39.7 1.5 %copy-start.1 = (f32[2,2,1,64,1024]{4,3,1,0,2:T(8,128)S(1)}, f32[2,2,1,64,1024]{4,3,1,0,2:T(8,128)}, u32[]{:S(2)}) copy-start(f32[2,2,1,64,1024]{4,3,1,0,2:T(8,128)} %sub.148) | copy-start | bytes 3145732
  42.1 0.8 copy-start.8
  42.9 1.0 %copy-start.4 = (f32[2,1,64,1024]{3,2,1,0:T(8,128)S(1)}, f32[2,1,64,1024]{3,2,1,0:T(8,128)}, u32[]{:S(2)}) copy-start(f32[2,1,64,1024]{3,2,1,0:T(8,128)} %add.188) | copy-start | bytes 1572868
  42.9 1.2 %copy-start.5 = (f32[2,1,64,1024]{3,2,1,0:T(8,128)S(1)}, f32[2,1,64,1024]{3,2,1,0:T(8,128)}, u32[]{:S(2)}) copy-start(f32[2,1,64,1024]{3,2,1,0:T(8,128)} %add.194) | copy-start | bytes 1572868
  42.9 1.4 %copy-start.6 = (f32[2,1,64,1024]{3,2,1,0:T(8,128)S(1)}, f32[2,1,64,1024]{3,2,1,0:T(8,128)}, u32[]{:S(2)}) copy-start(f32[2,1,64,1024]{3,2,1,0:T(8,128)} %sub.151) | copy-start | bytes 1572868
  42.9 1.5 %copy-start.7 = (f32[2,1,64,1024]{3,2,1,0:T(8,128)S(1)}, f32[2,1,64,1024]{3,2,1,0:T(8,128)}, u32[]{:S(2)}) copy-start(f32[2,1,64,1024]{3,2,1,0:T(8,128)} %sub.157) | copy-start | bytes 1572868
  45.1 1.0 %copy-start.9 = (bf16[2,2,64,1024]{3,2,0,1:T(8,128)(2,1)S(1)}, bf16[2,2,64,1024]{3,2,0,1:T(8,128)(2,1)}, u32[]{:S(2)}) copy-start(bf16[2,2,64,1024]{3,2,0,1:T(8,128)(2,1)} %copy-done.8) | copy-start | bytes 1572868
  46.1 5.8 %copy-start.2 = (f32[2,1,64,1024]{3,2,1,0:T(8,128)S(1)}, f32[2,1,64,1024]{3,2,1,0:T(8,128)}, u32[]{:S(2)}) copy-start(f32[2,1,64,1024]{3,2,1,0:T(8,128)} %sub.154) | copy-start | bytes 1572868
  46.1 5.8 %copy-start.3 = (f32[2,1,64,1024]{3,2,1,0:T(8,128)S(1)}, f32[2,1,64,1024]{3,2,1,0:T(8,128)}, u32[]{:S(2)}) copy-start(f32[2,1,64,1024]{3,2,1,0:T(8,128)} %sub.160) | copy-start | bytes 1572868

commit v4 on v3

--- a/solution.py
+++ b/solution.py
@@ -10,6 +10,7 @@
 B = 1024
 NR = 1024
 GROUP_SUBS = 4
+CHUNKS = 2
 
 
 def odd_values(beam_total):
@@ -56,6 +57,34 @@
     return product.reshape(children.shape[:-1] + (kernel.shape[1],))
 
 
+def merge_rows(children, offsets, rows_at, group_at):
+    ratios = NR / (NR + rows_at.astype(jnp.float32))
+    shifts = lax.dynamic_slice_in_dim(offsets, group_at * GROUP_SUBS, GROUP_SUBS, 0)
+    rows = children.shape[2]
+    scale_one = shifts[:, None] * ratios[None, :]
+    odd_one = odd_local(children, jnp.asarray(odd_values(B)))
+    even_one = spin(children.astype(jnp.float32), scale_one, 2, 0, 2 * B)
+    odd_one = spin(odd_one, scale_one, 2, 1, 2 * B)
+    pairs = (GROUP_SUBS // 2, 2, 2, rows, B)
+    first = jnp.concatenate(
+        [even_one.reshape(pairs).sum(1), odd_one.reshape(pairs).sum(1)], -1
+    ).astype(jnp.bfloat16)
+    order = split_order(2 * B)
+    kernel_two = jnp.asarray(odd_values(2 * B)[order][:, order])
+    centers = (shifts[0::2] + shifts[1::2]) * 0.5
+    scale_two = centers[:, None] * ratios[None, :]
+    odd_two = odd_local(first, kernel_two)
+    first_f = first.astype(jnp.float32)
+    return jnp.stack(
+        [
+            spin(first_f[..., :B], scale_two, 4, 0, 4 * B).sum(0),
+            spin(odd_two[..., :B], scale_two, 4, 1, 4 * B).sum(0),
+            spin(first_f[..., B:], scale_two, 4, 2, 4 * B).sum(0),
+            spin(odd_two[..., B:], scale_two, 4, 3, 4 * B).sum(0),
+        ]
+    ).astype(jnp.bfloat16)
+
+
 def body(images, offsets, owners):
     group_count = lax.axis_size("grp")
     sub_count = group_count * GROUP_SUBS
@@ -66,47 +95,32 @@
     members = GROUP_SUBS * beam_count
     half_rows = images.shape[2]
     own_rows = half_rows // members
+    chunks = CHUNKS if own_rows % (8 * CHUNKS) == 0 else 1
+    chunk_rows = own_rows // chunks
     local_beams = images.shape[3]
-
-    pieces = images[0].reshape(2, members, own_rows, local_beams).transpose(1, 0, 2, 3)
-    gathered = lax.all_to_all(pieces, ("sub4", "beam"), 0, 0, tiled=True)
-    gathered = gathered.reshape(GROUP_SUBS, beam_count, 2, own_rows, local_beams)
-    children = gathered.transpose(0, 2, 3, 1, 4)
-    rows_at = half_side * half_rows + member_at * own_rows + jnp.arange(own_rows, dtype=jnp.int32)
-    ratios = NR / (NR + rows_at.astype(jnp.float32))
-    shifts = lax.dynamic_slice_in_dim(offsets, group_at * GROUP_SUBS, GROUP_SUBS, 0)
-    children = children.reshape(GROUP_SUBS, 2, own_rows, B)
-    scale_one = shifts[:, None] * ratios[None, :]
-    odd_one = odd_local(children, jnp.asarray(odd_values(B)))
-    even_one = spin(children.astype(jnp.float32), scale_one, 2, 0, 2 * B)
-    odd_one = spin(odd_one, scale_one, 2, 1, 2 * B)
-    pairs = (GROUP_SUBS // 2, 2, 2, own_rows, B)
-    first = jnp.concatenate(
-        [even_one.reshape(pairs).sum(1), odd_one.reshape(pairs).sum(1)], -1
-    ).astype(jnp.bfloat16)
-    order = split_order(2 * B)
-    kernel_two = jnp.asarray(odd_values(2 * B)[order][:, order])
-    centers = (shifts[0::2] + shifts[1::2]) * 0.5
-    scale_two = centers[:, None] * ratios[None, :]
-    odd_two = odd_local(first, kernel_two)
-    first_f = first.astype(jnp.float32)
-    merged = jnp.stack(
-        [
-            spin(first_f[..., :B], scale_two, 4, 0, 4 * B).sum(0),
-            spin(odd_two[..., :B], scale_two, 4, 1, 4 * B).sum(0),
-            spin(first_f[..., B:], scale_two, 4, 2, 4 * B).sum(0),
-            spin(odd_two[..., B:], scale_two, 4, 3, 4 * B).sum(0),
-        ]
-    ).astype(jnp.bfloat16)
-
     sector_width = 4 * B // (beam_count * sub_count)
-    tiles = merged.reshape(4, 2, own_rows, beam_count, sub_count, sector_width // 4)
     beam_ids = jnp.arange(beam_count, dtype=jnp.int32)[:, None]
-    picked = tiles[:, :, :, beam_ids, owners, :]
-    outgoing = picked.transpose(4, 3, 1, 5, 0, 2).reshape(
-        sub_count * beam_count, 2, sector_width, own_rows
-    )
-    received = lax.all_to_all(outgoing, ("grp", "sub4", "beam"), 0, 0, tiled=True)
+    split_rows = images[0].reshape(2, members, chunks, chunk_rows, local_beams)
+    results = []
+    for chunk in range(chunks):
+        pieces = split_rows[:, :, chunk].transpose(1, 0, 2, 3)
+        gathered = lax.all_to_all(pieces, ("sub4", "beam"), 0, 0, tiled=True)
+        gathered = gathered.reshape(GROUP_SUBS, beam_count, 2, chunk_rows, local_beams)
+        children = gathered.transpose(0, 2, 3, 1, 4).reshape(GROUP_SUBS, 2, chunk_rows, B)
+        rows_at = (
+            half_side * half_rows
+            + member_at * own_rows
+            + chunk * chunk_rows
+            + jnp.arange(chunk_rows, dtype=jnp.int32)
+        )
+        merged = merge_rows(children, offsets, rows_at, group_at)
+        tiles = merged.reshape(4, 2, chunk_rows, beam_count, sub_count, sector_width // 4)
+        picked = tiles[:, :, :, beam_ids, owners, :]
+        outgoing = picked.transpose(4, 3, 1, 5, 0, 2).reshape(
+            sub_count * beam_count, 2, sector_width, chunk_rows
+        )
+        results.append(lax.all_to_all(outgoing, ("grp", "sub4", "beam"), 0, 0, tiled=True))
+    received = jnp.stack(results, -2)
     received = received.reshape(group_count, members, 2, sector_width, own_rows)
     received = received.transpose(0, 2, 3, 1, 4)
     return received.reshape(1, group_count, 2, sector_width, members * own_rows)

time: 87.6 us -> 109 us (1.24)
  local copies, waits for them, and re-layouts: 29.8 us -> 42.5 us
  starting transfers between devices: 7.28 us -> 19.4 us
  blocking collectives: 29.3 us -> 17.9 us
  matrix products: 7.06 us -> 14.4 us
  waiting for transfers between devices: 2.04 us -> 0.73 us
  other arithmetic: 11 us -> 12.1 us
    all_to_all x1, blocking collectives: 29.3 us -> 17.9 us  [body(): lax.all_to_all(outgoing, ('grp', 'sub4', 'beam'), 0, 0, tiled=True)]
    dot_general x2 -> x4, matrix products: 7.06 us -> 14.4 us  [odd_local(): jnp.dot(children.reshape(-1, children.shape[-1]), kernel, preferred_eleme...]
    all_to_all x0 -> x1, starting transfers between devices: none -> 6.12 us  [body(): lax.all_to_all(outgoing, ('grp', 'sub4', 'beam'), 0, 0, tiled=True)]
    all_to_all x1 -> x2, starting transfers between devices: 7.28 us -> 13.3 us  [body(): gathered = lax.all_to_all(pieces, ('sub4', 'beam'), 0, 0, tiled=True)]
    slice x2 -> x4, local copies, waits for them, and re-layouts: 0.49 us -> 3.64 us  [spin(): real_part = parts[..., 0, :, :].reshape(grid)]
    transpose x1 -> x4, local copies, waits for them, and re-layouts: 2.34 us -> 5 us  [the longest x3 4.91 us: body(): pieces = split_rows[:, :, chunk].transpose(1, 0, 2, 3)]
    add x6 -> x12, local copies, waits for them, and re-layouts: 7.59 us -> 9.93 us  [spin(): sines = s1 * c2 + c1 * s2]
    all_to_all x1 -> x2, waiting for transfers between devices: 2.04 us -> 0.01 us  [body(): gathered = lax.all_to_all(pieces, ('sub4', 'beam'), 0, 0, tiled=True)]
  transfers between devices with their start and end apart: 1 -> 3, of which waited for: 1 -> 1; matrix products, arithmetic and copies ran while one was open for 27% -> 40% of each run, Pallas kernels for 0% -> 0%
where the time goes in v4:
time: 109 us; the launch traced here: 108 us
  local copies, waits for them, and re-layouts  42.5 us (39%)
  starting transfers between devices  19.4 us (18%)
  blocking collectives  17.9 us (16%)
  matrix products  14.4 us (13%)
  other arithmetic  12.1 us (11%)
    all_to_all x1, blocking collectives, body(): lax.all_to_all(outgoing, ('grp', 'sub4', 'beam'), 0, 0, tiled=True)  17.9 us
    dot_general x4, matrix products, odd_local(): jnp.dot(children.reshape(-1, children.shape[-1]), kernel, preferred_eleme...  14.4 us
    all_to_all x2, starting transfers between devices, body(): gathered = lax.all_to_all(pieces, ('sub4', 'beam'), 0, 0, tiled=True)  13.3 us
    add x12, local copies, waits for them, and re-layouts, spin(): sines = s1 * c2 + c1 * s2  9.93 us
    sub x12, local copies, waits for them, and re-layouts, spin(): cosine = c1 * c2 - s1 * s2  9.75 us
    all_to_all x1, starting transfers between devices, body(): lax.all_to_all(outgoing, ('grp', 'sub4', 'beam'), 0, 0, tiled=True)  6.12 us
    unnamed x80, local copies, waits for them, and re-layouts  5.54 us
    transpose x3, local copies, waits for them, and re-layouts, body(): pieces = split_rows[:, :, chunk].transpose(1, 0, 2, 3)  4.91 us
  transfers between devices with their start and end apart: 3, of which 1 were waited for; matrix products, arithmetic and copies ran while one was open for 40% of the time, Pallas kernels for 0%

profile of v4, /device:TPU:0, one launch (start us, length us, event | category | flops | bytes accessed | tf_op | source)
XLA Modules:
  0.0 107.9 jit_solution(2005216168161892727)
XLA Ops:
  0.0 2.1 %slice_bitcast_fusion.1 = (bf16[8,2,32,512]{3,2,0,1:T(8,128)(2,1)S(1)}, bf16[8,2,32,512]{3,2,0,1:T(8,128)(2,1)}) fusion(bf16[2,8,2,32,512]{4,3,2,1,0:T(8,128)(2,1)} %bitcast.132), kind=kLoop, calls=%fused_computation.10 | loop fusion | bytes 2097152 | tf_op jit(solution)/shard_map/transpose | solution.py:106
  3.0 7.3 %all-to-all-start = ((bf16[8,2,32,512]{3,2,1,0:T(8,128)(2,1)}), bf16[8,2,32,512]{3,2,1,0:T(8,128)(2,1)S(1)}, u32[]{:S(2)}, u32[]{:S(2)}) async-start(bf16[8,2,32,512]{3,2,1,0:T(8,128)(2,1)} %copy.54), calls=%async_computation | async-start | bytes 1048576 | tf_op jit(solution)/shard_map/all_to_all | solution.py:107
  11.1 1.0 multiply_cosine_fusion.2
  15.6 1.8 %multiply_cosine_fusion.10 = (f32[2,32,8]{2,1,0:T(8,128)}, f32[2,32,8]{2,1,0:T(8,128)}, f32[2,32,8]{2,1,0:T(8,128)}, f32[2,32,8]{2,1,0:T(8,128)}, f32[2,32,8]{2,...) fusion(f32[2,32]{1,0:T(2,128)S(1)} %get-tuple-element.154, ...), kind=kLoop, calls=%fused_computation.100 | loop fusion | flops 4096 | bytes 33408 | tf_op jit(solution)/shard_map/cos | solution.py:38
  27.3 1.9 %copy.64 = bf16[8,2,32,512]{3,2,1,0:T(8,128)(2,1)} copy(bf16[8,2,32,512]{3,2,0,1:T(8,128)(2,1)} %get-tuple-element.36) | data formatting | bytes 1048576 | tf_op jit(solution)/shard_map/transpose | solution.py:106
  30.2 6.0 %all-to-all-start.2 = ((bf16[8,2,32,512]{3,2,1,0:T(8,128)(2,1)}), bf16[8,2,32,512]{3,2,1,0:T(8,128)(2,1)S(1)}, u32[]{:S(2)}, u32[]{:S(2)}) async-start(bf16[8,2,32,512]{3,2,1,0:T(8,128)(2,1)} %copy.64), calls=%async_computation.2 | async-start | bytes 1048576 | tf_op jit(solution)/shard_map/all_to_all | solution.py:107
  36.3 2.3 %multiply_add_fusion.15 = (f32[2,32,8,128]{3,2,1,0:T(8,128)}, f32[2,32,8,128]{3,2,1,0:T(8,128)}, f32[2,32,8,128]{3,2,1,0:T(8,128)S(1)}, f32[2,32,8,128]{3,2,1,0:...) fusion(f32[2,32,128]{2,1,0:T(8,128)} %get-tuple-element.151, ...), kind=kLoop, calls=%fused_computation.61 | loop fusion | flops 1572864 | bytes 2179072 | tf_op jit(solution)/shard_map/add | solution.py:43
  38.5 1.7 %add.380 = f32[2,1,32,1024]{3,2,1,0:T(8,128)} reshape(f32[2,32,8,128]{3,2,1,0:T(8,128)} %get-tuple-element.65) | data formatting | bytes 524288 | tf_op jit(solution)/shard_map/add | solution.py:43
  40.3 1.7 %add.386 = f32[2,1,32,1024]{3,2,1,0:T(8,128)} reshape(f32[2,32,8,128]{3,2,1,0:T(8,128)} %get-tuple-element.84) | data formatting | bytes 524288 | tf_op jit(solution)/shard_map/add | solution.py:43
  42.0 1.7 %sub.313 = f32[2,1,32,1024]{3,2,1,0:T(8,128)} reshape(f32[2,32,8,128]{3,2,1,0:T(8,128)} %get-tuple-element.66) | data formatting | bytes 524288 | tf_op jit(solution)/shard_map/sub | solution.py:42
  46.8 1.1 %fusion.12 = (f32[4,1,32,1024]{3,2,1,0:T(8,128)}, f32[4,1,32,1024]{3,2,1,0:T(8,128)}) fusion(bf16[4,2,32,1024]{3,2,1,0:T(8,128)(2,1)S(1)} %bitcast.115), kind=kLoop, calls=%fused_computation.127 | loop fusion | bytes 2097152 | tf_op jit(solution)/shard_map/slice | solution.py:45
  48.7 1.7 %convolution_bitcast_fusion.1 = f32[4,2,32,1024]{3,2,1,0:T(8,128)} fusion(bf16[1024,1024,1,1]{1,0,3,2:T(8,128)(2,1)S(1)} %copy-done.39, bf16[4,2,32,1024]{3,2,1,0:T(8,128)(2,1)S(1)} %bitcast.116), kind=kOutput, calls=%fused_computation.3 | convolution fusion | flops 536870912 | bytes 3670016 | tf_op jit(solution)/shard_map/dot_general | solution.py:54
  50.5 3.3 %convolution_bitcast_fusion = f32[4,2,32,1024]{3,2,1,0:T(8,128)} fusion(bf16[1024,1024,1,1]{1,0,3,2:T(8,128)(2,1)} %constant.91, bf16[4,2,32,1024]{3,2,1,0:T(8,128)(2,1)S(1)} %bitcast.113), kind=kOutput, calls=%fused_computation.2 | convolution fusion | flops 536870912 | bytes 3670016 | tf_op jit(solution)/shard_map/dot_general | solution.py:54
  53.8 1.2 %fusion.13 = (f32[4,1,32,1024]{3,2,1,0:T(8,128)}, f32[4,1,32,1024]{3,2,1,0:T(8,128)}) fusion(bf16[4,2,32,1024]{3,2,1,0:T(8,128)(2,1)S(1)} %bitcast.114), kind=kLoop, calls=%fused_computation.128 | loop fusion | bytes 2097152 | tf_op jit(solution)/shard_map/slice | solution.py:45
  58.9 4.7 %fusion.2 = f32[2,2,32,2048]{3,2,1,0:T(8,128)S(1)} fusion(bf16[2048,2048,1,1]{1,0,3,2:T(8,128)(2,1)} %constant.92, bf16[2,2,32,1024]{3,2,0,1:T(8,128)(2,1)S(1)} %maximum_reduce_fusion, bf16[2,2,32,1024]{3,2,0,1:T(8,128)(2,1)S(1)} %maximum_reduce_fusion.1), kind=kOutput, calls=%fused_computation.45 | convolution fusion | flops 1074790400 | bytes 9961472 | tf_op jit(solution)/shard_map/dot_general | solution.py:54
  65.0 1.3 %copy.62 = bf16[4,2,2,128,4,32]{5,4,3,2,1,0:T(4,128)(2,1)S(1)} copy(bf16[4,2,2,128,4,32]{3,5,2,4,0,1:T(8,128)(2,1)S(1)} %bitcast.120) | data formatting | bytes 1048576 | tf_op jit(solution)/shard_map/transpose | solution.py:119
  66.3 1.5 %copy.63 = bf16[8,2,512,32]{2,3,1,0:T(8,128)(2,1)} copy(bf16[8,2,512,32]{3,2,1,0:T(8,128)(2,1)S(1)} %bitcast.111) | data formatting | bytes 1048576 | tf_op jit(solution)/shard_map/reshape | solution.py:119
  67.8 6.1 %all-to-all-start.1 = ((bf16[8,2,512,32]{2,3,1,0:T(8,128)(2,1)}), bf16[8,2,512,32]{2,3,1,0:T(8,128)(2,1)}, u32[]{:S(2)}, u32[]{:S(2)}) async-start(bf16[8,2,512,32]{2,3,1,0:T(8,128)(2,1)} %copy.63), calls=%async_computation.1 | async-start | bytes 1048576 | tf_op jit(solution)/shard_map/all_to_all | solution.py:122
  73.9 1.3 %fusion.11 = (f32[4,1,32,1024]{3,2,1,0:T(8,128)S(1)}, f32[4,1,32,1024]{3,2,1,0:T(8,128)S(1)}) fusion(f32[4,2,32,1024]{3,2,1,0:T(8,128)} %convolution_bitcast_fusion), kind=kLoop, calls=%fused_computation.126 | loop fusion | bytes 2097152 | tf_op jit(solution)/shard_map/slice | solution.py:45
  78.5 4.7 %fusion = f32[2,2,32,2048]{3,2,1,0:T(8,128)S(1)} fusion(bf16[2048,2048,1,1]{1,0,3,2:T(8,128)(2,1)} %constant.92, bf16[2,2,32,1024]{3,2,0,1:T(8,128)(2,1)S(1)} %maximum_reduce_fusion.2, bf16[2,2,32,1024]{3,2,0,1:T(8,128)(2,1)S(1)} %maximum_reduce_fusion.3), kind=kOutput, calls=%fused_computation.43 | convolution fusion | flops 1074790400 | bytes 9961472 | tf_op jit(solution)/shard_map/dot_general | solution.py:54
  84.6 1.3 %copy.72 = bf16[4,2,2,128,4,32]{5,4,3,2,1,0:T(4,128)(2,1)S(1)} copy(bf16[4,2,2,128,4,32]{3,5,2,4,0,1:T(8,128)(2,1)S(1)} %bitcast.119) | data formatting | bytes 1048576 | tf_op jit(solution)/shard_map/transpose | solution.py:119
  87.4 17.9 %all_to_all.20 = bf16[8,2,512,32]{2,3,1,0:T(8,128)(2,1)S(1)} all-to-all(bf16[8,2,512,32]{2,3,1,0:T(8,128)(2,1)S(1)} %copy.73), channel_id=1, replica_groups=mesh['swath'=2,'sub'=4,'beam'=2,'half'=2] {'sub','beam'}, dimensions={0} | all-to-all | bytes 1048576 | tf_op jit(solution)/shard_map/all_to_all | solution.py:122
  105.3 1.1 %pad_maximum_fusion = bf16[8,2,512,2,32]{2,4,3,1,0:T(8,128)(2,1)S(1)} fusion(bf16[8,2,512,1,32]{2,4,3,1,0:T(8,128)(2,1)S(1)} %bitcast.123, bf16[8,2,512,1,32]{2,4,3,1,0:T(8,128)(2,1)} %bitcast.18), kind=kLoop, calls=%fused_computation.8 | loop fusion | flops 524288 | bytes 2097152 | tf_op jit(solution)/shard_map/stack | solution.py:123
  106.5 1.3 %copy.75 = bf16[1,1,2,512,512]{4,3,2,1,0:T(8,128)(2,1)} copy(bf16[1,1,2,512,512]{3,4,2,1,0:T(8,128)(2,1)S(1)} %bitcast.118) | data formatting | bytes 2097152 | tf_op jit(solution)/shard_map/reshape | solution.py:126
  (165 shorter events, 31.0 us)
Async XLA Ops:
  0.0 10.3 %copy-start.32 = (f32[4]{0:T(128)S(1)}, f32[4]{0:T(128)}, u32[]{:S(2)}) copy-start(f32[4]{0:T(128)} %param.32) | copy-start | bytes 52
  0.0 10.5 %copy-start.30 = (f32[128]{0:T(128)S(1)}, f32[128]{0:T(128)}, u32[]{:S(2)}) copy-start(f32[128]{0:T(128)} %constant.57.clone) | copy-start | bytes 1540
  0.0 11.1 %copy-start.37 = (f32[8]{0:T(128)S(1)}, f32[8]{0:T(128)}, u32[]{:S(2)}) copy-start(f32[8]{0:T(128)} %constant.56.clone) | copy-start | bytes 100
  0.0 11.1 %copy-start.38 = (f32[8]{0:T(128)S(1)}, f32[8]{0:T(128)}, u32[]{:S(2)}) copy-start(f32[8]{0:T(128)} %constant.58.clone) | copy-start | bytes 100
  3.0 27.2 %all-to-all-start = ((bf16[8,2,32,512]{3,2,1,0:T(8,128)(2,1)}), bf16[8,2,32,512]{3,2,1,0:T(8,128)(2,1)S(1)}, u32[]{:S(2)}, u32[]{:S(2)}) async-start(bf16[8,2,32,512]{3,2,1,0:T(8,128)(2,1)} %copy.54), calls=%async_computation | async-start | bytes 1048576 | tf_op jit(solution)/shard_map/all_to_all | solution.py:107
  12.7 2.9 %copy-start.33 = (f32[8]{0:T(128)S(1)}, f32[8]{0:T(128)}, u32[]{:S(2)}) copy-start(f32[8]{0:T(128)} %constant.60.clone) | copy-start | bytes 100
  12.7 2.8 %copy-start.34 = (f32[8]{0:T(128)S(1)}, f32[8]{0:T(128)}, u32[]{:S(2)}) copy-start(f32[8]{0:T(128)} %constant.61.clone) | copy-start | bytes 100
  12.7 2.8 %copy-start.35 = (f32[8]{0:T(128)S(1)}, f32[8]{0:T(128)}, u32[]{:S(2)}) copy-start(f32[8]{0:T(128)} %constant.62.clone) | copy-start | bytes 100
  18.8 6.1 %copy-start.31 = (s32[2,4]{1,0:T(2,128)S(1)}, s32[2,4]{1,0:T(2,128)}, u32[]{:S(2)}) copy-start(s32[2,4]{1,0:T(2,128)} %param.33) | copy-start | bytes 100
  27.3 8.9 %copy-start.26 = (f32[2,32,8]{2,1,0:T(8,128)S(1)}, f32[2,32,8]{2,1,0:T(8,128)}, u32[]{:S(2)}) copy-start(f32[2,32,8]{2,1,0:T(8,128)} %get-tuple-element.113) | copy-start | bytes 6148
  27.3 8.9 %copy-start.27 = (f32[2,32,8]{2,1,0:T(8,128)S(1)}, f32[2,32,8]{2,1,0:T(8,128)}, u32[]{:S(2)}) copy-start(f32[2,32,8]{2,1,0:T(8,128)} %get-tuple-element.114) | copy-start | bytes 6148
  27.3 8.9 %copy-start.28 = (f32[2,32,8]{2,1,0:T(8,128)S(1)}, f32[2,32,8]{2,1,0:T(8,128)}, u32[]{:S(2)}) copy-start(f32[2,32,8]{2,1,0:T(8,128)} %get-tuple-element.133) | copy-start | bytes 6148
  27.3 8.9 %copy-start.29 = (f32[2,32,8]{2,1,0:T(8,128)S(1)}, f32[2,32,8]{2,1,0:T(8,128)}, u32[]{:S(2)}) copy-start(f32[2,32,8]{2,1,0:T(8,128)} %get-tuple-element.134) | copy-start | bytes 6148
  30.2 20.2 %all-to-all-start.2 = ((bf16[8,2,32,512]{3,2,1,0:T(8,128)(2,1)}), bf16[8,2,32,512]{3,2,1,0:T(8,128)(2,1)S(1)}, u32[]{:S(2)}, u32[]{:S(2)}) async-start(bf16[8,2,32,512]{3,2,1,0:T(8,128)(2,1)} %copy.64), calls=%async_computation.2 | async-start | bytes 1048576 | tf_op jit(solution)/shard_map/all_to_all | solution.py:107
  58.8 4.8 %copy-start.17 = (f32[2,1,32,1024]{3,2,1,0:T(8,128)S(1)}, f32[2,1,32,1024]{3,2,1,0:T(8,128)}, u32[]{:S(2)}) copy-start(f32[2,1,32,1024]{3,2,1,0:T(8,128)} %add.360) | copy-start | bytes 786436
  58.8 4.8 %copy-start.18 = (f32[2,1,32,1024]{3,2,1,0:T(8,128)S(1)}, f32[2,1,32,1024]{3,2,1,0:T(8,128)}, u32[]{:S(2)}) copy-start(f32[2,1,32,1024]{3,2,1,0:T(8,128)} %add.366) | copy-start | bytes 786436
  58.9 4.8 %copy-start.19 = (f32[2,1,32,1024]{3,2,1,0:T(8,128)S(1)}, f32[2,1,32,1024]{3,2,1,0:T(8,128)}, u32[]{:S(2)}) copy-start(f32[2,1,32,1024]{3,2,1,0:T(8,128)} %sub.298) | copy-start | bytes 786436
  58.9 4.8 %copy-start.20 = (f32[2,1,32,1024]{3,2,1,0:T(8,128)S(1)}, f32[2,1,32,1024]{3,2,1,0:T(8,128)}, u32[]{:S(2)}) copy-start(f32[2,1,32,1024]{3,2,1,0:T(8,128)} %sub.304) | copy-start | bytes 786436
  67.8 7.4 %copy-start.4 = (f32[2,2,1,32,1024]{4,3,1,0,2:T(8,128)S(1)}, f32[2,2,1,32,1024]{4,3,1,0,2:T(8,128)}, u32[]{:S(2)}) copy-start(f32[2,2,1,32,1024]{4,3,1,0,2:T(8,128)} %add.377) | copy-start | bytes 1572868
  67.8 7.4 %copy-start.5 = (f32[2,2,1,32,1024]{4,3,1,0,2:T(8,128)S(1)}, f32[2,2,1,32,1024]{4,3,1,0,2:T(8,128)}, u32[]{:S(2)}) copy-start(f32[2,2,1,32,1024]{4,3,1,0,2:T(8,128)} %sub.310) | copy-start | bytes 1572868
  67.8 19.6 %all-to-all-start.1 = ((bf16[8,2,512,32]{2,3,1,0:T(8,128)(2,1)}), bf16[8,2,512,32]{2,3,1,0:T(8,128)(2,1)}, u32[]{:S(2)}, u32[]{:S(2)}) async-start(bf16[8,2,512,32]{2,3,1,0:T(8,128)(2,1)} %copy.63), calls=%async_computation.1 | async-start | bytes 1048576 | tf_op jit(solution)/shard_map/all_to_all | solution.py:122
  78.4 4.7 %copy-start.10 = (f32[2,1,32,1024]{3,2,1,0:T(8,128)S(1)}, f32[2,1,32,1024]{3,2,1,0:T(8,128)}, u32[]{:S(2)}) copy-start(f32[2,1,32,1024]{3,2,1,0:T(8,128)} %add.389) | copy-start | bytes 786436
  78.5 4.7 %copy-start.11 = (f32[2,1,32,1024]{3,2,1,0:T(8,128)S(1)}, f32[2,1,32,1024]{3,2,1,0:T(8,128)}, u32[]{:S(2)}) copy-start(f32[2,1,32,1024]{3,2,1,0:T(8,128)} %sub.316) | copy-start | bytes 786436
  78.5 4.7 %copy-start.12 = (f32[2,1,32,1024]{3,2,1,0:T(8,128)S(1)}, f32[2,1,32,1024]{3,2,1,0:T(8,128)}, u32[]{:S(2)}) copy-start(f32[2,1,32,1024]{3,2,1,0:T(8,128)} %sub.322) | copy-start | bytes 786436
  (19 other events, 25.7 us)

commit v5 on v3

--- a/solution.py
+++ b/solution.py
@@ -56,6 +56,17 @@
     return product.reshape(children.shape[:-1] + (kernel.shape[1],))
 
 
+def swap_pieces(pieces, place, axes):
+    count = pieces.shape[0]
+    flips = jnp.bitwise_xor(place, jnp.arange(count, dtype=jnp.int32))
+    ordered = jnp.take(pieces, flips, axis=0)
+    moved = [ordered[0]]
+    for flip in range(1, count):
+        pairs = [(i, i ^ flip) for i in range(count)]
+        moved.append(lax.ppermute(ordered[flip], axes, pairs))
+    return jnp.take(jnp.stack(moved), flips, axis=0)
+
+
 def body(images, offsets, owners):
     group_count = lax.axis_size("grp")
     sub_count = group_count * GROUP_SUBS
@@ -106,7 +117,10 @@
     outgoing = picked.transpose(4, 3, 1, 5, 0, 2).reshape(
         sub_count * beam_count, 2, sector_width, own_rows
     )
-    received = lax.all_to_all(outgoing, ("grp", "sub4", "beam"), 0, 0, tiled=True)
+    if group_count == 1:
+        received = swap_pieces(outgoing, member_at, ("sub4", "beam"))
+    else:
+        received = lax.all_to_all(outgoing, ("grp", "sub4", "beam"), 0, 0, tiled=True)
     received = received.reshape(group_count, members, 2, sector_width, own_rows)
     received = received.transpose(0, 2, 3, 1, 4)
     return received.reshape(1, group_count, 2, sector_width, members * own_rows)

time: 87.6 us -> 86.1 us (0.983)
  blocking collectives: 29.3 us -> 0 us
  waiting for transfers between devices: 2.04 us -> 17.5 us
  starting transfers between devices: 7.28 us -> 17.4 us
  local copies, waits for them, and re-layouts: 29.8 us -> 31.1 us
    all_to_all x1 -> x0, blocking collectives: 29.3 us -> none  [body(): lax.all_to_all(outgoing, ('grp', 'sub4', 'beam'), 0, 0, tiled=True)]
    ppermute x0 -> x7, waiting for transfers between devices: none -> 15.4 us  [swap_pieces(): moved.append(lax.ppermute(ordered[flip], axes, pairs))]
    ppermute x0 -> x7, starting transfers between devices: none -> 10.1 us  [swap_pieces(): moved.append(lax.ppermute(ordered[flip], axes, pairs))]
    gather x1 -> x2, local copies, waits for them, and re-layouts: 0.75 us -> 2.1 us  [body(): picked = tiles[:, :, :, beam_ids, owners, :]]
    transpose x1, local copies, waits for them, and re-layouts: 1.35 us -> 0.09 us  [body(): received = received.transpose(0, 2, 3, 1, 4)]
    gather x0 -> x2, local copies, waits for them, and re-layouts: none -> 1.23 us  [the longest x1 0.61 us: swap_pieces(): ordered = jnp.take(pieces, flips, axis=0)]
    unnamed x40 -> x46, local copies, waits for them, and re-layouts: 4.57 us -> 4.63 us
  transfers between devices with their start and end apart: 1 -> 8, of which waited for: 1 -> 5; matrix products, arithmetic and copies ran while one was open for 27% -> 28% of each run, Pallas kernels for 0% -> 0%
where the time goes in v5:
time: 86.1 us; the launch traced here: 84.9 us
  local copies, waits for them, and re-layouts  31.1 us (36%)
  waiting for transfers between devices  17.5 us (20%)
  starting transfers between devices  17.4 us (20%)
  other arithmetic  11.2 us (13%)
  matrix products  7.06 us (8%)
    ppermute x7, waiting for transfers between devices, swap_pieces(): moved.append(lax.ppermute(ordered[flip], axes, pairs))  15.4 us
    ppermute x7, starting transfers between devices, swap_pieces(): moved.append(lax.ppermute(ordered[flip], axes, pairs))  10.1 us
    sub x6, local copies, waits for them, and re-layouts, spin(): cosine = c1 * c2 - s1 * s2  7.97 us
    add x6, local copies, waits for them, and re-layouts, spin(): sines = s1 * c2 + c1 * s2  7.55 us
    all_to_all x1, starting transfers between devices, body(): gathered = lax.all_to_all(pieces, ('sub4', 'beam'), 0, 0, tiled=True)  7.28 us
    dot_general x2, matrix products, odd_local(): jnp.dot(children.reshape(-1, children.shape[-1]), kernel, preferred_eleme...  7.06 us
    add x2, other arithmetic, spin(): sines = s1 * c2 + c1 * s2  4.8 us
    unnamed x46, local copies, waits for them, and re-layouts  4.63 us
  transfers between devices with their start and end apart: 8, of which 5 were waited for; matrix products, arithmetic and copies ran while one was open for 28% of the time, Pallas kernels for 0%

profile of v5, /device:TPU:0, one launch (start us, length us, event | category | flops | bytes accessed | tf_op | source)
XLA Modules:
  0.0 84.9 jit_solution(17258160965194100902)
XLA Ops:
  0.0 2.3 %copy.32 = bf16[8,2,64,512]{3,2,1,0:T(8,128)(2,1)} copy(bf16[8,2,64,512]{3,2,0,1:T(8,128)(2,1)} %bitcast.99) | data formatting | bytes 2097152 | tf_op jit(solution)/shard_map/transpose | solution.py:82
  2.4 7.3 %all-to-all-start = ((bf16[8,2,64,512]{3,2,1,0:T(8,128)(2,1)}), bf16[8,2,64,512]{3,2,1,0:T(8,128)(2,1)}, u32[]{:S(2)}, u32[]{:S(2)}) async-start(bf16[8,2,64,512]{3,2,1,0:T(8,128)(2,1)} %copy.32), calls=%async_computation | async-start | bytes 2097152 | tf_op jit(solution)/shard_map/all_to_all | solution.py:83
  11.3 2.4 %multiply_add_fusion.3 = (f32[4,64,8,128]{3,2,1,0:T(8,128)S(1)}, f32[4,64,8,128]{3,2,1,0:T(8,128)S(1)}, f32[4,64,8,128]{3,2,1,0:T(8,128)S(1)}, f32[4,64,8,128]{3,2,1,0:T(8,128)}) fusion(f32[4,64,128]{2,1,0:T(8,128)S(1)} %get-tuple-element.57, f32[4,64,8]{2,1,0:T(8,128)S(1)} %get-tuple-element.55, f32[4,64,128]{2,1,0:T(8,128)S(1)} %get-tuple-element.56, ...), kind=kLoop, calls=%fused_computation.21 | loop fusion | flops 3145728 | bytes 4489216 | tf_op jit(solution)/shard_map/add | solution.py:42
  13.9 2.3 %add.187 = f32[2,2,1,64,1024]{4,3,1,0,2:T(8,128)} reshape(f32[4,64,8,128]{3,2,1,0:T(8,128)} %get-tuple-element.45) | data formatting | bytes 2097152 | tf_op jit(solution)/shard_map/add | solution.py:42
  19.1 2.4 %multiply_add_fusion.11 = (f32[2,64,8,128]{3,2,1,0:T(8,128)}, f32[2,64,8,128]{3,2,1,0:T(8,128)}, f32[2,64,8,128]{3,2,1,0:T(8,128)}, f32[2,64,8,128]{3,2,1,0:T(8,...) fusion(f32[2,64,128]{2,1,0:T(8,128)S(1)} %get-tuple-element.69,, ...), kind=kLoop, calls=%fused_computation.40 | loop fusion | flops 3145728 | bytes 4358144 | tf_op jit(solution)/shard_map/add | solution.py:42
  21.5 1.9 %add.191 = f32[2,1,64,1024]{3,2,1,0:T(8,128)} reshape(f32[2,64,8,128]{3,2,1,0:T(8,128)} %get-tuple-element.38) | data formatting | bytes 1048576 | tf_op jit(solution)/shard_map/add | solution.py:42
  23.5 1.9 %add.197 = f32[2,1,64,1024]{3,2,1,0:T(8,128)} reshape(f32[2,64,8,128]{3,2,1,0:T(8,128)} %get-tuple-element.51) | data formatting | bytes 1048576 | tf_op jit(solution)/shard_map/add | solution.py:42
  25.4 1.9 %sub.151 = f32[2,1,64,1024]{3,2,1,0:T(8,128)} reshape(f32[2,64,8,128]{3,2,1,0:T(8,128)} %get-tuple-element.39) | data formatting | bytes 1048576 | tf_op jit(solution)/shard_map/sub | solution.py:41
  29.4 1.9 %sub.154 = f32[2,1,64,1024]{3,2,1,0:T(8,128)} reshape(f32[2,64,8,128]{3,2,1,0:T(8,128)} %get-tuple-element.48) | data formatting | bytes 1048576 | tf_op jit(solution)/shard_map/sub | solution.py:41
  31.3 1.9 %sub.160 = f32[2,1,64,1024]{3,2,1,0:T(8,128)} reshape(f32[2,64,8,128]{3,2,1,0:T(8,128)} %get-tuple-element.52) | data formatting | bytes 1048576 | tf_op jit(solution)/shard_map/sub | solution.py:41
  33.4 2.1 %all-to-all-done = bf16[8,2,64,512]{3,2,1,0:T(8,128)(2,1)} async-done(((bf16[8,2,64,512]{3,2,1,0:T(8,128)(2,1)}), bf16[8,2,64,512]{3,2,1,0:T(8,128)(2,1)}, u32[]{:S(2)}, u32[]{:S(2)}) %all-to-all-start) | async-done | bytes 1048608 | tf_op jit(solution)/shard_map/all_to_all | solution.py:83
  35.5 1.3 %copy.46 = bf16[4,2,2,8,8,512]{5,4,1,3,2,0:T(8,128)(2,1)S(1)} copy(bf16[4,2,2,8,8,512]{5,4,3,2,1,0:T(8,128)(2,1)} %bitcast.40) | data formatting | bytes 2097152 | tf_op jit(solution)/shard_map/reshape | solution.py:89
  37.1 1.3 %copy-done.19 = bf16[1024,1024,1,1]{1,0,3,2:T(8,128)(2,1)S(1)} copy-done((bf16[1024,1024,1,1]{1,0,3,2:T(8,128)(2,1)S(1)}, bf16[1024,1024,1,1]{1,0,3,2:T(8,128)(2,1)}, u32[]{:S(2)}) %copy-start.19) | copy-done | bytes 2097176
  38.4 1.3 %convolution_bitcast_fusion = f32[4,2,64,1024]{3,2,1,0:T(8,128)S(1)} fusion(bf16[1024,1024,1,1]{1,0,3,2:T(8,128)(2,1)S(1)} %copy-done.19, bf16[4,2,64,1024]{3,2,1,0:T(8,128)(2,1)S(1)} %bitcast.91), kind=kOutput, calls=%fused_computation.5 | convolution fusion | flops 1073741824 | bytes 5242880 | tf_op jit(solution)/shard_map/dot_general | solution.py:53
  46.1 5.8 %fusion = f32[2,2,64,2048]{3,2,1,0:T(8,128)S(1)} fusion(bf16[2048,2048,1,1]{1,0,3,2:T(8,128)(2,1)} %constant.87, bf16[2,2,64,1024]{3,2,0,1:T(8,128)(2,1)S(1)} %maximum_reduce_fusion, bf16[2,2,64,1024]{3,2,0,1:T(8,128)(2,1)S(1)} %copy-done.9), kind=kOutput, calls=%fused_computation.24 | convolution fusion | flops 2149580800 | bytes 11534336 | tf_op jit(solution)/shard_map/dot_general | solution.py:53
  53.9 1.4 %copy.40 = bf16[2,4,4,2,64,128]{4,2,5,3,0,1:T(4,128)(2,1)S(1)} copy(bf16[2,4,4,2,64,128]{5,4,3,2,1,0:T(8,128)(2,1)S(1)} %bitcast.93) | data formatting | bytes 2097152 | tf_op jit(solution)/shard_map/gather | solution.py:116
  57.0 1.5 %collective-permute-start = (bf16[2,512,64]{1,2,0:T(8,128)(2,1)S(1)}, bf16[2,512,64]{1,2,0:T(8,128)(2,1)S(1)}, u32[]{:S(2)}, u32[]{:S(2)}) collective-permute-start(bf16[2,512,64]{1,2,0:T(8,128)(2,1)S(1)} %get-tuple-element.30), channel_id=1, source_target_pairs={{0,2},{2,0},{4,6},{6,4},{8,10},{10,8},{12,14},{14,12},{1,3},{3,1},... | collective-permute-start | bytes 393224 | tf_op jit(solution)/shard_map/ppermute | solution.py:66
  58.5 2.1 %collective-permute-start.2 = (bf16[2,512,64]{1,2,0:T(8,128)(2,1)S(1)}, bf16[2,512,64]{1,2,0:T(8,128)(2,1)S(1)}, u32[]{:S(2)}, u32[]{:S(2)}) collective-permute-start(bf16[2,512,64]{1,2,0:T(8,128)(2,1)S(1)} %get-tuple-element.28), channel_id=1, source_target_pairs={{0,6},{2,4},{4,2},{6,0},{8,14},{10,12},{12,10},{14,8},{1,7},{3,5},... | collective-permute-start | bytes 393224 | tf_op jit(solution)/shard_map/ppermute | solution.py:66
  61.4 3.0 %collective-permute-start.4 = (bf16[2,512,64]{1,2,0:T(8,128)(2,1)S(1)}, bf16[2,512,64]{1,2,0:T(8,128)(2,1)S(1)}, u32[]{:S(2)}, u32[]{:S(2)}) collective-permute-start(bf16[2,512,64]{1,2,0:T(8,128)(2,1)S(1)} %get-tuple-element.26), channel_id=1, source_target_pairs={{0,10},{2,8},{4,14},{6,12},{8,2},{10,0},{12,6},{14,4},{1,11},{3,9}... | collective-permute-start | bytes 393224 | tf_op jit(solution)/shard_map/ppermute | solution.py:66
  64.3 1.7 %collective-permute-start.5 = (bf16[2,512,64]{1,2,0:T(8,128)(2,1)S(1)}, bf16[2,512,64]{1,2,0:T(8,128)(2,1)S(1)}, u32[]{:S(2)}, u32[]{:S(2)}) collective-permute-start(bf16[2,512,64]{1,2,0:T(8,128)(2,1)S(1)} %get-tuple-element.25), channel_id=1, source_target_pairs={{0,12},{2,14},{4,8},{6,10},{8,4},{10,6},{12,0},{14,2},{1,13},{3,15... | collective-permute-start | bytes 393224 | tf_op jit(solution)/shard_map/ppermute | solution.py:66
  66.1 1.1 %collective-permute-done.1 = bf16[2,512,64]{1,2,0:T(8,128)(2,1)S(1)} collective-permute-done((bf16[2,512,64]{1,2,0:T(8,128)(2,1)S(1)}, bf16[2,512,64]{1,2,0:T(8,128)(2,1)S(1)}, u32[]{:S(2)}, u32[]{:S(2)}) %collective-permute-start.1) | collective-permute-done | bytes 131104 | tf_op jit(solution)/shard_map/ppermute | solution.py:66
  68.6 10.1 %collective-permute-done.3 = bf16[2,512,64]{1,2,0:T(8,128)(2,1)S(1)} collective-permute-done((bf16[2,512,64]{1,2,0:T(8,128)(2,1)S(1)}, bf16[2,512,64]{1,2,0:T(8,128)(2,1)S(1)}, u32[]{:S(2)}, u32[]{:S(2)}) %collective-permute-start.3) | collective-permute-done | bytes 131104 | tf_op jit(solution)/shard_map/ppermute | solution.py:66
  78.7 3.8 %collective-permute-done.4 = bf16[2,512,64]{1,2,0:T(8,128)(2,1)S(1)} collective-permute-done((bf16[2,512,64]{1,2,0:T(8,128)(2,1)S(1)}, bf16[2,512,64]{1,2,0:T(8,128)(2,1)S(1)}, u32[]{:S(2)}, u32[]{:S(2)}) %collective-permute-start.4) | collective-permute-done | bytes 131104 | tf_op jit(solution)/shard_map/ppermute | solution.py:66
  83.5 1.3 %copy.43 = bf16[1,1,2,512,512]{4,3,2,1,0:T(8,128)(2,1)} copy(bf16[1,1,2,512,512]{3,4,2,1,0:T(8,128)(2,1)S(1)} %bitcast.94) | data formatting | bytes 2097152 | tf_op jit(solution)/shard_map/reshape | solution.py:126
  (102 shorter events, 20.1 us)
Async XLA Ops:
  0.0 9.6 %copy-start.12 = (f32[4]{0:T(128)S(1)}, f32[4]{0:T(128)}, u32[]{:S(2)}) copy-start(f32[4]{0:T(128)} %param.20) | copy-start | bytes 52
  0.0 9.7 %copy-start.10 = (f32[128]{0:T(128)S(1)}, f32[128]{0:T(128)}, u32[]{:S(2)}) copy-start(f32[128]{0:T(128)} %constant.65.clone) | copy-start | bytes 1540
  0.0 10.3 %copy-start.17 = (f32[8]{0:T(128)S(1)}, f32[8]{0:T(128)}, u32[]{:S(2)}) copy-start(f32[8]{0:T(128)} %constant.64.clone) | copy-start | bytes 100
  0.0 10.3 %copy-start.18 = (f32[8]{0:T(128)S(1)}, f32[8]{0:T(128)}, u32[]{:S(2)}) copy-start(f32[8]{0:T(128)} %constant.66.clone) | copy-start | bytes 100
  2.4 33.2 %all-to-all-start = ((bf16[8,2,64,512]{3,2,1,0:T(8,128)(2,1)}), bf16[8,2,64,512]{3,2,1,0:T(8,128)(2,1)}, u32[]{:S(2)}, u32[]{:S(2)}) async-start(bf16[8,2,64,512]{3,2,1,0:T(8,128)(2,1)} %copy.32), calls=%async_computation | async-start | bytes 2097152 | tf_op jit(solution)/shard_map/all_to_all | solution.py:83
  28.2 5.1 %copy-start.11 = (s32[2,4]{1,0:T(2,128)S(1)}, s32[2,4]{1,0:T(2,128)}, u32[]{:S(2)}) copy-start(s32[2,4]{1,0:T(2,128)} %param.21) | copy-start | bytes 100
  36.9 1.6 %copy-start.19 = (bf16[1024,1024,1,1]{1,0,3,2:T(8,128)(2,1)S(1)}, bf16[1024,1024,1,1]{1,0,3,2:T(8,128)(2,1)}, u32[]{:S(2)}) copy-start(bf16[1024,1024,1,1]{1,0,3,2:T(8,128)(2,1)} %constant.86) | copy-start | bytes 6291460
  39.7 1.2 %copy-start = (f32[2,2,1,64,1024]{4,3,1,0,2:T(8,128)S(1)}, f32[2,2,1,64,1024]{4,3,1,0,2:T(8,128)}, u32[]{:S(2)}) copy-start(f32[2,2,1,64,1024]{4,3,1,0,2:T(8,128)} %add.187) | copy-start | bytes 3145732
  39.7 1.5 %copy-start.1 = (f32[2,2,1,64,1024]{4,3,1,0,2:T(8,128)S(1)}, f32[2,2,1,64,1024]{4,3,1,0,2:T(8,128)}, u32[]{:S(2)}) copy-start(f32[2,2,1,64,1024]{4,3,1,0,2:T(8,128)} %sub.148) | copy-start | bytes 3145732
  42.1 0.8 copy-start.8
  42.9 1.0 %copy-start.4 = (f32[2,1,64,1024]{3,2,1,0:T(8,128)S(1)}, f32[2,1,64,1024]{3,2,1,0:T(8,128)}, u32[]{:S(2)}) copy-start(f32[2,1,64,1024]{3,2,1,0:T(8,128)} %add.191) | copy-start | bytes 1572868
  42.9 1.2 %copy-start.5 = (f32[2,1,64,1024]{3,2,1,0:T(8,128)S(1)}, f32[2,1,64,1024]{3,2,1,0:T(8,128)}, u32[]{:S(2)}) copy-start(f32[2,1,64,1024]{3,2,1,0:T(8,128)} %add.197) | copy-start | bytes 1572868
  42.9 1.4 %copy-start.6 = (f32[2,1,64,1024]{3,2,1,0:T(8,128)S(1)}, f32[2,1,64,1024]{3,2,1,0:T(8,128)}, u32[]{:S(2)}) copy-start(f32[2,1,64,1024]{3,2,1,0:T(8,128)} %sub.151) | copy-start | bytes 1572868
  42.9 1.5 %copy-start.7 = (f32[2,1,64,1024]{3,2,1,0:T(8,128)S(1)}, f32[2,1,64,1024]{3,2,1,0:T(8,128)}, u32[]{:S(2)}) copy-start(f32[2,1,64,1024]{3,2,1,0:T(8,128)} %sub.157) | copy-start | bytes 1572868
  45.1 1.0 %copy-start.9 = (bf16[2,2,64,1024]{3,2,0,1:T(8,128)(2,1)S(1)}, bf16[2,2,64,1024]{3,2,0,1:T(8,128)(2,1)}, u32[]{:S(2)}) copy-start(bf16[2,2,64,1024]{3,2,0,1:T(8,128)(2,1)} %copy-done.8) | copy-start | bytes 1572868
  46.1 5.8 %copy-start.2 = (f32[2,1,64,1024]{3,2,1,0:T(8,128)S(1)}, f32[2,1,64,1024]{3,2,1,0:T(8,128)}, u32[]{:S(2)}) copy-start(f32[2,1,64,1024]{3,2,1,0:T(8,128)} %sub.154) | copy-start | bytes 1572868
  46.1 5.8 %copy-start.3 = (f32[2,1,64,1024]{3,2,1,0:T(8,128)S(1)}, f32[2,1,64,1024]{3,2,1,0:T(8,128)}, u32[]{:S(2)}) copy-start(f32[2,1,64,1024]{3,2,1,0:T(8,128)} %sub.160) | copy-start | bytes 1572868
  57.0 7.3 %collective-permute-start = (bf16[2,512,64]{1,2,0:T(8,128)(2,1)S(1)}, bf16[2,512,64]{1,2,0:T(8,128)(2,1)S(1)}, u32[]{:S(2)}, u32[]{:S(2)}) collective-permute-start(bf16[2,512,64]{1,2,0:T(8,128)(2,1)S(1)} %get-tuple-element.30), channel_id=1, source_target_pairs={{0,2},{2,0},{4,6},{6,4},{8,10},{10,8},{12,14},{14,12},{1,3},{3,1},... | collective-permute-start | bytes 393224 | tf_op jit(solution)/shard_map/ppermute | solution.py:66
  58.5 8.8 %collective-permute-start.1 = (bf16[2,512,64]{1,2,0:T(8,128)(2,1)S(1)}, bf16[2,512,64]{1,2,0:T(8,128)(2,1)S(1)}, u32[]{:S(2)}, u32[]{:S(2)}) collective-permute-start(bf16[2,512,64]{1,2,0:T(8,128)(2,1)S(1)} %get-tuple-element.29), channel_id=1, source_target_pairs={{0,4},{2,6},{4,0},{6,2},{8,12},{10,14},{12,8},{14,10},{1,5},{3,7},... | collective-permute-start | bytes 393224 | tf_op jit(solution)/shard_map/ppermute | solution.py:66
  58.5 10.1 %collective-permute-start.2 = (bf16[2,512,64]{1,2,0:T(8,128)(2,1)S(1)}, bf16[2,512,64]{1,2,0:T(8,128)(2,1)S(1)}, u32[]{:S(2)}, u32[]{:S(2)}) collective-permute-start(bf16[2,512,64]{1,2,0:T(8,128)(2,1)S(1)} %get-tuple-element.28), channel_id=1, source_target_pairs={{0,6},{2,4},{4,2},{6,0},{8,14},{10,12},{12,10},{14,8},{1,7},{3,5},... | collective-permute-start | bytes 393224 | tf_op jit(solution)/shard_map/ppermute | solution.py:66
  60.6 18.2 %collective-permute-start.3 = (bf16[2,512,64]{1,2,0:T(8,128)(2,1)S(1)}, bf16[2,512,64]{1,2,0:T(8,128)(2,1)S(1)}, u32[]{:S(2)}, u32[]{:S(2)}) collective-permute-start(bf16[2,512,64]{1,2,0:T(8,128)(2,1)S(1)} %get-tuple-element.27), channel_id=1, source_target_pairs={{0,8},{2,10},{4,12},{6,14},{8,0},{10,2},{12,4},{14,6},{1,9},{3,11}... | collective-permute-start | bytes 393224 | tf_op jit(solution)/shard_map/ppermute | solution.py:66
  61.4 21.2 %collective-permute-start.4 = (bf16[2,512,64]{1,2,0:T(8,128)(2,1)S(1)}, bf16[2,512,64]{1,2,0:T(8,128)(2,1)S(1)}, u32[]{:S(2)}, u32[]{:S(2)}) collective-permute-start(bf16[2,512,64]{1,2,0:T(8,128)(2,1)S(1)} %get-tuple-element.26), channel_id=1, source_target_pairs={{0,10},{2,8},{4,14},{6,12},{8,2},{10,0},{12,6},{14,4},{1,11},{3,9}... | collective-permute-start | bytes 393224 | tf_op jit(solution)/shard_map/ppermute | solution.py:66
  64.3 18.3 %collective-permute-start.5 = (bf16[2,512,64]{1,2,0:T(8,128)(2,1)S(1)}, bf16[2,512,64]{1,2,0:T(8,128)(2,1)S(1)}, u32[]{:S(2)}, u32[]{:S(2)}) collective-permute-start(bf16[2,512,64]{1,2,0:T(8,128)(2,1)S(1)} %get-tuple-element.25), channel_id=1, source_target_pairs={{0,12},{2,14},{4,8},{6,10},{8,4},{10,6},{12,0},{14,2},{1,13},{3,15... | collective-permute-start | bytes 393224 | tf_op jit(solution)/shard_map/ppermute | solution.py:66
  67.2 15.4 %collective-permute-start.6 = (bf16[2,512,64]{1,2,0:T(8,128)(2,1)S(1)}, bf16[2,512,64]{1,2,0:T(8,128)(2,1)S(1)}, u32[]{:S(2)}, u32[]{:S(2)}) collective-permute-start(bf16[2,512,64]{1,2,0:T(8,128)(2,1)S(1)} %get-tuple-element.24), channel_id=1, source_target_pairs={{0,14},{2,12},{4,10},{6,8},{8,6},{10,4},{12,2},{14,0},{1,15},{3,13... | collective-permute-start | bytes 393224 | tf_op jit(solution)/shard_map/ppermute | solution.py:66
  (4 other events, 3.0 us)

commit v6 on v3

--- a/solution.py
+++ b/solution.py
@@ -38,13 +38,13 @@
     s1 = jnp.sin(rough)[..., None]
     c2 = jnp.cos(small)[..., None, :]
     s2 = jnp.sin(small)[..., None, :]
-    cosine = c1 * c2 - s1 * s2
-    sines = s1 * c2 + c1 * s2
     grid = parts.shape[:-3] + (parts.shape[-2], count // lanes, lanes)
     real_part = parts[..., 0, :, :].reshape(grid)
     imag_part = parts[..., 1, :, :].reshape(grid)
+    real_fine = real_part * c2 - imag_part * s2
+    imag_fine = real_part * s2 + imag_part * c2
     turned = jnp.stack(
-        [real_part * cosine - imag_part * sines, real_part * sines + imag_part * cosine], -4
+        [real_fine * c1 - imag_fine * s1, real_fine * s1 + imag_fine * c1], -4
     )
     return turned.reshape(parts.shape)
 
@@ -54,6 +54,20 @@
         children.reshape(-1, children.shape[-1]), kernel, preferred_element_type=jnp.float32
     )
     return product.reshape(children.shape[:-1] + (kernel.shape[1],))
+
+
+def swap_sectors(tiles, owners, place, beam_count):
+    count = tiles.shape[3] * tiles.shape[4]
+    flips = jnp.bitwise_xor(place, jnp.arange(count, dtype=jnp.int32))
+    shard_ids = flips % beam_count
+    sector_ids = owners[shard_ids, flips // beam_count]
+    ordered = tiles[:, :, :, shard_ids, sector_ids, :].transpose(3, 0, 1, 2, 4)
+    moved = [ordered[0]]
+    for flip in range(1, count):
+        pairs = [(i, i ^ flip) for i in range(count)]
+        moved.append(lax.ppermute(ordered[flip], ("sub4", "beam"), pairs))
+    senders = jnp.take(jnp.stack(moved), flips, axis=0)
+    return senders.transpose(2, 4, 1, 0, 3)
 
 
 def body(images, offsets, owners):
@@ -101,6 +115,9 @@
 
     sector_width = 4 * B // (beam_count * sub_count)
     tiles = merged.reshape(4, 2, own_rows, beam_count, sub_count, sector_width // 4)
+    if group_count == 1:
+        received = swap_sectors(tiles, owners, member_at, beam_count)
+        return received.reshape(1, 1, 2, sector_width, members * own_rows)
     beam_ids = jnp.arange(beam_count, dtype=jnp.int32)[:, None]
     picked = tiles[:, :, :, beam_ids, owners, :]
     outgoing = picked.transpose(4, 3, 1, 5, 0, 2).reshape(

time: 87.6 us -> 122 us (1.39); the launches traced: 86.9 us -> 120 us
  local copies, waits for them, and re-layouts: 29.8 us -> 66.8 us
  blocking collectives: 29.3 us -> 0 us
  starting transfers between devices: 7.28 us -> 19.6 us
  waiting for transfers between devices: 2.04 us -> 14 us
  other arithmetic: 11 us -> 14.6 us
  matrix products: 7.06 us -> 3.84 us
    mul x0 -> x32, local copies, waits for them, and re-layouts: none -> 44.3 us  [the longest x12 16.9 us: spin(): imag_fine * s1]
    all_to_all x1 -> x0, blocking collectives: 29.3 us -> none  [body(): lax.all_to_all(outgoing, ('grp', 'sub4', 'beam'), 0, 0, tiled=True)]
    ppermute x0 -> x7, waiting for transfers between devices: none -> 14 us  [swap_sectors(): moved.append(lax.ppermute(ordered[flip], ('sub4', 'beam'), pairs))]
    ppermute x0 -> x7, starting transfers between devices: none -> 12.3 us  [swap_sectors(): moved.append(lax.ppermute(ordered[flip], ('sub4', 'beam'), pairs))]
    sub x6 -> x0, local copies, waits for them, and re-layouts: 7.99 us -> none  [spin(): cosine = c1 * c2 - s1 * s2]
    add x6 -> x0, local copies, waits for them, and re-layouts: 7.59 us -> none  [spin(): sines = s1 * c2 + c1 * s2]
    dot_general x2, matrix products: 7.06 us -> 3.84 us  [odd_local(): jnp.dot(children.reshape(-1, children.shape[-1]), kernel, preferred_eleme...]
    another operation x8, local copies, waits for them, and re-layouts: 0.85 us -> 3.96 us  [body(): jnp.stack([spin(first_f[..., :B], scale_two, 4, 0, 4 * B).sum(0), spin(od...]
  transfers between devices with their start and end apart: 1 -> 8, of which waited for: 1 -> 3; matrix products, arithmetic and copies ran while one was open for 27% -> 42% of each run, Pallas kernels for 0% -> 0%
where the time goes in v6:
time: 122 us; the launch traced here: 120 us
  local copies, waits for them, and re-layouts  66.8 us (55%)
  starting transfers between devices  19.6 us (16%)
  other arithmetic  14.6 us (12%)
  waiting for transfers between devices  14 us (11%)
  matrix products  3.84 us (3%)
    mul x12, local copies, waits for them, and re-layouts, spin(): imag_fine * s1  16.9 us
    mul x12, local copies, waits for them, and re-layouts, spin(): real_fine * c1 - imag_fine * s1  15 us
    ppermute x7, waiting for transfers between devices, swap_sectors(): moved.append(lax.ppermute(ordered[flip], ('sub4', 'beam'), pairs))  14 us
    mul x8, local copies, waits for them, and re-layouts, spin(): real_fine = real_part * c2 - imag_part * s2  12.4 us
    ppermute x7, starting transfers between devices, swap_sectors(): moved.append(lax.ppermute(ordered[flip], ('sub4', 'beam'), pairs))  12.3 us
    all_to_all x1, starting transfers between devices, body(): gathered = lax.all_to_all(pieces, ('sub4', 'beam'), 0, 0, tiled=True)  7.28 us
    unnamed x68, local copies, waits for them, and re-layouts  5.9 us
    sub x2, other arithmetic, spin(): real_fine * c1 - imag_fine * s1  5.02 us
  transfers between devices with their start and end apart: 8, of which 3 were waited for; matrix products, arithmetic and copies ran while one was open for 42% of the time, Pallas kernels for 0%

profile of v6, /device:TPU:0, one launch (start us, length us, event | category | flops | bytes accessed | tf_op | source)
XLA Modules:
  0.0 119.5 jit_solution(16324790585766025118)
XLA Ops:
  0.0 2.3 %copy.34 = bf16[8,2,64,512]{3,2,1,0:T(8,128)(2,1)} copy(bf16[8,2,64,512]{3,2,0,1:T(8,128)(2,1)} %bitcast.103) | data formatting | bytes 2097152 | tf_op jit(solution)/shard_map/transpose | solution.py:85
  2.4 7.3 %all-to-all-start = ((bf16[8,2,64,512]{3,2,1,0:T(8,128)(2,1)}), bf16[8,2,64,512]{3,2,1,0:T(8,128)(2,1)}, u32[]{:S(2)}, u32[]{:S(2)}) async-start(bf16[8,2,64,512]{3,2,1,0:T(8,128)(2,1)} %copy.34), calls=%async_computation | async-start | bytes 2097152 | tf_op jit(solution)/shard_map/all_to_all | solution.py:86
  17.0 2.3 %mul.963 = f32[2,2,1,64,1024]{4,3,1,0,2:T(8,128)} reshape(f32[4,64,8,128]{3,2,1,0:T(8,128)} %mul.962) | data formatting | bytes 2097152 | tf_op jit(solution)/shard_map/mul | solution.py:47
  21.0 2.4 %mul.929 = f32[2,2,1,64,1024]{4,3,1,0,2:T(8,128)} reshape(f32[4,64,8,128]{3,2,1,0:T(8,128)} %mul.928) | data formatting | bytes 2097152 | tf_op jit(solution)/shard_map/mul | solution.py:44
  24.5 2.4 %mul.932 = f32[2,2,1,64,1024]{4,3,1,0,2:T(8,128)} reshape(f32[4,64,8,128]{3,2,1,0:T(8,128)} %mul.931) | data formatting | bytes 2097152 | tf_op jit(solution)/shard_map/mul | solution.py:44
  26.9 2.3 %multiply_cosine_fusion.6 = (f32[2,64,8]{2,1,0:T(8,128)S(1)}, f32[2,64,8]{2,1,0:T(8,128)S(1)}, f32[2,64,8]{2,1,0:T(8,128)}, f32[2,64,8]{2,1,0:T(8,128)S(1)}, f32...) fusion(f32[8]{0:T(128)} %constant.94.clone, ...), kind=kLoop, calls=%fused_computation.69 | loop fusion | flops 4096 | bytes 33408 | tf_op jit(solution)/shard_map/cos | solution.py:37
  30.2 1.9 %mul.1004 = f32[2,1,64,1024]{3,2,1,0:T(8,128)} reshape(f32[2,64,8,128]{3,2,1,0:T(8,128)} %mul.1003) | data formatting | bytes 1048576 | tf_op jit(solution)/shard_map/mul | solution.py:47
  34.0 1.9 %mul.1009 = f32[2,1,64,1024]{3,2,1,0:T(8,128)} reshape(f32[2,64,8,128]{3,2,1,0:T(8,128)} %mul.1008) | data formatting | bytes 1048576 | tf_op jit(solution)/shard_map/mul | solution.py:47
  37.0 1.9 %mul.1024 = f32[2,1,64,1024]{3,2,1,0:T(8,128)} reshape(f32[2,64,8,128]{3,2,1,0:T(8,128)} %mul.1023) | data formatting | bytes 1048576 | tf_op jit(solution)/shard_map/mul | solution.py:47
  39.9 1.9 %mul.1029 = f32[2,1,64,1024]{3,2,1,0:T(8,128)} reshape(f32[2,64,8,128]{3,2,1,0:T(8,128)} %mul.1028) | data formatting | bytes 1048576 | tf_op jit(solution)/shard_map/mul | solution.py:47
  42.8 1.9 %mul.1044 = f32[2,1,64,1024]{3,2,1,0:T(8,128)} reshape(f32[2,64,8,128]{3,2,1,0:T(8,128)} %mul.1043) | data formatting | bytes 1048576 | tf_op jit(solution)/shard_map/mul | solution.py:47
  45.7 2.0 %mul.1049 = f32[2,1,64,1024]{3,2,1,0:T(8,128)} reshape(f32[2,64,8,128]{3,2,1,0:T(8,128)} %mul.1048) | data formatting | bytes 1048576 | tf_op jit(solution)/shard_map/mul | solution.py:47
  48.7 1.9 %mul.984 = f32[2,1,64,1024]{3,2,1,0:T(8,128)} reshape(f32[2,64,8,128]{3,2,1,0:T(8,128)} %mul.983) | data formatting | bytes 1048576 | tf_op jit(solution)/shard_map/mul | solution.py:47
  51.7 2.0 %mul.989 = f32[2,1,64,1024]{3,2,1,0:T(8,128)} reshape(f32[2,64,8,128]{3,2,1,0:T(8,128)} %mul.988) | data formatting | bytes 1048576 | tf_op jit(solution)/shard_map/mul | solution.py:47
  54.8 2.0 %mul.975 = f32[2,1,64,1024]{3,2,1,0:T(8,128)} reshape(f32[2,64,8,128]{3,2,1,0:T(8,128)} %mul.974) | data formatting | bytes 1048576 | tf_op jit(solution)/shard_map/mul | solution.py:44
  57.6 1.9 %mul.978 = f32[2,1,64,1024]{3,2,1,0:T(8,128)} reshape(f32[2,64,8,128]{3,2,1,0:T(8,128)} %mul.977) | data formatting | bytes 1048576 | tf_op jit(solution)/shard_map/mul | solution.py:44
  71.6 2.6 %fusion = f32[2,2,64,2048]{3,2,1,0:T(8,128)S(1)} fusion(bf16[2048,2048,1,1]{1,0,3,2:T(8,128)(2,1)S(1)} %bitcast.105, bf16[2,2,64,1024]{3,2,0,1:T(8,128)(2,1)S(1)} %get-tuple-element.74, bf16[2,2,64,1024]{3,2,0,1:T(8,128)(2,1)S(1)} %get-tuple-element.75), kind=kOutput, calls=%fused_computation.23 | convolution fusion | flops 2149580800 | bytes 11534336 | tf_op jit(solution)/shard_map/dot_general | solution.py:53
  74.3 3.4 %multiply_subtract_fusion.10 = (f32[2,1,64,1024]{3,2,1,0:T(8,128)S(1)}, f32[2,1,64,1024]{3,2,1,0:T(8,128)S(1)}, f32[2,1,64,1024]{3,2,1,0:T(8,128)S(1)}, f32[2,1,...) fusion(f32[2,1,64,1024]{3,2,1,0:T(8,128)S(1)} %copy-done.10, ...), kind=kLoop, calls=%fused_computation.38 | loop fusion | flops 4718592 | bytes 15728640 | tf_op jit(solution)/shard_map/sub | solution.py:47
  87.0 2.1 %collective-permute-start = (bf16[4,2,64,128]{3,2,1,0:T(8,128)(2,1)S(1)}, bf16[4,2,64,128]{3,2,1,0:T(8,128)(2,1)S(1)}, u32[]{:S(2)}, u32[]{:S(2)}) collective-permute-start(bf16[4,2,64,128]{3,2,1,0:T(8,128)(2,1)S(1)} %get-tuple-element.40), channel_id=1, source_target_pairs={{0,2},{2,0},{4,6},{6,4},{8,10},{10,8},{12,14},{14,12},{1,3},{3,1},... | collective-permute-start | bytes 393224 | tf_op jit(solution)/shard_map/ppermute | solution.py:68
  90.7 2.8 %collective-permute-start.3 = (bf16[4,2,64,128]{3,2,1,0:T(8,128)(2,1)S(1)}, bf16[4,2,64,128]{3,2,1,0:T(8,128)(2,1)S(1)}, u32[]{:S(2)}, u32[]{:S(2)}) collective-permute-start(bf16[4,2,64,128]{3,2,1,0:T(8,128)(2,1)S(1)} %get-tuple-element.37), channel_id=1, source_target_pairs={{0,8},{2,10},{4,12},{6,14},{8,0},{10,2},{12,4},{14,6},{1,9},{3,11}... | collective-permute-start | bytes 393224 | tf_op jit(solution)/shard_map/ppermute | solution.py:68
  95.0 3.3 %collective-permute-start.5 = (bf16[4,2,64,128]{3,2,1,0:T(8,128)(2,1)S(1)}, bf16[4,2,64,128]{3,2,1,0:T(8,128)(2,1)S(1)}, u32[]{:S(2)}, u32[]{:S(2)}) collective-permute-start(bf16[4,2,64,128]{3,2,1,0:T(8,128)(2,1)S(1)} %get-tuple-element.35), channel_id=1, source_target_pairs={{0,12},{2,14},{4,8},{6,10},{8,4},{10,6},{12,0},{14,2},{1,13},{3,15... | collective-permute-start | bytes 393224 | tf_op jit(solution)/shard_map/ppermute | solution.py:68
  100.4 13.1 %collective-permute-done.4 = bf16[4,2,64,128]{3,2,1,0:T(8,128)(2,1)S(1)} collective-permute-done((bf16[4,2,64,128]{3,2,1,0:T(8,128)(2,1)S(1)}, bf16[4,2,64,128]{3,2,1,0:T(8,128)(2,1)S(1)}, u32[]{:S(2)}, u32[]{:S(2)}) %collective-permute-start.4) | collective-permute-done | bytes 131104 | tf_op jit(solution)/shard_map/ppermute | solution.py:68
  114.5 3.0 %copy.42 = bf16[2,128,4,8,64]{4,3,2,1,0:T(8,128)(2,1)S(1)} copy(bf16[2,128,4,8,64]{1,4,0,2,3:T(8,128)(2,1)S(1)} %select_bitcast_fusion) | data formatting | bytes 2097152 | tf_op jit(solution)/shard_map/jit(_take)/select_n | solution.py:69
  117.5 2.1 %reshape.790 = bf16[1,1,2,512,512]{4,3,2,1,0:T(8,128)(2,1)} reshape(bf16[2,128,4,8,64]{4,3,2,1,0:T(8,128)(2,1)S(1)} %copy.42) | data formatting | bytes 2097152 | tf_op jit(solution)/shard_map/reshape | solution.py:120
  (145 shorter events, 48.2 us)
Async XLA Ops:
  0.0 59.5 %copy-start = (s32[2,4]{1,0:T(2,128)S(1)}, s32[2,4]{1,0:T(2,128)}, u32[]{:S(2)}) copy-start(s32[2,4]{1,0:T(2,128)} %param.19) | copy-start | bytes 100
  0.0 9.6 %copy-start.23 = (f32[4]{0:T(128)S(1)}, f32[4]{0:T(128)}, u32[]{:S(2)}) copy-start(f32[4]{0:T(128)} %param.18) | copy-start | bytes 52
  0.0 11.0 %copy-start.24 = (f32[8]{0:T(128)S(1)}, f32[8]{0:T(128)}, u32[]{:S(2)}) copy-start(f32[8]{0:T(128)} %constant.90.clone) | copy-start | bytes 100
  0.0 11.0 %copy-start.25 = (f32[8]{0:T(128)S(1)}, f32[8]{0:T(128)}, u32[]{:S(2)}) copy-start(f32[8]{0:T(128)} %constant.92.clone) | copy-start | bytes 100
  2.4 57.9 %all-to-all-start = ((bf16[8,2,64,512]{3,2,1,0:T(8,128)(2,1)}), bf16[8,2,64,512]{3,2,1,0:T(8,128)(2,1)}, u32[]{:S(2)}, u32[]{:S(2)}) async-start(bf16[8,2,64,512]{3,2,1,0:T(8,128)(2,1)} %copy.34), calls=%async_computation | async-start | bytes 2097152 | tf_op jit(solution)/shard_map/all_to_all | solution.py:86
  15.7 3.7 %copy-start.22 = (f32[128]{0:T(128)S(1)}, f32[128]{0:T(128)}, u32[]{:S(2)}) copy-start(f32[128]{0:T(128)} %constant.91.clone) | copy-start | bytes 1540
  23.3 3.5 %copy-start.27 = (f32[2]{0:T(128)S(1)}, f32[2]{0:T(128)}, u32[]{:S(2)}) copy-start(f32[2]{0:T(128)} %slice.83) | copy-start | bytes 28
  23.3 3.5 %copy-start.28 = (f32[2]{0:T(128)S(1)}, f32[2]{0:T(128)}, u32[]{:S(2)}) copy-start(f32[2]{0:T(128)} %slice.84) | copy-start | bytes 28
  68.4 3.1 %slice-start.1 = ((s8[8388608]{0:T(1024)(128)(4,1)}), s8[4194304]{0:T(1024)(128)(4,1)S(1)}, s32[]{:S(2)}) async-start(s8[8388608]{0:T(1024)(128)(4,1)} %bitcast.104), calls=%async_computation.2 | async-start | bytes 8388608
  71.6 2.7 %copy-start.6 = (f32[2,1,64,1024]{3,2,1,0:T(8,128)S(1)}, f32[2,1,64,1024]{3,2,1,0:T(8,128)}, u32[]{:S(2)}) copy-start(f32[2,1,64,1024]{3,2,1,0:T(8,128)} %mul.1029) | copy-start | bytes 1572868
  71.6 2.7 %copy-start.7 = (f32[2,1,64,1024]{3,2,1,0:T(8,128)S(1)}, f32[2,1,64,1024]{3,2,1,0:T(8,128)}, u32[]{:S(2)}) copy-start(f32[2,1,64,1024]{3,2,1,0:T(8,128)} %mul.1004) | copy-start | bytes 1572868
  71.6 2.7 %copy-start.8 = (f32[2,1,64,1024]{3,2,1,0:T(8,128)S(1)}, f32[2,1,64,1024]{3,2,1,0:T(8,128)}, u32[]{:S(2)}) copy-start(f32[2,1,64,1024]{3,2,1,0:T(8,128)} %mul.1009) | copy-start | bytes 1572868
  71.6 2.7 %copy-start.9 = (f32[2,1,64,1024]{3,2,1,0:T(8,128)S(1)}, f32[2,1,64,1024]{3,2,1,0:T(8,128)}, u32[]{:S(2)}) copy-start(f32[2,1,64,1024]{3,2,1,0:T(8,128)} %mul.984) | copy-start | bytes 1572868
  71.6 2.7 %copy-start.10 = (f32[2,1,64,1024]{3,2,1,0:T(8,128)S(1)}, f32[2,1,64,1024]{3,2,1,0:T(8,128)}, u32[]{:S(2)}) copy-start(f32[2,1,64,1024]{3,2,1,0:T(8,128)} %mul.989) | copy-start | bytes 1572868
  71.6 2.7 %copy-start.15 = (f32[2,1,64,1024]{3,2,1,0:T(8,128)S(1)}, f32[2,1,64,1024]{3,2,1,0:T(8,128)}, u32[]{:S(2)}) copy-start(f32[2,1,64,1024]{3,2,1,0:T(8,128)} %mul.975) | copy-start | bytes 1572868
  71.6 2.7 %copy-start.16 = (f32[2,1,64,1024]{3,2,1,0:T(8,128)S(1)}, f32[2,1,64,1024]{3,2,1,0:T(8,128)}, u32[]{:S(2)}) copy-start(f32[2,1,64,1024]{3,2,1,0:T(8,128)} %mul.978) | copy-start | bytes 1572868
  87.0 8.0 %collective-permute-start = (bf16[4,2,64,128]{3,2,1,0:T(8,128)(2,1)S(1)}, bf16[4,2,64,128]{3,2,1,0:T(8,128)(2,1)S(1)}, u32[]{:S(2)}, u32[]{:S(2)}) collective-permute-start(bf16[4,2,64,128]{3,2,1,0:T(8,128)(2,1)S(1)} %get-tuple-element.40), channel_id=1, source_target_pairs={{0,2},{2,0},{4,6},{6,4},{8,10},{10,8},{12,14},{14,12},{1,3},{3,1},... | collective-permute-start | bytes 393224 | tf_op jit(solution)/shard_map/ppermute | solution.py:68
  89.1 9.4 %collective-permute-start.1 = (bf16[4,2,64,128]{3,2,1,0:T(8,128)(2,1)S(1)}, bf16[4,2,64,128]{3,2,1,0:T(8,128)(2,1)S(1)}, u32[]{:S(2)}, u32[]{:S(2)}) collective-permute-start(bf16[4,2,64,128]{3,2,1,0:T(8,128)(2,1)S(1)} %get-tuple-element.39), channel_id=1, source_target_pairs={{0,4},{2,6},{4,0},{6,2},{8,12},{10,14},{12,8},{14,10},{1,5},{3,7},... | collective-permute-start | bytes 393224 | tf_op jit(solution)/shard_map/ppermute | solution.py:68
  90.6 9.7 %collective-permute-start.2 = (bf16[4,2,64,128]{3,2,1,0:T(8,128)(2,1)S(1)}, bf16[4,2,64,128]{3,2,1,0:T(8,128)(2,1)S(1)}, u32[]{:S(2)}, u32[]{:S(2)}) collective-permute-start(bf16[4,2,64,128]{3,2,1,0:T(8,128)(2,1)S(1)} %get-tuple-element.38), channel_id=1, source_target_pairs={{0,6},{2,4},{4,2},{6,0},{8,14},{10,12},{12,10},{14,8},{1,7},{3,5},... | collective-permute-start | bytes 393224 | tf_op jit(solution)/shard_map/ppermute | solution.py:68
  90.7 9.7 %collective-permute-start.3 = (bf16[4,2,64,128]{3,2,1,0:T(8,128)(2,1)S(1)}, bf16[4,2,64,128]{3,2,1,0:T(8,128)(2,1)S(1)}, u32[]{:S(2)}, u32[]{:S(2)}) collective-permute-start(bf16[4,2,64,128]{3,2,1,0:T(8,128)(2,1)S(1)} %get-tuple-element.37), channel_id=1, source_target_pairs={{0,8},{2,10},{4,12},{6,14},{8,0},{10,2},{12,4},{14,6},{1,9},{3,11}... | collective-permute-start | bytes 393224 | tf_op jit(solution)/shard_map/ppermute | solution.py:68
  93.6 19.9 %collective-permute-start.4 = (bf16[4,2,64,128]{3,2,1,0:T(8,128)(2,1)S(1)}, bf16[4,2,64,128]{3,2,1,0:T(8,128)(2,1)S(1)}, u32[]{:S(2)}, u32[]{:S(2)}) collective-permute-start(bf16[4,2,64,128]{3,2,1,0:T(8,128)(2,1)S(1)} %get-tuple-element.36), channel_id=1, source_target_pairs={{0,10},{2,8},{4,14},{6,12},{8,2},{10,0},{12,6},{14,4},{1,11},{3,9}... | collective-permute-start | bytes 393224 | tf_op jit(solution)/shard_map/ppermute | solution.py:68
  95.0 18.5 %collective-permute-start.5 = (bf16[4,2,64,128]{3,2,1,0:T(8,128)(2,1)S(1)}, bf16[4,2,64,128]{3,2,1,0:T(8,128)(2,1)S(1)}, u32[]{:S(2)}, u32[]{:S(2)}) collective-permute-start(bf16[4,2,64,128]{3,2,1,0:T(8,128)(2,1)S(1)} %get-tuple-element.35), channel_id=1, source_target_pairs={{0,12},{2,14},{4,8},{6,10},{8,4},{10,6},{12,0},{14,2},{1,13},{3,15... | collective-permute-start | bytes 393224 | tf_op jit(solution)/shard_map/ppermute | solution.py:68
  98.5 15.0 %collective-permute-start.6 = (bf16[4,2,64,128]{3,2,1,0:T(8,128)(2,1)S(1)}, bf16[4,2,64,128]{3,2,1,0:T(8,128)(2,1)S(1)}, u32[]{:S(2)}, u32[]{:S(2)}) collective-permute-start(bf16[4,2,64,128]{3,2,1,0:T(8,128)(2,1)S(1)} %get-tuple-element.34), channel_id=1, source_target_pairs={{0,14},{2,12},{4,10},{6,8},{8,6},{10,4},{12,2},{14,0},{1,15},{3,13... | collective-permute-start | bytes 393224 | tf_op jit(solution)/shard_map/ppermute | solution.py:68
  114.5 5.0 %copy-start.1 = (s32[2,4]{1,0:T(2,128)S(1)}, s32[2,4]{1,0:T(2,128)}, u32[]{:S(2)}) copy-start(s32[2,4]{1,0:T(2,128)} %param.19) | copy-start | bytes 100
  (15 other events, 29.3 us)

commit v7 on v5

--- a/solution.py
+++ b/solution.py
@@ -4,6 +4,8 @@
 import numpy as np
 import jax.numpy as jnp
 from jax import lax
+from jax.experimental import pallas as pl
+from jax.experimental.pallas import tpu as pltpu
 from jax.sharding import Mesh
 from jax.sharding import PartitionSpec as P
 
@@ -56,6 +58,130 @@
     return product.reshape(children.shape[:-1] + (kernel.shape[1],))
 
 
+LANES = 128
+
+
+def merge_kernel(x_ref, t1c, t1s, f1c, f1s, t2c, t2s, f2c, f2s, k1_hbm, k2_hbm, o_ref,
+                 k1_v, k2_v, first_v, odd1_v, odd2_v, sems):
+    members, _, rows, local = x_ref.shape
+    beam_count = members // 4
+    blocks = local // LANES
+    wide = beam_count * blocks
+    half = wide * LANES
+    load_one = pltpu.make_async_copy(k1_hbm, k1_v, sems.at[0])
+    load_two = pltpu.make_async_copy(k2_hbm, k2_v, sems.at[1])
+    load_one.start()
+    load_two.start()
+
+    def turn(xr, xi, c1, s1, c2, s2):
+        cosine = c1 * c2 - s1 * s2
+        sines = s1 * c2 + c1 * s2
+        return xr * cosine - xi * sines, xr * sines + xi * cosine
+
+    for pair in range(2):
+        for u in range(wide):
+            b, k = divmod(u, blocks)
+            cols = pl.ds(k * LANES, LANES)
+            re_sum = None
+            for m in range(2):
+                s = 2 * pair + m
+                xr = x_ref[s * beam_count + b, 0, :, cols].astype(jnp.float32)
+                xi = x_ref[s * beam_count + b, 1, :, cols].astype(jnp.float32)
+                re, im = turn(xr, xi, t1c[s, 0, u], t1s[s, 0, u], f1c[s], f1s[s])
+                re_sum = re if re_sum is None else re_sum + re
+                im_sum = im if m == 0 else im_sum + im
+            out_cols = pl.ds(u * LANES, LANES)
+            first_v[pair, pl.ds(0, rows), out_cols] = re_sum.astype(first_v.dtype)
+            first_v[pair, pl.ds(rows, rows), out_cols] = im_sum.astype(first_v.dtype)
+
+    load_one.wait()
+    for s in range(4):
+        total = None
+        for b in range(beam_count):
+            part = x_ref[s * beam_count + b].reshape(2 * rows, local)
+            term = jnp.dot(part, k1_v[pl.ds(b * local, local), :], preferred_element_type=jnp.float32)
+            total = term if total is None else total + term
+        odd1_v[s] = total
+
+    for pair in range(2):
+        for u in range(wide):
+            cols = pl.ds(u * LANES, LANES)
+            for m in range(2):
+                s = 2 * pair + m
+                xr = odd1_v[s, pl.ds(0, rows), cols]
+                xi = odd1_v[s, pl.ds(rows, rows), cols]
+                re, im = turn(xr, xi, t1c[s, 1, u], t1s[s, 1, u], f1c[s], f1s[s])
+                re_sum = re if m == 0 else re_sum + re
+                im_sum = im if m == 0 else im_sum + im
+            out_cols = pl.ds(half + u * LANES, LANES)
+            first_v[pair, pl.ds(0, rows), out_cols] = re_sum.astype(first_v.dtype)
+            first_v[pair, pl.ds(rows, rows), out_cols] = im_sum.astype(first_v.dtype)
+
+    load_two.wait()
+    for pair in range(2):
+        odd2_v[pair] = jnp.dot(first_v[pair], k2_v[...], preferred_element_type=jnp.float32)
+
+    for t in range(4):
+        for u in range(wide):
+            at = (t // 2) * half + u * LANES if t % 2 == 0 else (t // 2) * half + u * LANES
+            cols = pl.ds(at, LANES)
+            for pair in range(2):
+                if t % 2 == 0:
+                    xr = first_v[pair, pl.ds(0, rows), cols].astype(jnp.float32)
+                    xi = first_v[pair, pl.ds(rows, rows), cols].astype(jnp.float32)
+                else:
+                    xr = odd2_v[pair, pl.ds(0, rows), cols]
+                    xi = odd2_v[pair, pl.ds(rows, rows), cols]
+                re, im = turn(xr, xi, t2c[pair, t, u], t2s[pair, t, u], f2c[pair], f2s[pair])
+                re_sum = re if pair == 0 else re_sum + re
+                im_sum = im if pair == 0 else im_sum + im
+            o_ref[t, 0, :, pl.ds(u * LANES, LANES)] = re_sum.astype(o_ref.dtype)
+            o_ref[t, 1, :, pl.ds(u * LANES, LANES)] = im_sum.astype(o_ref.dtype)
+
+
+def merge_call(x, tables, k1, k2, interpret=False):
+    members, _, rows, local = x.shape
+    width = k1.shape[0]
+    vmem = pl.BlockSpec(memory_space=pltpu.VMEM)
+    hbm = pl.BlockSpec(memory_space=pl.ANY)
+    return pl.pallas_call(
+        merge_kernel,
+        out_shape=jax.ShapeDtypeStruct((4, 2, rows, width), jnp.bfloat16),
+        in_specs=[vmem] * 9 + [hbm, hbm],
+        out_specs=vmem,
+        scratch_shapes=[
+            pltpu.VMEM((width, width), jnp.bfloat16),
+            pltpu.VMEM((2 * width, 2 * width), jnp.bfloat16),
+            pltpu.VMEM((2, 2 * rows, 2 * width), jnp.bfloat16),
+            pltpu.VMEM((4, 2 * rows, width), jnp.float32),
+            pltpu.VMEM((2, 2 * rows, 2 * width), jnp.float32),
+            pltpu.SemaphoreType.DMA((2,)),
+        ],
+        compiler_params=pltpu.CompilerParams(vmem_limit_bytes=48 * 1024 * 1024),
+        interpret=interpret,
+    )(x, *tables, k1, k2)
+
+
+def merge_tables(shifts, ratios, width):
+    units = np.arange(width // LANES)
+    fine = jnp.asarray(np.arange(LANES) / 512.0, jnp.float32)
+    scale_one = shifts[:, None] * ratios[None, :]
+    coarse_one = jnp.asarray(
+        [0.25 * units + ((2 * t + 1) / (2 * width) - 1.0) for t in range(2)], jnp.float32
+    )
+    rough_one = (scale_one[:, None, None, :] * coarse_one[None, :, :, None])[..., None]
+    small_one = scale_one[:, :, None] * fine
+    centers = (shifts[0::2] + shifts[1::2]) * 0.5
+    scale_two = centers[:, None] * ratios[None, :]
+    coarse_two = jnp.asarray(
+        [0.25 * units + ((2 * t + 1) / (4 * width) - 1.0) for t in range(4)], jnp.float32
+    )
+    rough_two = (scale_two[:, None, None, :] * coarse_two[None, :, :, None])[..., None]
+    small_two = scale_two[:, :, None] * fine
+    return (jnp.cos(rough_one), jnp.sin(rough_one), jnp.cos(small_one), jnp.sin(small_one),
+            jnp.cos(rough_two), jnp.sin(rough_two), jnp.cos(small_two), jnp.sin(small_two))
+
+
 def swap_pieces(pieces, place, axes):
     count = pieces.shape[0]
     flips = jnp.bitwise_xor(place, jnp.arange(count, dtype=jnp.int32))
@@ -81,34 +207,16 @@
 
     pieces = images[0].reshape(2, members, own_rows, local_beams).transpose(1, 0, 2, 3)
     gathered = lax.all_to_all(pieces, ("sub4", "beam"), 0, 0, tiled=True)
-    gathered = gathered.reshape(GROUP_SUBS, beam_count, 2, own_rows, local_beams)
-    children = gathered.transpose(0, 2, 3, 1, 4)
     rows_at = half_side * half_rows + member_at * own_rows + jnp.arange(own_rows, dtype=jnp.int32)
     ratios = NR / (NR + rows_at.astype(jnp.float32))
     shifts = lax.dynamic_slice_in_dim(offsets, group_at * GROUP_SUBS, GROUP_SUBS, 0)
-    children = children.reshape(GROUP_SUBS, 2, own_rows, B)
-    scale_one = shifts[:, None] * ratios[None, :]
-    odd_one = odd_local(children, jnp.asarray(odd_values(B)))
-    even_one = spin(children.astype(jnp.float32), scale_one, 2, 0, 2 * B)
-    odd_one = spin(odd_one, scale_one, 2, 1, 2 * B)
-    pairs = (GROUP_SUBS // 2, 2, 2, own_rows, B)
-    first = jnp.concatenate(
-        [even_one.reshape(pairs).sum(1), odd_one.reshape(pairs).sum(1)], -1
-    ).astype(jnp.bfloat16)
     order = split_order(2 * B)
-    kernel_two = jnp.asarray(odd_values(2 * B)[order][:, order])
-    centers = (shifts[0::2] + shifts[1::2]) * 0.5
-    scale_two = centers[:, None] * ratios[None, :]
-    odd_two = odd_local(first, kernel_two)
-    first_f = first.astype(jnp.float32)
-    merged = jnp.stack(
-        [
-            spin(first_f[..., :B], scale_two, 4, 0, 4 * B).sum(0),
-            spin(odd_two[..., :B], scale_two, 4, 1, 4 * B).sum(0),
-            spin(first_f[..., B:], scale_two, 4, 2, 4 * B).sum(0),
-            spin(odd_two[..., B:], scale_two, 4, 3, 4 * B).sum(0),
-        ]
-    ).astype(jnp.bfloat16)
+    merged = merge_call(
+        gathered,
+        merge_tables(shifts, ratios, B),
+        jnp.asarray(odd_values(B)),
+        jnp.asarray(odd_values(2 * B)[order][:, order]),
+    )
 
     sector_width = 4 * B // (beam_count * sub_count)
     tiles = merged.reshape(4, 2, own_rows, beam_count, sub_count, sector_width // 4)

time: 86.1 us -> 81 us (0.941)
  local copies, waits for them, and re-layouts: 31.1 us -> 11.4 us
  Pallas kernels: 0 us -> 9.95 us
  other arithmetic: 11.2 us -> 18.3 us
  matrix products: 7.06 us -> 0 us
  waiting for transfers between devices: 17.5 us -> 23.1 us
    sin x0 -> x4, other arithmetic: none -> 17.8 us  [the longest x1 8.56 us: merge_tables(): jnp.sin(rough_two)]
    pallas_call x0 -> x1, Pallas kernels: none -> 9.95 us  [merge_call(): pl.pallas_call(merge_kernel, out_shape=jax.ShapeDtypeStruct((4, 2, rows,...]
    sub x6 -> x0, local copies, waits for them, and re-layouts: 7.97 us -> none  [spin(): cosine = c1 * c2 - s1 * s2]
    add x6 -> x0, local copies, waits for them, and re-layouts: 7.55 us -> none  [spin(): sines = s1 * c2 + c1 * s2]
    dot_general x2 -> x0, matrix products: 7.06 us -> none  [odd_local(): jnp.dot(children.reshape(-1, children.shape[-1]), kernel, preferred_eleme...]
    all_to_all x1, waiting for transfers between devices: 2.14 us -> 7.42 us  [body(): gathered = lax.all_to_all(pieces, ('sub4', 'beam'), 0, 0, tiled=True)]
    add x2 -> x0, other arithmetic: 4.8 us -> none  [spin(): sines = s1 * c2 + c1 * s2]
    unnamed x46 -> x18, local copies, waits for them, and re-layouts: 4.63 us -> 1.05 us
  transfers between devices with their start and end apart: 8 -> 8, of which waited for: 5 -> 4; matrix products, arithmetic and copies ran while one was open for 28% -> 23% of each run, Pallas kernels for 0% -> 0%
where the time goes in v7:
time: 81 us; the launch traced here: 79.8 us
  waiting for transfers between devices  23.1 us (29%)
  other arithmetic  18.3 us (23%)
  starting transfers between devices  16.7 us (21%)
  local copies, waits for them, and re-layouts  11.4 us (14%)
  Pallas kernels  9.95 us (12%)
    ppermute x7, waiting for transfers between devices, swap_pieces(): moved.append(lax.ppermute(ordered[flip], axes, pairs))  15.7 us
    pallas_call x1, Pallas kernels, merge_call(): pl.pallas_call(merge_kernel, out_shape=jax.ShapeDtypeStruct((4, 2, rows,...  9.95 us
    ppermute x7, starting transfers between devices, swap_pieces(): moved.append(lax.ppermute(ordered[flip], axes, pairs))  9.45 us
    sin x1, other arithmetic, merge_tables(): jnp.sin(rough_two)  8.56 us
    sin x1, other arithmetic, merge_tables(): jnp.sin(rough_one)  8.41 us
    all_to_all x1, waiting for transfers between devices, body(): gathered = lax.all_to_all(pieces, ('sub4', 'beam'), 0, 0, tiled=True)  7.42 us
    all_to_all x1, starting transfers between devices, body(): gathered = lax.all_to_all(pieces, ('sub4', 'beam'), 0, 0, tiled=True)  7.28 us
    another operation x1, local copies, waits for them, and re-layouts, body(): images[0].reshape(2, members, own_rows, local_beams).transpose(1, 0, 2, 3)  2.34 us
  transfers between devices with their start and end apart: 8, of which 4 were waited for; matrix products, arithmetic and copies ran while one was open for 23% of the time, Pallas kernels for 0%

profile of v7, /device:TPU:0, one launch (start us, length us, event | category | flops | bytes accessed | tf_op | source)
XLA Modules:
  0.0 79.8 jit_solution(13593028673653229781)
XLA Ops:
  0.0 2.3 %copy.21 = bf16[2,8,64,512]{3,2,0,1:T(8,128)(2,1)} copy(bf16[2,8,64,512]{3,2,1,0:T(8,128)(2,1)} %bitcast.52) | data formatting | bytes 2097152 | tf_op jit(solution)/shard_map/reshape;squeeze | solution.py:208
  2.4 7.3 %all-to-all-start = ((bf16[8,2,64,512]{3,2,1,0:T(8,128)(2,1)}), bf16[8,2,64,512]{3,2,1,0:T(8,128)(2,1)S(1)}, u32[]{:S(2)}, u32[]{:S(2)}) async-start(bf16[8,2,64,512]{3,2,1,0:T(8,128)(2,1)} %bitcast.48), calls=%async_computation | async-start | bytes 2097152 | tf_op jit(solution)/shard_map/all_to_all | solution.py:209
  10.1 0.3 multiply_sine_fusion.3
  10.5 0.5 multiply_sine_fusion.2
  11.0 8.4 %multiply_sine_fusion.1 = (f32[4,2,8,64,1]{4,3,2,1,0:T(8,128)}, f32[4,2,8,64,1]{4,3,2,1,0:T(8,128)S(1)}) fusion(f32[2,8]{1,0:T(2,128)S(1)} %copy-done.3, f32[4,64]{1,0:T(4,128)S(1)} %broadcast_multiply_fusion), kind=kLoop, calls=%fused_computation.5 | loop fusion | flops 4096 | bytes 33856 | tf_op jit(solution)/shard_map/sin | solution.py:181
  19.4 8.6 %multiply_sine_fusion = (f32[2,4,8,64,1]{4,3,2,1,0:T(8,128)}, f32[2,4,8,64,1]{4,3,2,1,0:T(8,128)}) fusion(f32[4,8]{1,0:T(4,128)S(1)} %copy-done.1, f32[2,64]{1,0:T(2,128)S(1)} %broadcast_multiply_fusion.1), kind=kLoop, calls=%fused_computation.3 | loop fusion | flops 4096 | bytes 33408 | tf_op jit(solution)/shard_map/sin | solution.py:182
  28.0 7.4 %all-to-all-done.x_ref = bf16[8,2,64,512]{3,2,1,0:T(8,128)(2,1)S(1)} async-done(((bf16[8,2,64,512]{3,2,1,0:T(8,128)(2,1)}), bf16[8,2,64,512]{3,2,1,0:T(8,128)(2,1)S(1)}, u32[]{:S(2)}, u32[]{:S(2)}) %all-to-all-start) | async-done | bytes 1048608 | tf_op jit(solution)/shard_map/all_to_all | solution.py:209
  35.4 10.0 %shard_map.82 = bf16[4,2,64,1024]{3,2,1,0:T(8,128)(2,1)S(1)} custom-call(bf16[8,2,64,512]{3,2,1,0:T(8,128)(2,1)S(1)} %all-to-all-done.x_ref, f32[4,2,8,64,1]{4,3,2,1,0:T(8,128)S(1)} %get-tuple-element.17.t1c, f32[4,2,8,64,1]{4,3,2,1,0:T(8,128)} %get-tuple-element.16.t1s, f32[4,64,128]{2,1,0:T(8,128)S(1)} %get-tuple-element.19.f1c, ...), custom_call_target="tpu_custom_call" | custom-call | tf_op jit(solution)/shard_map/pallas_call | solution.py:147
  45.4 1.0 %copy-done = bf16[4,2,64,1024]{3,2,1,0:T(8,128)(2,1)} copy-done((bf16[4,2,64,1024]{3,2,1,0:T(8,128)(2,1)}, bf16[4,2,64,1024]{3,2,1,0:T(8,128)(2,1)S(1)}, u32[]{:S(2)}) %copy-start) | copy-done | bytes 1048600
  46.3 1.8 %reshape.149 = bf16[4,2,64,2,4,128]{5,4,3,2,1,0:T(4,128)(2,1)S(1)} reshape(bf16[4,2,64,1024]{3,2,1,0:T(8,128)(2,1)} %copy-done) | data formatting | bytes 2097152 | tf_op jit(solution)/shard_map/reshape | solution.py:222
  48.4 0.8 gather_fusion
  49.2 1.4 %copy.16 = bf16[2,4,4,2,64,128]{4,2,5,3,0,1:T(4,128)(2,1)S(1)} copy(bf16[2,4,4,2,64,128]{5,4,3,2,1,0:T(8,128)(2,1)S(1)} %bitcast.50) | data formatting | bytes 2097152 | tf_op jit(solution)/shard_map/gather | solution.py:224
  50.5 0.8 %copy.17 = bf16[8,2,512,64]{2,3,1,0:T(8,128)(2,1)S(1)} copy(bf16[8,2,512,64]{3,2,1,0:T(8,128)(2,1)S(1)} %bitcast.49) | data formatting | bytes 2097152 | tf_op jit(solution)/shard_map/reshape | solution.py:225
  51.4 0.6 gather_fusion.1
  52.3 1.5 %collective-permute-start = (bf16[2,512,64]{1,2,0:T(8,128)(2,1)S(1)}, bf16[2,512,64]{1,2,0:T(8,128)(2,1)S(1)}, u32[]{:S(2)}, u32[]{:S(2)}) collective-permute-start(bf16[2,512,64]{1,2,0:T(8,128)(2,1)S(1)} %get-tuple-element.12), channel_id=1, source_target_pairs={{0,2},{2,0},{4,6},{6,4},{8,10},{10,8},{12,14},{14,12},{1,3},{3,1},... | collective-permute-start | bytes 393224 | tf_op jit(solution)/shard_map/ppermute | solution.py:192
  53.8 2.0 %collective-permute-start.2 = (bf16[2,512,64]{1,2,0:T(8,128)(2,1)S(1)}, bf16[2,512,64]{1,2,0:T(8,128)(2,1)S(1)}, u32[]{:S(2)}, u32[]{:S(2)}) collective-permute-start(bf16[2,512,64]{1,2,0:T(8,128)(2,1)S(1)} %get-tuple-element.10), channel_id=1, source_target_pairs={{0,6},{2,4},{4,2},{6,0},{8,14},{10,12},{12,10},{14,8},{1,7},{3,5},... | collective-permute-start | bytes 393224 | tf_op jit(solution)/shard_map/ppermute | solution.py:192
  55.8 3.8 %collective-permute-start.4 = (bf16[2,512,64]{1,2,0:T(8,128)(2,1)S(1)}, bf16[2,512,64]{1,2,0:T(8,128)(2,1)S(1)}, u32[]{:S(2)}, u32[]{:S(2)}) collective-permute-start(bf16[2,512,64]{1,2,0:T(8,128)(2,1)S(1)} %get-tuple-element.8), channel_id=1, source_target_pairs={{0,10},{2,8},{4,14},{6,12},{8,2},{10,0},{12,6},{14,4},{1,11},{3,9}... | collective-permute-start | bytes 393224 | tf_op jit(solution)/shard_map/ppermute | solution.py:192
  59.7 1.4 %collective-permute-start.5 = (bf16[2,512,64]{1,2,0:T(8,128)(2,1)S(1)}, bf16[2,512,64]{1,2,0:T(8,128)(2,1)S(1)}, u32[]{:S(2)}, u32[]{:S(2)}) collective-permute-start(bf16[2,512,64]{1,2,0:T(8,128)(2,1)S(1)} %get-tuple-element.7), channel_id=1, source_target_pairs={{0,12},{2,14},{4,8},{6,10},{8,4},{10,6},{12,0},{14,2},{1,13},{3,15... | collective-permute-start | bytes 393224 | tf_op jit(solution)/shard_map/ppermute | solution.py:192
  61.1 1.8 %collective-permute-done.1 = bf16[2,512,64]{1,2,0:T(8,128)(2,1)S(1)} collective-permute-done((bf16[2,512,64]{1,2,0:T(8,128)(2,1)S(1)}, bf16[2,512,64]{1,2,0:T(8,128)(2,1)S(1)}, u32[]{:S(2)}, u32[]{:S(2)}) %collective-permute-start.1) | collective-permute-done | bytes 131104 | tf_op jit(solution)/shard_map/ppermute | solution.py:192
  62.9 0.7 collective-permute-start.6
  63.6 10.8 %collective-permute-done.3 = bf16[2,512,64]{1,2,0:T(8,128)(2,1)S(1)} collective-permute-done((bf16[2,512,64]{1,2,0:T(8,128)(2,1)S(1)}, bf16[2,512,64]{1,2,0:T(8,128)(2,1)S(1)}, u32[]{:S(2)}, u32[]{:S(2)}) %collective-permute-start.3) | collective-permute-done | bytes 131104 | tf_op jit(solution)/shard_map/ppermute | solution.py:192
  74.4 3.1 %collective-permute-done.4 = bf16[2,512,64]{1,2,0:T(8,128)(2,1)S(1)} collective-permute-done((bf16[2,512,64]{1,2,0:T(8,128)(2,1)S(1)}, bf16[2,512,64]{1,2,0:T(8,128)(2,1)S(1)}, u32[]{:S(2)}, u32[]{:S(2)}) %collective-permute-start.4) | collective-permute-done | bytes 131104 | tf_op jit(solution)/shard_map/ppermute | solution.py:192
  77.6 0.6 gather_fusion.2
  78.5 1.3 %copy.19 = bf16[1,1,2,512,512]{4,3,2,1,0:T(8,128)(2,1)} copy(bf16[1,1,2,512,512]{3,4,2,1,0:T(8,128)(2,1)S(1)} %bitcast.51) | data formatting | bytes 2097152 | tf_op jit(solution)/shard_map/reshape | solution.py:234
  (40 shorter events, 1.3 us)
Async XLA Ops:
  0.0 9.7 %copy-start.4 = (s32[2,4]{1,0:T(2,128)S(1)}, s32[2,4]{1,0:T(2,128)}, u32[]{:S(2)}) copy-start(s32[2,4]{1,0:T(2,128)} %param.12) | copy-start | bytes 100
  0.0 9.7 %copy-start.5 = (f32[4]{0:T(128)S(1)}, f32[4]{0:T(128)}, u32[]{:S(2)}) copy-start(f32[4]{0:T(128)} %param.11) | copy-start | bytes 52
  0.0 10.1 %copy-start.2 = (f32[128]{0:T(128)S(1)}, f32[128]{0:T(128)}, u32[]{:S(2)}) copy-start(f32[128]{0:T(128)} %constant.53.clone) | copy-start | bytes 1540
  0.0 11.0 %copy-start.3 = (f32[2,8]{1,0:T(2,128)S(1)}, f32[2,8]{1,0:T(2,128)}, u32[]{:S(2)}) copy-start(f32[2,8]{1,0:T(2,128)} %constant.54.clone) | copy-start | bytes 196
  2.4 33.0 %all-to-all-start = ((bf16[8,2,64,512]{3,2,1,0:T(8,128)(2,1)}), bf16[8,2,64,512]{3,2,1,0:T(8,128)(2,1)S(1)}, u32[]{:S(2)}, u32[]{:S(2)}) async-start(bf16[8,2,64,512]{3,2,1,0:T(8,128)(2,1)} %bitcast.48), calls=%async_computation | async-start | bytes 2097152 | tf_op jit(solution)/shard_map/all_to_all | solution.py:209
  11.0 8.4 %copy-start.1 = (f32[4,8]{1,0:T(4,128)S(1)}, f32[4,8]{1,0:T(4,128)}, u32[]{:S(2)}) copy-start(f32[4,8]{1,0:T(4,128)} %constant.55.clone) | copy-start | bytes 388
  45.4 1.0 %copy-start = (bf16[4,2,64,1024]{3,2,1,0:T(8,128)(2,1)}, bf16[4,2,64,1024]{3,2,1,0:T(8,128)(2,1)S(1)}, u32[]{:S(2)}) copy-start(bf16[4,2,64,1024]{3,2,1,0:T(8,128)(2,1)S(1)} %shard_map.82) | copy-start | bytes 3145732
  52.3 7.4 %collective-permute-start = (bf16[2,512,64]{1,2,0:T(8,128)(2,1)S(1)}, bf16[2,512,64]{1,2,0:T(8,128)(2,1)S(1)}, u32[]{:S(2)}, u32[]{:S(2)}) collective-permute-start(bf16[2,512,64]{1,2,0:T(8,128)(2,1)S(1)} %get-tuple-element.12), channel_id=1, source_target_pairs={{0,2},{2,0},{4,6},{6,4},{8,10},{10,8},{12,14},{14,12},{1,3},{3,1},... | collective-permute-start | bytes 393224 | tf_op jit(solution)/shard_map/ppermute | solution.py:192
  53.8 9.1 %collective-permute-start.1 = (bf16[2,512,64]{1,2,0:T(8,128)(2,1)S(1)}, bf16[2,512,64]{1,2,0:T(8,128)(2,1)S(1)}, u32[]{:S(2)}, u32[]{:S(2)}) collective-permute-start(bf16[2,512,64]{1,2,0:T(8,128)(2,1)S(1)} %get-tuple-element.11), channel_id=1, source_target_pairs={{0,4},{2,6},{4,0},{6,2},{8,12},{10,14},{12,8},{14,10},{1,5},{3,7},... | collective-permute-start | bytes 393224 | tf_op jit(solution)/shard_map/ppermute | solution.py:192
  53.8 9.8 %collective-permute-start.2 = (bf16[2,512,64]{1,2,0:T(8,128)(2,1)S(1)}, bf16[2,512,64]{1,2,0:T(8,128)(2,1)S(1)}, u32[]{:S(2)}, u32[]{:S(2)}) collective-permute-start(bf16[2,512,64]{1,2,0:T(8,128)(2,1)S(1)} %get-tuple-element.10), channel_id=1, source_target_pairs={{0,6},{2,4},{4,2},{6,0},{8,14},{10,12},{12,10},{14,8},{1,7},{3,5},... | collective-permute-start | bytes 393224 | tf_op jit(solution)/shard_map/ppermute | solution.py:192
  55.8 18.5 %collective-permute-start.3 = (bf16[2,512,64]{1,2,0:T(8,128)(2,1)S(1)}, bf16[2,512,64]{1,2,0:T(8,128)(2,1)S(1)}, u32[]{:S(2)}, u32[]{:S(2)}) collective-permute-start(bf16[2,512,64]{1,2,0:T(8,128)(2,1)S(1)} %get-tuple-element.9), channel_id=1, source_target_pairs={{0,8},{2,10},{4,12},{6,14},{8,0},{10,2},{12,4},{14,6},{1,9},{3,11}... | collective-permute-start | bytes 393224 | tf_op jit(solution)/shard_map/ppermute | solution.py:192
  55.8 21.7 %collective-permute-start.4 = (bf16[2,512,64]{1,2,0:T(8,128)(2,1)S(1)}, bf16[2,512,64]{1,2,0:T(8,128)(2,1)S(1)}, u32[]{:S(2)}, u32[]{:S(2)}) collective-permute-start(bf16[2,512,64]{1,2,0:T(8,128)(2,1)S(1)} %get-tuple-element.8), channel_id=1, source_target_pairs={{0,10},{2,8},{4,14},{6,12},{8,2},{10,0},{12,6},{14,4},{1,11},{3,9}... | collective-permute-start | bytes 393224 | tf_op jit(solution)/shard_map/ppermute | solution.py:192
  59.7 17.9 %collective-permute-start.5 = (bf16[2,512,64]{1,2,0:T(8,128)(2,1)S(1)}, bf16[2,512,64]{1,2,0:T(8,128)(2,1)S(1)}, u32[]{:S(2)}, u32[]{:S(2)}) collective-permute-start(bf16[2,512,64]{1,2,0:T(8,128)(2,1)S(1)} %get-tuple-element.7), channel_id=1, source_target_pairs={{0,12},{2,14},{4,8},{6,10},{8,4},{10,6},{12,0},{14,2},{1,13},{3,15... | collective-permute-start | bytes 393224 | tf_op jit(solution)/shard_map/ppermute | solution.py:192
  62.9 14.6 %collective-permute-start.6 = (bf16[2,512,64]{1,2,0:T(8,128)(2,1)S(1)}, bf16[2,512,64]{1,2,0:T(8,128)(2,1)S(1)}, u32[]{:S(2)}, u32[]{:S(2)}) collective-permute-start(bf16[2,512,64]{1,2,0:T(8,128)(2,1)S(1)} %get-tuple-element.6), channel_id=1, source_target_pairs={{0,14},{2,12},{4,10},{6,8},{8,6},{10,4},{12,2},{14,0},{1,15},{3,13... | collective-permute-start | bytes 393224 | tf_op jit(solution)/shard_map/ppermute | solution.py:192

commit v8 on v7

--- a/solution.py
+++ b/solution.py
@@ -61,7 +61,7 @@
 LANES = 128
 
 
-def merge_kernel(x_ref, t1c, t1s, f1c, f1s, t2c, t2s, f2c, f2s, k1_hbm, k2_hbm, o_ref,
+def merge_kernel(slot_ref, x_ref, t1c, t1s, f1c, f1s, t2c, t2s, f2c, f2s, k1_hbm, k2_hbm, o_ref,
                  k1_v, k2_v, first_v, odd1_v, odd2_v, sems):
     members, _, rows, local = x_ref.shape
     beam_count = members // 4
@@ -135,19 +135,21 @@
                 re, im = turn(xr, xi, t2c[pair, t, u], t2s[pair, t, u], f2c[pair], f2s[pair])
                 re_sum = re if pair == 0 else re_sum + re
                 im_sum = im if pair == 0 else im_sum + im
-            o_ref[t, 0, :, pl.ds(u * LANES, LANES)] = re_sum.astype(o_ref.dtype)
-            o_ref[t, 1, :, pl.ds(u * LANES, LANES)] = im_sum.astype(o_ref.dtype)
-
-
-def merge_call(x, tables, k1, k2, interpret=False):
+            slot = slot_ref[u]
+            o_ref[slot, t, 0] = re_sum.astype(o_ref.dtype)
+            o_ref[slot, t, 1] = im_sum.astype(o_ref.dtype)
+
+
+def merge_call(slots, x, tables, k1, k2, interpret=False):
     members, _, rows, local = x.shape
     width = k1.shape[0]
     vmem = pl.BlockSpec(memory_space=pltpu.VMEM)
     hbm = pl.BlockSpec(memory_space=pl.ANY)
+    smem = pl.BlockSpec(memory_space=pltpu.SMEM)
     return pl.pallas_call(
         merge_kernel,
-        out_shape=jax.ShapeDtypeStruct((4, 2, rows, width), jnp.bfloat16),
-        in_specs=[vmem] * 9 + [hbm, hbm],
+        out_shape=jax.ShapeDtypeStruct((width // LANES, 4, 2, rows, LANES), jnp.bfloat16),
+        in_specs=[smem] + [vmem] * 9 + [hbm, hbm],
         out_specs=vmem,
         scratch_shapes=[
             pltpu.VMEM((width, width), jnp.bfloat16),
@@ -159,7 +161,7 @@
         ],
         compiler_params=pltpu.CompilerParams(vmem_limit_bytes=48 * 1024 * 1024),
         interpret=interpret,
-    )(x, *tables, k1, k2)
+    )(slots, x, *tables, k1, k2)
 
 
 def merge_tables(shifts, ratios, width):
@@ -182,14 +184,13 @@
             jnp.cos(rough_two), jnp.sin(rough_two), jnp.cos(small_two), jnp.sin(small_two))
 
 
-def swap_pieces(pieces, place, axes):
-    count = pieces.shape[0]
-    flips = jnp.bitwise_xor(place, jnp.arange(count, dtype=jnp.int32))
-    ordered = jnp.take(pieces, flips, axis=0)
+def swap_ordered(ordered, place, axes):
+    count = ordered.shape[0]
     moved = [ordered[0]]
     for flip in range(1, count):
         pairs = [(i, i ^ flip) for i in range(count)]
         moved.append(lax.ppermute(ordered[flip], axes, pairs))
+    flips = jnp.bitwise_xor(place, jnp.arange(count, dtype=jnp.int32))
     return jnp.take(jnp.stack(moved), flips, axis=0)
 
 
@@ -211,24 +212,37 @@
     ratios = NR / (NR + rows_at.astype(jnp.float32))
     shifts = lax.dynamic_slice_in_dim(offsets, group_at * GROUP_SUBS, GROUP_SUBS, 0)
     order = split_order(2 * B)
+    blocks = B // LANES
+    sector_width = 4 * B // (beam_count * sub_count)
+    direct = group_count == 1 and sector_width == 4 * LANES
+    if direct:
+        shard_of = jnp.arange(blocks, dtype=jnp.int32) // sub_count
+        sector_of = jnp.arange(blocks, dtype=jnp.int32) % sub_count
+        holder = jnp.argmax(owners[shard_of] == sector_of[:, None], axis=1).astype(jnp.int32)
+        slots = jnp.bitwise_xor(member_at, holder * beam_count + shard_of)
+    else:
+        slots = jnp.arange(blocks, dtype=jnp.int32)
     merged = merge_call(
+        slots,
         gathered,
         merge_tables(shifts, ratios, B),
         jnp.asarray(odd_values(B)),
         jnp.asarray(odd_values(2 * B)[order][:, order]),
     )
-
-    sector_width = 4 * B // (beam_count * sub_count)
+    if direct:
+        ordered = merged.transpose(0, 2, 4, 1, 3).reshape(blocks, 2, sector_width, own_rows)
+        received = swap_ordered(ordered, member_at, ("sub4", "beam"))
+        received = received.transpose(1, 2, 0, 3)
+        return received.reshape(1, 1, 2, sector_width, members * own_rows)
+    merged = merged.transpose(1, 2, 3, 0, 4).reshape(4, 2, own_rows, B)
+
     tiles = merged.reshape(4, 2, own_rows, beam_count, sub_count, sector_width // 4)
     beam_ids = jnp.arange(beam_count, dtype=jnp.int32)[:, None]
     picked = tiles[:, :, :, beam_ids, owners, :]
     outgoing = picked.transpose(4, 3, 1, 5, 0, 2).reshape(
         sub_count * beam_count, 2, sector_width, own_rows
     )
-    if group_count == 1:
-        received = swap_pieces(outgoing, member_at, ("sub4", "beam"))
-    else:
-        received = lax.all_to_all(outgoing, ("grp", "sub4", "beam"), 0, 0, tiled=True)
+    received = lax.all_to_all(outgoing, ("grp", "sub4", "beam"), 0, 0, tiled=True)
     received = received.reshape(group_count, members, 2, sector_width, own_rows)
     received = received.transpose(0, 2, 3, 1, 4)
     return received.reshape(1, group_count, 2, sector_width, members * own_rows)

time: 81 us -> 76.1 us (0.940)
  the two profiles are of different devices: /device:TPU:0 before, /device:TPU:12 now
where the time goes in v8:
time: 76.1 us; the launch traced here: 75.9 us
  waiting for transfers between devices  22.1 us (29%)
  other arithmetic  19 us (25%)
  starting transfers between devices  16.5 us (22%)
  Pallas kernels  10.2 us (13%)
  local copies, waits for them, and re-layouts  7.83 us (10%)
    ppermute x7, waiting for transfers between devices, swap_ordered(): moved.append(lax.ppermute(ordered[flip], axes, pairs))  18.5 us
    ppermute x7, starting transfers between devices, swap_ordered(): moved.append(lax.ppermute(ordered[flip], axes, pairs))  10.2 us
    pallas_call x1, Pallas kernels, merge_call(): pl.pallas_call(merge_kernel, out_shape=jax.ShapeDtypeStruct((width // LAN...  10.2 us
    sin x1, other arithmetic, merge_tables(): jnp.sin(rough_two)  8.56 us
    sin x1, other arithmetic, merge_tables(): jnp.sin(rough_one)  8.45 us
    all_to_all x1, starting transfers between devices, body(): gathered = lax.all_to_all(pieces, ('sub4', 'beam'), 0, 0, tiled=True)  6.25 us
    all_to_all x1, waiting for transfers between devices, body(): gathered = lax.all_to_all(pieces, ('sub4', 'beam'), 0, 0, tiled=True)  3.68 us
    another operation x1, local copies, waits for them, and re-layouts, body(): images[0].reshape(2, members, own_rows, local_beams).transpose(1, 0, 2, 3)  2.32 us
  transfers between devices with their start and end apart: 8, of which 5 were waited for; matrix products, arithmetic and copies ran while one was open for 29% of the time, Pallas kernels for 0%

profile of v8, /device:TPU:12, one launch (start us, length us, event | category | flops | bytes accessed | tf_op | source)
XLA Modules:
  0.0 75.9 jit_solution(9677973663184844763)
XLA Ops:
  0.0 2.3 %copy.29 = bf16[2,8,64,512]{3,2,0,1:T(8,128)(2,1)} copy(bf16[2,8,64,512]{3,2,1,0:T(8,128)(2,1)} %bitcast.44) | data formatting | bytes 2097152 | tf_op jit(solution)/shard_map/reshape;squeeze | solution.py:209
  2.4 6.3 %all-to-all-start = ((bf16[8,2,64,512]{3,2,1,0:T(8,128)(2,1)}), bf16[8,2,64,512]{3,2,1,0:T(8,128)(2,1)S(1)}, u32[]{:S(2)}, u32[]{:S(2)}) async-start(bf16[8,2,64,512]{3,2,1,0:T(8,128)(2,1)} %bitcast.33), calls=%async_computation | async-start | bytes 2097152 | tf_op jit(solution)/shard_map/all_to_all | solution.py:210
  8.7 0.6 gather_fusion
  9.2 0.8 %iota_reduce_fusion = (pred[8]{0:T(512)(128)(4,1)}, s32[8]{0:T(128)S(1)}) fusion(s32[8,4]{1,0:T(8,128)S(1)} %gather_fusion, s32[8]{0:T(128)S(1)} %and_select_fusion.1), kind=kLoop, calls=%fused_computation.22 | loop fusion | flops 200 | bytes 200 | tf_op jit(solution)/shard_map/body/reduce | solution.py:221
  10.4 0.3 multiply_sine_fusion.3
  10.7 0.5 multiply_sine_fusion.2
  11.3 8.4 %multiply_sine_fusion.1 = (f32[4,2,8,64,1]{4,3,2,1,0:T(8,128)}, f32[4,2,8,64,1]{4,3,2,1,0:T(8,128)S(1)}) fusion(f32[2,8]{1,0:T(2,128)S(1)} %copy-done.3, f32[4,64]{1,0:T(4,128)S(1)} %broadcast_multiply_fusion), kind=kLoop, calls=%fused_computation.4 | loop fusion | flops 4096 | bytes 33856 | tf_op jit(solution)/shard_map/sin | solution.py:183
  19.7 8.6 %multiply_sine_fusion = (f32[2,4,8,64,1]{4,3,2,1,0:T(8,128)}, f32[2,4,8,64,1]{4,3,2,1,0:T(8,128)}) fusion(f32[4,8]{1,0:T(4,128)S(1)} %copy-done.1, f32[2,64]{1,0:T(2,128)S(1)} %broadcast_multiply_fusion.1), kind=kLoop, calls=%fused_computation.2 | loop fusion | flops 4096 | bytes 33408 | tf_op jit(solution)/shard_map/sin | solution.py:184
  28.3 3.7 %all-to-all-done.x_ref = bf16[8,2,64,512]{3,2,1,0:T(8,128)(2,1)S(1)} async-done(((bf16[8,2,64,512]{3,2,1,0:T(8,128)(2,1)}), bf16[8,2,64,512]{3,2,1,0:T(8,128)(2,1)S(1)}, u32[]{:S(2)}, u32[]{:S(2)}) %all-to-all-start) | async-done | bytes 1048608 | tf_op jit(solution)/shard_map/all_to_all | solution.py:210
  32.0 10.2 %shard_map.82 = bf16[8,4,2,64,128]{4,3,2,1,0:T(8,128)(2,1)S(1)} custom-call(s32[8]{0:T(128)S(1)} %fusion.3.slot_ref, bf16[8,2,64,512]{3,2,1,0:T(8,128)(2,1)S(1)} %all-to-all-done.x_ref, f32[4,2,8,64,1]{4,3,2,1,0:T(8,128)S(1)} %get-tuple-element.18.t1c, f32[4,2,8,64,1]{4,3,2,1,0:T(8,128)} %get-tuple-element.17.t1s, f32[4,64,128]{2,1,0:T(8,128)S(1)} %get-tuple-element.20.f1c, ...), custom_call_target="tpu_custom_call" | custom-call | tf_op jit(solution)/shard_map/pallas_call | solution.py:149
  42.2 0.2 copy.11
  42.5 0.6 collective-permute-start
  43.5 0.2 copy.13
  43.9 3.3 %collective-permute-start.1 = (bf16[2,512,64]{1,2,0:T(8,128)(2,1)S(1)}, bf16[2,512,64]{1,2,0:T(8,128)(2,1)S(1)}, u32[]{:S(2)}, u32[]{:S(2)}) collective-permute-start(bf16[2,512,64]{1,2,0:T(8,128)(2,1)S(1)} %copy.14), channel_id=1, source_target_pairs={{0,4},{2,6},{4,0},{6,2},{8,12},{10,14},{12,8},{14,10},{1,5},{3,7},... | collective-permute-start | bytes 393224 | tf_op jit(solution)/shard_map/ppermute | solution.py:192
  48.0 1.8 %collective-permute-start.3 = (bf16[2,512,64]{1,2,0:T(8,128)(2,1)S(1)}, bf16[2,512,64]{1,2,0:T(8,128)(2,1)S(1)}, u32[]{:S(2)}, u32[]{:S(2)}) collective-permute-start(bf16[2,512,64]{1,2,0:T(8,128)(2,1)S(1)} %copy.18), channel_id=1, source_target_pairs={{0,8},{2,10},{4,12},{6,14},{8,0},{10,2},{12,4},{14,6},{1,9},{3,11}... | collective-permute-start | bytes 393224 | tf_op jit(solution)/shard_map/ppermute | solution.py:192
  50.1 2.1 %collective-permute-start.4 = (bf16[2,512,64]{1,2,0:T(8,128)(2,1)S(1)}, bf16[2,512,64]{1,2,0:T(8,128)(2,1)S(1)}, u32[]{:S(2)}, u32[]{:S(2)}) collective-permute-start(bf16[2,512,64]{1,2,0:T(8,128)(2,1)S(1)} %copy.20), channel_id=1, source_target_pairs={{0,10},{2,8},{4,14},{6,12},{8,2},{10,0},{12,6},{14,4},{1,11},{3,9}... | collective-permute-start | bytes 393224 | tf_op jit(solution)/shard_map/ppermute | solution.py:192
  52.9 0.6 collective-permute-start.5
  53.6 1.6 %collective-permute-start.6 = (bf16[2,512,64]{1,2,0:T(8,128)(2,1)S(1)}, bf16[2,512,64]{1,2,0:T(8,128)(2,1)S(1)}, u32[]{:S(2)}, u32[]{:S(2)}) collective-permute-start(bf16[2,512,64]{1,2,0:T(8,128)(2,1)S(1)} %copy.24), channel_id=1, source_target_pairs={{0,14},{2,12},{4,10},{6,8},{8,6},{10,4},{12,2},{14,0},{1,15},{3,13... | collective-permute-start | bytes 393224 | tf_op jit(solution)/shard_map/ppermute | solution.py:192
  55.2 9.3 %collective-permute-done.3 = bf16[2,512,64]{1,2,0:T(8,128)(2,1)S(1)} collective-permute-done((bf16[2,512,64]{1,2,0:T(8,128)(2,1)S(1)}, bf16[2,512,64]{1,2,0:T(8,128)(2,1)S(1)}, u32[]{:S(2)}, u32[]{:S(2)}) %collective-permute-start.3) | collective-permute-done | bytes 131104 | tf_op jit(solution)/shard_map/ppermute | solution.py:192
  64.5 2.8 %collective-permute-done.4 = bf16[2,512,64]{1,2,0:T(8,128)(2,1)S(1)} collective-permute-done((bf16[2,512,64]{1,2,0:T(8,128)(2,1)S(1)}, bf16[2,512,64]{1,2,0:T(8,128)(2,1)S(1)}, u32[]{:S(2)}, u32[]{:S(2)}) %collective-permute-start.4) | collective-permute-done | bytes 131104 | tf_op jit(solution)/shard_map/ppermute | solution.py:192
  67.3 4.9 %collective-permute-done.5 = bf16[2,512,64]{1,2,0:T(8,128)(2,1)S(1)} collective-permute-done((bf16[2,512,64]{1,2,0:T(8,128)(2,1)S(1)}, bf16[2,512,64]{1,2,0:T(8,128)(2,1)S(1)}, u32[]{:S(2)}, u32[]{:S(2)}) %collective-permute-start.5) | collective-permute-done | bytes 131104 | tf_op jit(solution)/shard_map/ppermute | solution.py:192
  72.2 1.5 %collective-permute-done.6 = bf16[2,512,64]{1,2,0:T(8,128)(2,1)S(1)} collective-permute-done((bf16[2,512,64]{1,2,0:T(8,128)(2,1)S(1)}, bf16[2,512,64]{1,2,0:T(8,128)(2,1)S(1)}, u32[]{:S(2)}, u32[]{:S(2)}) %collective-permute-start.6) | collective-permute-done | bytes 131104 | tf_op jit(solution)/shard_map/ppermute | solution.py:192
  73.7 0.6 gather_fusion.1
  74.6 1.3 %copy.27 = bf16[1,1,2,512,512]{4,3,2,1,0:T(8,128)(2,1)} copy(bf16[1,1,2,512,512]{3,4,2,1,0:T(8,128)(2,1)S(1)} %bitcast.35) | data formatting | bytes 2097152 | tf_op jit(solution)/shard_map/reshape | solution.py:236
  (52 shorter events, 3.1 us)
Async XLA Ops:
  0.0 8.7 %copy-start = (s32[2,4]{1,0:T(2,128)S(1)}, s32[2,4]{1,0:T(2,128)}, u32[]{:S(2)}) copy-start(s32[2,4]{1,0:T(2,128)} %param.10) | copy-start | bytes 100
  0.0 10.0 %copy-start.4 = (f32[4]{0:T(128)S(1)}, f32[4]{0:T(128)}, u32[]{:S(2)}) copy-start(f32[4]{0:T(128)} %param.9) | copy-start | bytes 52
  0.0 10.4 %copy-start.2 = (f32[128]{0:T(128)S(1)}, f32[128]{0:T(128)}, u32[]{:S(2)}) copy-start(f32[128]{0:T(128)} %constant.89.clone) | copy-start | bytes 1540
  0.0 11.2 %copy-start.3 = (f32[2,8]{1,0:T(2,128)S(1)}, f32[2,8]{1,0:T(2,128)}, u32[]{:S(2)}) copy-start(f32[2,8]{1,0:T(2,128)} %constant.90.clone) | copy-start | bytes 196
  2.4 29.6 %all-to-all-start = ((bf16[8,2,64,512]{3,2,1,0:T(8,128)(2,1)}), bf16[8,2,64,512]{3,2,1,0:T(8,128)(2,1)S(1)}, u32[]{:S(2)}, u32[]{:S(2)}) async-start(bf16[8,2,64,512]{3,2,1,0:T(8,128)(2,1)} %bitcast.33), calls=%async_computation | async-start | bytes 2097152 | tf_op jit(solution)/shard_map/all_to_all | solution.py:210
  11.2 8.5 %copy-start.1 = (f32[4,8]{1,0:T(4,128)S(1)}, f32[4,8]{1,0:T(4,128)}, u32[]{:S(2)}) copy-start(f32[4,8]{1,0:T(4,128)} %constant.91.clone) | copy-start | bytes 388
  42.5 10.4 %collective-permute-start = (bf16[2,512,64]{1,2,0:T(8,128)(2,1)S(1)}, bf16[2,512,64]{1,2,0:T(8,128)(2,1)S(1)}, u32[]{:S(2)}, u32[]{:S(2)}) collective-permute-start(bf16[2,512,64]{1,2,0:T(8,128)(2,1)S(1)} %copy.12), channel_id=1, source_target_pairs={{0,2},{2,0},{4,6},{6,4},{8,10},{10,8},{12,14},{14,12},{1,3},{3,1},... | collective-permute-start | bytes 393224 | tf_op jit(solution)/shard_map/ppermute | solution.py:192
  43.9 9.7 %collective-permute-start.1 = (bf16[2,512,64]{1,2,0:T(8,128)(2,1)S(1)}, bf16[2,512,64]{1,2,0:T(8,128)(2,1)S(1)}, u32[]{:S(2)}, u32[]{:S(2)}) collective-permute-start(bf16[2,512,64]{1,2,0:T(8,128)(2,1)S(1)} %copy.14), channel_id=1, source_target_pairs={{0,4},{2,6},{4,0},{6,2},{8,12},{10,14},{12,8},{14,10},{1,5},{3,7},... | collective-permute-start | bytes 393224 | tf_op jit(solution)/shard_map/ppermute | solution.py:192
  47.5 7.6 %collective-permute-start.2 = (bf16[2,512,64]{1,2,0:T(8,128)(2,1)S(1)}, bf16[2,512,64]{1,2,0:T(8,128)(2,1)S(1)}, u32[]{:S(2)}, u32[]{:S(2)}) collective-permute-start(bf16[2,512,64]{1,2,0:T(8,128)(2,1)S(1)} %copy.16), channel_id=1, source_target_pairs={{0,6},{2,4},{4,2},{6,0},{8,14},{10,12},{12,10},{14,8},{1,7},{3,5},... | collective-permute-start | bytes 393224 | tf_op jit(solution)/shard_map/ppermute | solution.py:192
  48.0 16.5 %collective-permute-start.3 = (bf16[2,512,64]{1,2,0:T(8,128)(2,1)S(1)}, bf16[2,512,64]{1,2,0:T(8,128)(2,1)S(1)}, u32[]{:S(2)}, u32[]{:S(2)}) collective-permute-start(bf16[2,512,64]{1,2,0:T(8,128)(2,1)S(1)} %copy.18), channel_id=1, source_target_pairs={{0,8},{2,10},{4,12},{6,14},{8,0},{10,2},{12,4},{14,6},{1,9},{3,11}... | collective-permute-start | bytes 393224 | tf_op jit(solution)/shard_map/ppermute | solution.py:192
  50.1 17.2 %collective-permute-start.4 = (bf16[2,512,64]{1,2,0:T(8,128)(2,1)S(1)}, bf16[2,512,64]{1,2,0:T(8,128)(2,1)S(1)}, u32[]{:S(2)}, u32[]{:S(2)}) collective-permute-start(bf16[2,512,64]{1,2,0:T(8,128)(2,1)S(1)} %copy.20), channel_id=1, source_target_pairs={{0,10},{2,8},{4,14},{6,12},{8,2},{10,0},{12,6},{14,4},{1,11},{3,9}... | collective-permute-start | bytes 393224 | tf_op jit(solution)/shard_map/ppermute | solution.py:192
  52.9 19.3 %collective-permute-start.5 = (bf16[2,512,64]{1,2,0:T(8,128)(2,1)S(1)}, bf16[2,512,64]{1,2,0:T(8,128)(2,1)S(1)}, u32[]{:S(2)}, u32[]{:S(2)}) collective-permute-start(bf16[2,512,64]{1,2,0:T(8,128)(2,1)S(1)} %copy.22), channel_id=1, source_target_pairs={{0,12},{2,14},{4,8},{6,10},{8,4},{10,6},{12,0},{14,2},{1,13},{3,15... | collective-permute-start | bytes 393224 | tf_op jit(solution)/shard_map/ppermute | solution.py:192
  53.6 20.1 %collective-permute-start.6 = (bf16[2,512,64]{1,2,0:T(8,128)(2,1)S(1)}, bf16[2,512,64]{1,2,0:T(8,128)(2,1)S(1)}, u32[]{:S(2)}, u32[]{:S(2)}) collective-permute-start(bf16[2,512,64]{1,2,0:T(8,128)(2,1)S(1)} %copy.24), channel_id=1, source_target_pairs={{0,14},{2,12},{4,10},{6,8},{8,6},{10,4},{12,2},{14,0},{1,15},{3,13... | collective-permute-start | bytes 393224 | tf_op jit(solution)/shard_map/ppermute | solution.py:192

commit v9 on v8

--- a/solution.py
+++ b/solution.py
@@ -61,7 +61,7 @@
 LANES = 128
 
 
-def merge_kernel(slot_ref, x_ref, t1c, t1s, f1c, f1s, t2c, t2s, f2c, f2s, k1_hbm, k2_hbm, o_ref,
+def merge_kernel(slot_ref, sender_ref, x_ref, t1c, t1s, f1c, f1s, t2c, t2s, f2c, f2s, k1_hbm, k2_hbm, o_ref,
                  k1_v, k2_v, first_v, odd1_v, odd2_v, sems):
     members, _, rows, local = x_ref.shape
     beam_count = members // 4
@@ -85,8 +85,8 @@
             re_sum = None
             for m in range(2):
                 s = 2 * pair + m
-                xr = x_ref[s * beam_count + b, 0, :, cols].astype(jnp.float32)
-                xi = x_ref[s * beam_count + b, 1, :, cols].astype(jnp.float32)
+                xr = x_ref[sender_ref[s * beam_count + b], 0, :, cols].astype(jnp.float32)
+                xi = x_ref[sender_ref[s * beam_count + b], 1, :, cols].astype(jnp.float32)
                 re, im = turn(xr, xi, t1c[s, 0, u], t1s[s, 0, u], f1c[s], f1s[s])
                 re_sum = re if re_sum is None else re_sum + re
                 im_sum = im if m == 0 else im_sum + im
@@ -98,7 +98,7 @@
     for s in range(4):
         total = None
         for b in range(beam_count):
-            part = x_ref[s * beam_count + b].reshape(2 * rows, local)
+            part = x_ref[sender_ref[s * beam_count + b]].reshape(2 * rows, local)
             term = jnp.dot(part, k1_v[pl.ds(b * local, local), :], preferred_element_type=jnp.float32)
             total = term if total is None else total + term
         odd1_v[s] = total
@@ -140,7 +140,7 @@
             o_ref[slot, t, 1] = im_sum.astype(o_ref.dtype)
 
 
-def merge_call(slots, x, tables, k1, k2, interpret=False):
+def merge_call(slots, senders, x, tables, k1, k2, interpret=False):
     members, _, rows, local = x.shape
     width = k1.shape[0]
     vmem = pl.BlockSpec(memory_space=pltpu.VMEM)
@@ -149,7 +149,7 @@
     return pl.pallas_call(
         merge_kernel,
         out_shape=jax.ShapeDtypeStruct((width // LANES, 4, 2, rows, LANES), jnp.bfloat16),
-        in_specs=[smem] + [vmem] * 9 + [hbm, hbm],
+        in_specs=[smem, smem] + [vmem] * 9 + [hbm, hbm],
         out_specs=vmem,
         scratch_shapes=[
             pltpu.VMEM((width, width), jnp.bfloat16),
@@ -161,7 +161,7 @@
         ],
         compiler_params=pltpu.CompilerParams(vmem_limit_bytes=48 * 1024 * 1024),
         interpret=interpret,
-    )(slots, x, *tables, k1, k2)
+    )(slots, senders, x, *tables, k1, k2)
 
 
 def merge_tables(shifts, ratios, width):
@@ -171,17 +171,21 @@
     coarse_one = jnp.asarray(
         [0.25 * units + ((2 * t + 1) / (2 * width) - 1.0) for t in range(2)], jnp.float32
     )
-    rough_one = (scale_one[:, None, None, :] * coarse_one[None, :, :, None])[..., None]
+    rough_one = scale_one[:, None, None, :] * coarse_one[None, :, :, None]
     small_one = scale_one[:, :, None] * fine
     centers = (shifts[0::2] + shifts[1::2]) * 0.5
     scale_two = centers[:, None] * ratios[None, :]
     coarse_two = jnp.asarray(
         [0.25 * units + ((2 * t + 1) / (4 * width) - 1.0) for t in range(4)], jnp.float32
     )
-    rough_two = (scale_two[:, None, None, :] * coarse_two[None, :, :, None])[..., None]
+    rough_two = scale_two[:, None, None, :] * coarse_two[None, :, :, None]
     small_two = scale_two[:, :, None] * fine
-    return (jnp.cos(rough_one), jnp.sin(rough_one), jnp.cos(small_one), jnp.sin(small_one),
-            jnp.cos(rough_two), jnp.sin(rough_two), jnp.cos(small_two), jnp.sin(small_two))
+    compact = lax.optimization_barrier(
+        (jnp.cos(rough_one), jnp.sin(rough_one), jnp.cos(rough_two), jnp.sin(rough_two))
+    )
+    c1, s1, c2, s2 = (part[..., None] for part in compact)
+    return (c1, s1, jnp.cos(small_one), jnp.sin(small_one),
+            c2, s2, jnp.cos(small_two), jnp.sin(small_two))
 
 
 def swap_ordered(ordered, place, axes):
@@ -206,8 +210,14 @@
     own_rows = half_rows // members
     local_beams = images.shape[3]
 
-    pieces = images[0].reshape(2, members, own_rows, local_beams).transpose(1, 0, 2, 3)
-    gathered = lax.all_to_all(pieces, ("sub4", "beam"), 0, 0, tiled=True)
+    flips = jnp.bitwise_xor(member_at, jnp.arange(members, dtype=jnp.int32))
+    image = images[0]
+    moved = [lax.dynamic_slice_in_dim(image, member_at * own_rows, own_rows, 1)]
+    for flip in range(1, members):
+        piece = lax.dynamic_slice_in_dim(image, flips[flip] * own_rows, own_rows, 1)
+        pairs = [(i, i ^ flip) for i in range(members)]
+        moved.append(lax.ppermute(piece, ("sub4", "beam"), pairs))
+    gathered = jnp.stack(moved)
     rows_at = half_side * half_rows + member_at * own_rows + jnp.arange(own_rows, dtype=jnp.int32)
     ratios = NR / (NR + rows_at.astype(jnp.float32))
     shifts = lax.dynamic_slice_in_dim(offsets, group_at * GROUP_SUBS, GROUP_SUBS, 0)
@@ -224,6 +234,7 @@
         slots = jnp.arange(blocks, dtype=jnp.int32)
     merged = merge_call(
         slots,
+        flips,
         gathered,
         merge_tables(shifts, ratios, B),
         jnp.asarray(odd_values(B)),

time: 76.1 us -> 85.7 us (1.13)
  local copies, waits for them, and re-layouts: 7.83 us -> 22.9 us
  other arithmetic: 19 us -> 4.75 us
  between operations: 0.33 us -> 4.79 us
  starting transfers between devices: 16.5 us -> 19.3 us
    broadcast_in_dim x0 -> x4, local copies, waits for them, and re-layouts: none -> 9.76 us  [merge_tables(): c1, s1, c2, s2 = (part[..., None] for part in compact)]
    ppermute x0 -> x7, starting transfers between devices: none -> 9.4 us  [body(): moved.append(lax.ppermute(piece, ('sub4', 'beam'), pairs))]
    sin x1, other arithmetic: 8.56 us -> 0.82 us  [merge_tables(): jnp.sin(rough_two)]
    sin x1, other arithmetic: 8.45 us -> 0.82 us  [merge_tables(): jnp.sin(rough_one)]
    all_to_all x1 -> x0, starting transfers between devices: 6.25 us -> none  [body(): gathered = lax.all_to_all(pieces, ('sub4', 'beam'), 0, 0, tiled=True)]
    ppermute x0 -> x7, waiting for transfers between devices: none -> 5.75 us  [body(): moved.append(lax.ppermute(piece, ('sub4', 'beam'), pairs))]
    unnamed x17 -> x23, local copies, waits for them, and re-layouts: 0.09 us -> 4.67 us
    all_to_all x1 -> x0, waiting for transfers between devices: 3.68 us -> none  [body(): gathered = lax.all_to_all(pieces, ('sub4', 'beam'), 0, 0, tiled=True)]
  transfers between devices with their start and end apart: 8 -> 14, of which waited for: 5 -> 6; matrix products, arithmetic and copies ran while one was open for 29% -> 26% of each run, Pallas kernels for 0% -> 0%
where the time goes in v9:
time: 85.7 us; the launch traced here: 85.2 us
  local copies, waits for them, and re-layouts  22.9 us (27%)
  waiting for transfers between devices  22.8 us (27%)
  starting transfers between devices  19.3 us (23%)
  Pallas kernels  10.7 us (12%)
  between operations  4.79 us (6%)
  other arithmetic  4.75 us (6%)
    ppermute x7, waiting for transfers between devices, swap_ordered(): moved.append(lax.ppermute(ordered[flip], axes, pairs))  17.1 us
    pallas_call x1, Pallas kernels, merge_call(): pl.pallas_call(merge_kernel, out_shape=jax.ShapeDtypeStruct((width // LAN...  10.7 us
    ppermute x7, starting transfers between devices, swap_ordered(): moved.append(lax.ppermute(ordered[flip], axes, pairs))  9.86 us
    broadcast_in_dim x4, local copies, waits for them, and re-layouts, merge_tables(): c1, s1, c2, s2 = (part[..., None] for part in compact)  9.76 us
    ppermute x7, starting transfers between devices, body(): moved.append(lax.ppermute(piece, ('sub4', 'beam'), pairs))  9.4 us
    ppermute x7, waiting for transfers between devices, body(): moved.append(lax.ppermute(piece, ('sub4', 'beam'), pairs))  5.75 us
    unnamed x23, local copies, waits for them, and re-layouts  4.67 us
    dynamic_slice x1, local copies, waits for them, and re-layouts, body(): piece = lax.dynamic_slice_in_dim(image, flips[flip] * own_rows, own_rows, 1)  2.23 us
  transfers between devices with their start and end apart: 14, of which 6 were waited for; matrix products, arithmetic and copies ran while one was open for 26% of the time, Pallas kernels for 0%

profile of v9, /device:TPU:12, one launch (start us, length us, event | category | flops | bytes accessed | tf_op | source)
XLA Modules:
  0.0 85.2 jit_solution(2936897941650745237)
XLA Ops:
  5.1 2.2 %dynamic-slice_bitcast_fusion = (bf16[2,64,512]{2,1,0:T(8,128)(2,1)}, bf16[2,64,512]{2,1,0:T(8,128)(2,1)}, bf16[2,64,512]{2,1,0:T(8,128)(2,1)}, bf16[2,64,512]{2...) fusion(bf16[1,2,512,512]{3,2,1,0:T(8,128)(2,1)} %param.8, ...), kind=kLoop, calls=%fused_computation.19 | loop fusion | bytes 2097184 | tf_op jit(solution)/shard_map/dynamic_slice | solution.py:217
  7.4 1.5 %collective-permute-start = (bf16[2,64,512]{2,1,0:T(8,128)(2,1)}, bf16[2,64,512]{2,1,0:T(8,128)(2,1)}, u32[]{:S(2)}, u32[]{:S(2)}) collective-permute-start(bf16[2,64,512]{2,1,0:T(8,128)(2,1)} %get-tuple-element.28), channel_id=1, source_target_pairs={{0,2},{2,0},{4,6},{6,4},{8,10},{10,8},{12,14},{14,12},{1,3},{3,1},... | collective-permute-start | bytes 393224 | tf_op jit(solution)/shard_map/ppermute | solution.py:219
  9.3 1.5 %collective-permute-start.2 = (bf16[2,64,512]{2,1,0:T(8,128)(2,1)}, bf16[2,64,512]{2,1,0:T(8,128)(2,1)}, u32[]{:S(2)}, u32[]{:S(2)}) collective-permute-start(bf16[2,64,512]{2,1,0:T(8,128)(2,1)} %get-tuple-element.26), channel_id=1, source_target_pairs={{0,6},{2,4},{4,2},{6,0},{8,14},{10,12},{12,10},{14,8},{1,7},{3,5},... | collective-permute-start | bytes 393224 | tf_op jit(solution)/shard_map/ppermute | solution.py:219
  10.9 2.6 %collective-permute-start.3 = (bf16[2,64,512]{2,1,0:T(8,128)(2,1)}, bf16[2,64,512]{2,1,0:T(8,128)(2,1)}, u32[]{:S(2)}, u32[]{:S(2)}) collective-permute-start(bf16[2,64,512]{2,1,0:T(8,128)(2,1)} %get-tuple-element.25), channel_id=1, source_target_pairs={{0,8},{2,10},{4,12},{6,14},{8,0},{10,2},{12,4},{14,6},{1,9},{3,11}... | collective-permute-start | bytes 393224 | tf_op jit(solution)/shard_map/ppermute | solution.py:219
  13.4 1.3 %collective-permute-start.4 = (bf16[2,64,512]{2,1,0:T(8,128)(2,1)}, bf16[2,64,512]{2,1,0:T(8,128)(2,1)}, u32[]{:S(2)}, u32[]{:S(2)}) collective-permute-start(bf16[2,64,512]{2,1,0:T(8,128)(2,1)} %get-tuple-element.24), channel_id=1, source_target_pairs={{0,10},{2,8},{4,14},{6,12},{8,2},{10,0},{12,6},{14,4},{1,11},{3,9}... | collective-permute-start | bytes 393224 | tf_op jit(solution)/shard_map/ppermute | solution.py:219
  19.5 1.4 %copy.31.t1c = f32[4,2,8,64,1]{4,3,2,1,0:T(8,128)S(1)} copy(f32[4,2,8,64,1]{3,2,1,0,4:T(8,128)} %bitcast.82) | data formatting | bytes 32768 | tf_op jit(solution)/shard_map/broadcast_in_dim | solution.py:186
  20.9 2.8 %copy.32.t1s = f32[4,2,8,64,1]{4,3,2,1,0:T(8,128)} copy(f32[4,2,8,64,1]{3,2,1,0,4:T(8,128)} %bitcast.81) | data formatting | bytes 32768 | tf_op jit(solution)/shard_map/broadcast_in_dim | solution.py:186
  23.7 2.8 %copy.33.t2c = f32[2,4,8,64,1]{4,3,2,1,0:T(8,128)} copy(f32[2,4,8,64,1]{3,2,1,0,4:T(8,128)} %bitcast.80) | data formatting | bytes 32768 | tf_op jit(solution)/shard_map/broadcast_in_dim | solution.py:186
  26.5 2.8 %copy.34.t2s = f32[2,4,8,64,1]{4,3,2,1,0:T(8,128)} copy(f32[2,4,8,64,1]{3,2,1,0,4:T(8,128)} %bitcast.79) | data formatting | bytes 32768 | tf_op jit(solution)/shard_map/broadcast_in_dim | solution.py:186
  29.9 1.6 %collective-permute-start.5 = (bf16[2,64,512]{2,1,0:T(8,128)(2,1)}, bf16[2,64,512]{2,1,0:T(8,128)(2,1)S(1)}, u32[]{:S(2)}, u32[]{:S(2)}) collective-permute-start(bf16[2,64,512]{2,1,0:T(8,128)(2,1)} %get-tuple-element.30), channel_id=1, source_target_pairs={{0,12},{2,14},{4,8},{6,10},{8,4},{10,6},{12,0},{14,2},{1,13},{3,15... | collective-permute-start | bytes 393224 | tf_op jit(solution)/shard_map/ppermute | solution.py:219
  33.8 0.9 %bitcast_dynamic-update-slice_fusion.11 = bf16[8,2,64,512]{3,2,1,0:T(8,128)(2,1)S(1)} fusion(bf16[8,2,64,512]{3,2,1,0:T(8,128)(2,1)S(1)} %bitcast_dynamic-update-slice_fusion.12, bf16[2,64,512]{2,1,0:T(8,128)(2,1)} %collective-permute-done.2), kind=kLoop, calls=%fused_computation.16 | loop fusion | bytes 262144
  36.6 4.1 %collective-permute-done.5 = bf16[2,64,512]{2,1,0:T(8,128)(2,1)S(1)} collective-permute-done((bf16[2,64,512]{2,1,0:T(8,128)(2,1)}, bf16[2,64,512]{2,1,0:T(8,128)(2,1)S(1)}, u32[]{:S(2)}, u32[]{:S(2)}) %collective-permute-start.5) | collective-permute-done | bytes 131104 | tf_op jit(solution)/shard_map/ppermute | solution.py:219
  40.7 1.6 %collective-permute-done.6 = bf16[2,64,512]{2,1,0:T(8,128)(2,1)S(1)} collective-permute-done((bf16[2,64,512]{2,1,0:T(8,128)(2,1)}, bf16[2,64,512]{2,1,0:T(8,128)(2,1)S(1)}, u32[]{:S(2)}, u32[]{:S(2)}) %collective-permute-start.6) | collective-permute-done | bytes 131104 | tf_op jit(solution)/shard_map/ppermute | solution.py:219
  42.3 10.7 %shard_map.82 = bf16[8,4,2,64,128]{4,3,2,1,0:T(8,128)(2,1)S(1)} custom-call(s32[8]{0:T(128)S(1)} %fusion.3.slot_ref, s32[8]{0:T(128)S(1)} %iota_xor_fusion.sender_ref, bf16[8,2,64,512]{3,2,1,0:T(8,128)(2,1)S(1)} %bitcast_dynamic-update-slice_fusion.7.x_ref, f32[4,2,8,64,1]{4,3,2,1,0:T(8,128)S(1)} %copy.31.t1c, f32[4,2,8,64,1]{4,3,2,1,0:T(8,128)} %copy.32.t1s, ...), custom_call_target="tpu_custom_call" | custom-call | tf_op jit(solution)/shard_map/pallas_call | solution.py:149
  53.4 1.5 %collective-permute-start.7 = (bf16[2,512,64]{1,2,0:T(8,128)(2,1)S(1)}, bf16[2,512,64]{1,2,0:T(8,128)(2,1)S(1)}, u32[]{:S(2)}, u32[]{:S(2)}) collective-permute-start(bf16[2,512,64]{1,2,0:T(8,128)(2,1)S(1)} %copy.37), channel_id=1, source_target_pairs={{0,2},{2,0},{4,6},{6,4},{8,10},{10,8},{12,14},{14,12},{1,3},{3,1},... | collective-permute-start | bytes 393224 | tf_op jit(solution)/shard_map/ppermute | solution.py:196
  56.1 2.1 %collective-permute-start.9 = (bf16[2,512,64]{1,2,0:T(8,128)(2,1)S(1)}, bf16[2,512,64]{1,2,0:T(8,128)(2,1)S(1)}, u32[]{:S(2)}, u32[]{:S(2)}) collective-permute-start(bf16[2,512,64]{1,2,0:T(8,128)(2,1)S(1)} %copy.41), channel_id=1, source_target_pairs={{0,6},{2,4},{4,2},{6,0},{8,14},{10,12},{12,10},{14,8},{1,7},{3,5},... | collective-permute-start | bytes 393224 | tf_op jit(solution)/shard_map/ppermute | solution.py:196
  58.5 1.6 %collective-permute-start.10 = (bf16[2,512,64]{1,2,0:T(8,128)(2,1)S(1)}, bf16[2,512,64]{1,2,0:T(8,128)(2,1)S(1)}, u32[]{:S(2)}, u32[]{:S(2)}) collective-permute-start(bf16[2,512,64]{1,2,0:T(8,128)(2,1)S(1)} %copy.43), channel_id=1, source_target_pairs={{0,8},{2,10},{4,12},{6,14},{8,0},{10,2},{12,4},{14,6},{1,9},{3,11}... | collective-permute-start | bytes 393224 | tf_op jit(solution)/shard_map/ppermute | solution.py:196
  60.4 2.4 %collective-permute-start.11 = (bf16[2,512,64]{1,2,0:T(8,128)(2,1)S(1)}, bf16[2,512,64]{1,2,0:T(8,128)(2,1)S(1)}, u32[]{:S(2)}, u32[]{:S(2)}) collective-permute-start(bf16[2,512,64]{1,2,0:T(8,128)(2,1)S(1)} %copy.45), channel_id=1, source_target_pairs={{0,10},{2,8},{4,14},{6,12},{8,2},{10,0},{12,6},{14,4},{1,11},{3,9}... | collective-permute-start | bytes 393224 | tf_op jit(solution)/shard_map/ppermute | solution.py:196
  63.5 1.6 %collective-permute-start.12 = (bf16[2,512,64]{1,2,0:T(8,128)(2,1)S(1)}, bf16[2,512,64]{1,2,0:T(8,128)(2,1)S(1)}, u32[]{:S(2)}, u32[]{:S(2)}) collective-permute-start(bf16[2,512,64]{1,2,0:T(8,128)(2,1)S(1)} %copy.47), channel_id=1, source_target_pairs={{0,12},{2,14},{4,8},{6,10},{8,4},{10,6},{12,0},{14,2},{1,13},{3,15... | collective-permute-start | bytes 393224 | tf_op jit(solution)/shard_map/ppermute | solution.py:196
  65.8 8.5 %collective-permute-done.10 = bf16[2,512,64]{1,2,0:T(8,128)(2,1)S(1)} collective-permute-done((bf16[2,512,64]{1,2,0:T(8,128)(2,1)S(1)}, bf16[2,512,64]{1,2,0:T(8,128)(2,1)S(1)}, u32[]{:S(2)}, u32[]{:S(2)}) %collective-permute-start.10) | collective-permute-done | bytes 131104 | tf_op jit(solution)/shard_map/ppermute | solution.py:196
  74.3 2.8 %collective-permute-done.11 = bf16[2,512,64]{1,2,0:T(8,128)(2,1)S(1)} collective-permute-done((bf16[2,512,64]{1,2,0:T(8,128)(2,1)S(1)}, bf16[2,512,64]{1,2,0:T(8,128)(2,1)S(1)}, u32[]{:S(2)}, u32[]{:S(2)}) %collective-permute-start.11) | collective-permute-done | bytes 131104 | tf_op jit(solution)/shard_map/ppermute | solution.py:196
  77.1 3.2 %collective-permute-done.12 = bf16[2,512,64]{1,2,0:T(8,128)(2,1)S(1)} collective-permute-done((bf16[2,512,64]{1,2,0:T(8,128)(2,1)S(1)}, bf16[2,512,64]{1,2,0:T(8,128)(2,1)S(1)}, u32[]{:S(2)}, u32[]{:S(2)}) %collective-permute-start.12) | collective-permute-done | bytes 131104 | tf_op jit(solution)/shard_map/ppermute | solution.py:196
  80.3 2.6 %collective-permute-done.13 = bf16[2,512,64]{1,2,0:T(8,128)(2,1)S(1)} collective-permute-done((bf16[2,512,64]{1,2,0:T(8,128)(2,1)S(1)}, bf16[2,512,64]{1,2,0:T(8,128)(2,1)S(1)}, u32[]{:S(2)}, u32[]{:S(2)}) %collective-permute-start.13) | collective-permute-done | bytes 131104 | tf_op jit(solution)/shard_map/ppermute | solution.py:196
  83.8 1.3 %copy.52 = bf16[1,1,2,512,512]{4,3,2,1,0:T(8,128)(2,1)} copy(bf16[1,1,2,512,512]{3,4,2,1,0:T(8,128)(2,1)S(1)} %bitcast.70) | data formatting | bytes 2097152 | tf_op jit(solution)/shard_map/reshape | solution.py:247
  (77 shorter events, 15.0 us)
Async XLA Ops:
  0.0 17.6 %copy-start = (s32[2,4]{1,0:T(2,128)S(1)}, s32[2,4]{1,0:T(2,128)}, u32[]{:S(2)}) copy-start(s32[2,4]{1,0:T(2,128)} %param.10) | copy-start | bytes 100
  0.0 15.1 %copy-start.2 = (f32[4,8]{1,0:T(4,128)S(1)}, f32[4,8]{1,0:T(4,128)}, u32[]{:S(2)}) copy-start(f32[4,8]{1,0:T(4,128)} %constant.107.clone) | copy-start | bytes 388
  0.0 15.9 %copy-start.1 = (f32[128]{0:T(128)S(1)}, f32[128]{0:T(128)}, u32[]{:S(2)}) copy-start(f32[128]{0:T(128)} %constant.105.clone) | copy-start | bytes 1540
  0.0 16.8 %copy-start.3 = (f32[2,8]{1,0:T(2,128)S(1)}, f32[2,8]{1,0:T(2,128)}, u32[]{:S(2)}) copy-start(f32[2,8]{1,0:T(2,128)} %constant.106.clone) | copy-start | bytes 196
  0.0 14.7 %copy-start.4 = (f32[4]{0:T(128)S(1)}, f32[4]{0:T(128)}, u32[]{:S(2)}) copy-start(f32[4]{0:T(128)} %param.9) | copy-start | bytes 52
  7.4 22.5 %collective-permute-start = (bf16[2,64,512]{2,1,0:T(8,128)(2,1)}, bf16[2,64,512]{2,1,0:T(8,128)(2,1)}, u32[]{:S(2)}, u32[]{:S(2)}) collective-permute-start(bf16[2,64,512]{2,1,0:T(8,128)(2,1)} %get-tuple-element.28), channel_id=1, source_target_pairs={{0,2},{2,0},{4,6},{6,4},{8,10},{10,8},{12,14},{14,12},{1,3},{3,1},... | collective-permute-start | bytes 393224 | tf_op jit(solution)/shard_map/ppermute | solution.py:219
  8.9 23.5 %collective-permute-start.1 = (bf16[2,64,512]{2,1,0:T(8,128)(2,1)}, bf16[2,64,512]{2,1,0:T(8,128)(2,1)}, u32[]{:S(2)}, u32[]{:S(2)}) collective-permute-start(bf16[2,64,512]{2,1,0:T(8,128)(2,1)} %get-tuple-element.27), channel_id=1, source_target_pairs={{0,4},{2,6},{4,0},{6,2},{8,12},{10,14},{12,8},{14,10},{1,5},{3,7},... | collective-permute-start | bytes 393224 | tf_op jit(solution)/shard_map/ppermute | solution.py:219
  9.3 24.5 %collective-permute-start.2 = (bf16[2,64,512]{2,1,0:T(8,128)(2,1)}, bf16[2,64,512]{2,1,0:T(8,128)(2,1)}, u32[]{:S(2)}, u32[]{:S(2)}) collective-permute-start(bf16[2,64,512]{2,1,0:T(8,128)(2,1)} %get-tuple-element.26), channel_id=1, source_target_pairs={{0,6},{2,4},{4,2},{6,0},{8,14},{10,12},{12,10},{14,8},{1,7},{3,5},... | collective-permute-start | bytes 393224 | tf_op jit(solution)/shard_map/ppermute | solution.py:219
  10.9 23.9 %collective-permute-start.3 = (bf16[2,64,512]{2,1,0:T(8,128)(2,1)}, bf16[2,64,512]{2,1,0:T(8,128)(2,1)}, u32[]{:S(2)}, u32[]{:S(2)}) collective-permute-start(bf16[2,64,512]{2,1,0:T(8,128)(2,1)} %get-tuple-element.25), channel_id=1, source_target_pairs={{0,8},{2,10},{4,12},{6,14},{8,0},{10,2},{12,4},{14,6},{1,9},{3,11}... | collective-permute-start | bytes 393224 | tf_op jit(solution)/shard_map/ppermute | solution.py:219
  13.4 22.2 %collective-permute-start.4 = (bf16[2,64,512]{2,1,0:T(8,128)(2,1)}, bf16[2,64,512]{2,1,0:T(8,128)(2,1)}, u32[]{:S(2)}, u32[]{:S(2)}) collective-permute-start(bf16[2,64,512]{2,1,0:T(8,128)(2,1)} %get-tuple-element.24), channel_id=1, source_target_pairs={{0,10},{2,8},{4,14},{6,12},{8,2},{10,0},{12,6},{14,4},{1,11},{3,9}... | collective-permute-start | bytes 393224 | tf_op jit(solution)/shard_map/ppermute | solution.py:219
  29.9 10.8 %collective-permute-start.5 = (bf16[2,64,512]{2,1,0:T(8,128)(2,1)}, bf16[2,64,512]{2,1,0:T(8,128)(2,1)S(1)}, u32[]{:S(2)}, u32[]{:S(2)}) collective-permute-start(bf16[2,64,512]{2,1,0:T(8,128)(2,1)} %get-tuple-element.30), channel_id=1, source_target_pairs={{0,12},{2,14},{4,8},{6,10},{8,4},{10,6},{12,0},{14,2},{1,13},{3,15... | collective-permute-start | bytes 393224 | tf_op jit(solution)/shard_map/ppermute | solution.py:219
  32.4 9.9 %collective-permute-start.6 = (bf16[2,64,512]{2,1,0:T(8,128)(2,1)}, bf16[2,64,512]{2,1,0:T(8,128)(2,1)S(1)}, u32[]{:S(2)}, u32[]{:S(2)}) collective-permute-start(bf16[2,64,512]{2,1,0:T(8,128)(2,1)} %get-tuple-element.23), channel_id=1, source_target_pairs={{0,14},{2,12},{4,10},{6,8},{8,6},{10,4},{12,2},{14,0},{1,15},{3,13... | collective-permute-start | bytes 393224 | tf_op jit(solution)/shard_map/ppermute | solution.py:219
  53.4 10.1 %collective-permute-start.7 = (bf16[2,512,64]{1,2,0:T(8,128)(2,1)S(1)}, bf16[2,512,64]{1,2,0:T(8,128)(2,1)S(1)}, u32[]{:S(2)}, u32[]{:S(2)}) collective-permute-start(bf16[2,512,64]{1,2,0:T(8,128)(2,1)S(1)} %copy.37), channel_id=1, source_target_pairs={{0,2},{2,0},{4,6},{6,4},{8,10},{10,8},{12,14},{14,12},{1,3},{3,1},... | collective-permute-start | bytes 393224 | tf_op jit(solution)/shard_map/ppermute | solution.py:196
  55.7 9.5 %collective-permute-start.8 = (bf16[2,512,64]{1,2,0:T(8,128)(2,1)S(1)}, bf16[2,512,64]{1,2,0:T(8,128)(2,1)S(1)}, u32[]{:S(2)}, u32[]{:S(2)}) collective-permute-start(bf16[2,512,64]{1,2,0:T(8,128)(2,1)S(1)} %copy.39), channel_id=1, source_target_pairs={{0,4},{2,6},{4,0},{6,2},{8,12},{10,14},{12,8},{14,10},{1,5},{3,7},... | collective-permute-start | bytes 393224 | tf_op jit(solution)/shard_map/ppermute | solution.py:196
  56.1 9.7 %collective-permute-start.9 = (bf16[2,512,64]{1,2,0:T(8,128)(2,1)S(1)}, bf16[2,512,64]{1,2,0:T(8,128)(2,1)S(1)}, u32[]{:S(2)}, u32[]{:S(2)}) collective-permute-start(bf16[2,512,64]{1,2,0:T(8,128)(2,1)S(1)} %copy.41), channel_id=1, source_target_pairs={{0,6},{2,4},{4,2},{6,0},{8,14},{10,12},{12,10},{14,8},{1,7},{3,5},... | collective-permute-start | bytes 393224 | tf_op jit(solution)/shard_map/ppermute | solution.py:196
  58.5 15.8 %collective-permute-start.10 = (bf16[2,512,64]{1,2,0:T(8,128)(2,1)S(1)}, bf16[2,512,64]{1,2,0:T(8,128)(2,1)S(1)}, u32[]{:S(2)}, u32[]{:S(2)}) collective-permute-start(bf16[2,512,64]{1,2,0:T(8,128)(2,1)S(1)} %copy.43), channel_id=1, source_target_pairs={{0,8},{2,10},{4,12},{6,14},{8,0},{10,2},{12,4},{14,6},{1,9},{3,11}... | collective-permute-start | bytes 393224 | tf_op jit(solution)/shard_map/ppermute | solution.py:196
  60.4 16.7 %collective-permute-start.11 = (bf16[2,512,64]{1,2,0:T(8,128)(2,1)S(1)}, bf16[2,512,64]{1,2,0:T(8,128)(2,1)S(1)}, u32[]{:S(2)}, u32[]{:S(2)}) collective-permute-start(bf16[2,512,64]{1,2,0:T(8,128)(2,1)S(1)} %copy.45), channel_id=1, source_target_pairs={{0,10},{2,8},{4,14},{6,12},{8,2},{10,0},{12,6},{14,4},{1,11},{3,9}... | collective-permute-start | bytes 393224 | tf_op jit(solution)/shard_map/ppermute | solution.py:196
  63.5 16.8 %collective-permute-start.12 = (bf16[2,512,64]{1,2,0:T(8,128)(2,1)S(1)}, bf16[2,512,64]{1,2,0:T(8,128)(2,1)S(1)}, u32[]{:S(2)}, u32[]{:S(2)}) collective-permute-start(bf16[2,512,64]{1,2,0:T(8,128)(2,1)S(1)} %copy.47), channel_id=1, source_target_pairs={{0,12},{2,14},{4,8},{6,10},{8,4},{10,6},{12,0},{14,2},{1,13},{3,15... | collective-permute-start | bytes 393224 | tf_op jit(solution)/shard_map/ppermute | solution.py:196
  65.2 17.7 %collective-permute-start.13 = (bf16[2,512,64]{1,2,0:T(8,128)(2,1)S(1)}, bf16[2,512,64]{1,2,0:T(8,128)(2,1)S(1)}, u32[]{:S(2)}, u32[]{:S(2)}) collective-permute-start(bf16[2,512,64]{1,2,0:T(8,128)(2,1)S(1)} %copy.49), channel_id=1, source_target_pairs={{0,14},{2,12},{4,10},{6,8},{8,6},{10,4},{12,2},{14,0},{1,15},{3,13... | collective-permute-start | bytes 393224 | tf_op jit(solution)/shard_map/ppermute | solution.py:196

commit v10 on v8

--- a/solution.py
+++ b/solution.py
@@ -184,14 +184,21 @@
             jnp.cos(rough_two), jnp.sin(rough_two), jnp.cos(small_two), jnp.sin(small_two))
 
 
-def swap_ordered(ordered, place, axes):
+def flip_order(count, beam_count):
+    rest = sorted(range(1, count), key=lambda f: (-(f // beam_count), f))
+    return np.array([0] + rest, dtype=np.int32)
+
+
+def swap_ordered(ordered, place, axes, order):
     count = ordered.shape[0]
     moved = [ordered[0]]
-    for flip in range(1, count):
+    for at in range(1, count):
+        flip = int(order[at])
         pairs = [(i, i ^ flip) for i in range(count)]
-        moved.append(lax.ppermute(ordered[flip], axes, pairs))
-    flips = jnp.bitwise_xor(place, jnp.arange(count, dtype=jnp.int32))
-    return jnp.take(jnp.stack(moved), flips, axis=0)
+        moved.append(lax.ppermute(ordered[at], axes, pairs))
+    position = jnp.asarray(np.argsort(order).astype(np.int32))
+    senders = position[jnp.bitwise_xor(place, jnp.arange(count, dtype=jnp.int32))]
+    return jnp.take(jnp.stack(moved), senders, axis=0)
 
 
 def body(images, offsets, owners):
@@ -219,7 +226,9 @@
         shard_of = jnp.arange(blocks, dtype=jnp.int32) // sub_count
         sector_of = jnp.arange(blocks, dtype=jnp.int32) % sub_count
         holder = jnp.argmax(owners[shard_of] == sector_of[:, None], axis=1).astype(jnp.int32)
-        slots = jnp.bitwise_xor(member_at, holder * beam_count + shard_of)
+        sequence = flip_order(members, beam_count)
+        position = jnp.asarray(np.argsort(sequence).astype(np.int32))
+        slots = position[jnp.bitwise_xor(member_at, holder * beam_count + shard_of)]
     else:
         slots = jnp.arange(blocks, dtype=jnp.int32)
     merged = merge_call(
@@ -231,7 +240,7 @@
     )
     if direct:
         ordered = merged.transpose(0, 2, 4, 1, 3).reshape(blocks, 2, sector_width, own_rows)
-        received = swap_ordered(ordered, member_at, ("sub4", "beam"))
+        received = swap_ordered(ordered, member_at, ("sub4", "beam"), sequence)
         received = received.transpose(1, 2, 0, 3)
         return received.reshape(1, 1, 2, sector_width, members * own_rows)
     merged = merged.transpose(1, 2, 3, 0, 4).reshape(4, 2, own_rows, B)

time: 76.1 us -> 74.3 us (0.976)
  the two profiles are of different devices: /device:TPU:12 before, /device:TPU:0 now
where the time goes in v10:
time: 74.3 us; the launch traced here: 74.1 us
  starting transfers between devices  23.4 us (31%)
  other arithmetic  19.6 us (26%)
  waiting for transfers between devices  11.4 us (15%)
  Pallas kernels  10.2 us (14%)
  local copies, waits for them, and re-layouts  9.11 us (12%)
    ppermute x7, starting transfers between devices, swap_ordered(): moved.append(lax.ppermute(ordered[at], axes, pairs))  16 us
    pallas_call x1, Pallas kernels, merge_call(): pl.pallas_call(merge_kernel, out_shape=jax.ShapeDtypeStruct((width // LAN...  10.2 us
    sin x1, other arithmetic, merge_tables(): jnp.sin(rough_two)  8.59 us
    sin x1, other arithmetic, merge_tables(): jnp.sin(rough_one)  8.42 us
    all_to_all x1, starting transfers between devices, body(): gathered = lax.all_to_all(pieces, ('sub4', 'beam'), 0, 0, tiled=True)  7.41 us
    ppermute x7, waiting for transfers between devices, swap_ordered(): moved.append(lax.ppermute(ordered[at], axes, pairs))  7.2 us
    all_to_all x1, waiting for transfers between devices, body(): gathered = lax.all_to_all(pieces, ('sub4', 'beam'), 0, 0, tiled=True)  4.21 us
    another operation x1, local copies, waits for them, and re-layouts, body(): images[0].reshape(2, members, own_rows, local_beams).transpose(1, 0, 2, 3)  2.31 us
  transfers between devices with their start and end apart: 8, of which 5 were waited for; matrix products, arithmetic and copies ran while one was open for 32% of the time, Pallas kernels for 0%

profile of v10, /device:TPU:0, one launch (start us, length us, event | category | flops | bytes accessed | tf_op | source)
XLA Modules:
  0.0 74.1 jit_solution(3149138622058226477)
XLA Ops:
  0.0 2.3 %copy.31 = bf16[2,8,64,512]{3,2,0,1:T(8,128)(2,1)} copy(bf16[2,8,64,512]{3,2,1,0:T(8,128)(2,1)} %bitcast.48) | data formatting | bytes 2097152 | tf_op jit(solution)/shard_map/reshape;squeeze | solution.py:216
  2.3 7.4 %all-to-all-start = ((bf16[8,2,64,512]{3,2,1,0:T(8,128)(2,1)}), bf16[8,2,64,512]{3,2,1,0:T(8,128)(2,1)S(1)}, u32[]{:S(2)}, u32[]{:S(2)}) async-start(bf16[8,2,64,512]{3,2,1,0:T(8,128)(2,1)} %bitcast.37), calls=%async_computation | async-start | bytes 2097152 | tf_op jit(solution)/shard_map/all_to_all | solution.py:217
  9.8 0.6 gather_fusion
  10.4 0.6 fusion.3
  11.1 0.6 gather_fusion.1
  11.6 0.8 %iota_reduce_fusion = (pred[8]{0:T(512)(128)(4,1)}, s32[8]{0:T(128)S(1)}) fusion(s32[8,4]{1,0:T(8,128)S(1)} %gather_fusion.1, s32[8]{0:T(128)S(1)} %and_select_fusion.1), kind=kLoop, calls=%fused_computation.26 | loop fusion | flops 200 | bytes 200 | tf_op jit(solution)/shard_map/body/reduce | solution.py:228
  12.6 0.6 gather_fusion.2
  13.4 0.3 multiply_sine_fusion.3
  13.7 0.5 multiply_sine_fusion.2
  14.3 8.4 %multiply_sine_fusion.1 = (f32[4,2,8,64,1]{4,3,2,1,0:T(8,128)}, f32[4,2,8,64,1]{4,3,2,1,0:T(8,128)S(1)}) fusion(f32[2,8]{1,0:T(2,128)S(1)} %copy-done.4, f32[4,64]{1,0:T(4,128)S(1)} %broadcast_multiply_fusion), kind=kLoop, calls=%fused_computation.6 | loop fusion | flops 4096 | bytes 33856 | tf_op jit(solution)/shard_map/sin | solution.py:183
  22.7 8.6 %multiply_sine_fusion = (f32[2,4,8,64,1]{4,3,2,1,0:T(8,128)}, f32[2,4,8,64,1]{4,3,2,1,0:T(8,128)}) fusion(f32[4,8]{1,0:T(4,128)S(1)} %copy-done.2, f32[2,64]{1,0:T(2,128)S(1)} %broadcast_multiply_fusion.1), kind=kLoop, calls=%fused_computation.4 | loop fusion | flops 4096 | bytes 33408 | tf_op jit(solution)/shard_map/sin | solution.py:184
  31.3 4.2 %all-to-all-done.x_ref = bf16[8,2,64,512]{3,2,1,0:T(8,128)(2,1)S(1)} async-done(((bf16[8,2,64,512]{3,2,1,0:T(8,128)(2,1)}), bf16[8,2,64,512]{3,2,1,0:T(8,128)(2,1)S(1)}, u32[]{:S(2)}, u32[]{:S(2)}) %all-to-all-start) | async-done | bytes 1048608 | tf_op jit(solution)/shard_map/all_to_all | solution.py:217
  35.5 10.2 %shard_map.100 = bf16[8,4,2,64,128]{4,3,2,1,0:T(8,128)(2,1)S(1)} custom-call(s32[8]{0:T(128)S(1)} %gather_fusion.2, bf16[8,2,64,512]{3,2,1,0:T(8,128)(2,1)S(1)} %all-to-all-done.x_ref, f32[4,2,8,64,1]{4,3,2,1,0:T(8,128)S(1)} %get-tuple-element.18.t1c, f32[4,2,8,64,1]{4,3,2,1,0:T(8,128)} %get-tuple-element.17.t1s, f32[4,64,128]{2,1,0:T(8,128)S(1)} %get-tuple-element.20.f1c, ...), custom_call_target="tpu_custom_call" | custom-call | tf_op jit(solution)/shard_map/pallas_call | solution.py:149
  46.1 1.2 %collective-permute-start = (bf16[2,512,64]{1,2,0:T(8,128)(2,1)S(1)}, bf16[2,512,64]{1,2,0:T(8,128)(2,1)S(1)}, u32[]{:S(2)}, u32[]{:S(2)}) collective-permute-start(bf16[2,512,64]{1,2,0:T(8,128)(2,1)S(1)} %copy.14), channel_id=1, source_target_pairs={{0,12},{2,14},{4,8},{6,10},{8,4},{10,6},{12,0},{14,2},{1,13},{3,15... | collective-permute-start | bytes 393224 | tf_op jit(solution)/shard_map/ppermute | solution.py:198
  48.0 3.6 %collective-permute-start.1 = (bf16[2,512,64]{1,2,0:T(8,128)(2,1)S(1)}, bf16[2,512,64]{1,2,0:T(8,128)(2,1)S(1)}, u32[]{:S(2)}, u32[]{:S(2)}) collective-permute-start(bf16[2,512,64]{1,2,0:T(8,128)(2,1)S(1)} %copy.16), channel_id=1, source_target_pairs={{0,14},{2,12},{4,10},{6,8},{8,6},{10,4},{12,2},{14,0},{1,15},{3,13... | collective-permute-start | bytes 393224 | tf_op jit(solution)/shard_map/ppermute | solution.py:198
  52.4 3.0 %collective-permute-start.3 = (bf16[2,512,64]{1,2,0:T(8,128)(2,1)S(1)}, bf16[2,512,64]{1,2,0:T(8,128)(2,1)S(1)}, u32[]{:S(2)}, u32[]{:S(2)}) collective-permute-start(bf16[2,512,64]{1,2,0:T(8,128)(2,1)S(1)} %copy.20), channel_id=1, source_target_pairs={{0,10},{2,8},{4,14},{6,12},{8,2},{10,0},{12,6},{14,4},{1,11},{3,9}... | collective-permute-start | bytes 393224 | tf_op jit(solution)/shard_map/ppermute | solution.py:198
  56.5 6.8 %collective-permute-start.5 = (bf16[2,512,64]{1,2,0:T(8,128)(2,1)S(1)}, bf16[2,512,64]{1,2,0:T(8,128)(2,1)S(1)}, u32[]{:S(2)}, u32[]{:S(2)}) collective-permute-start(bf16[2,512,64]{1,2,0:T(8,128)(2,1)S(1)} %copy.24), channel_id=1, source_target_pairs={{0,6},{2,4},{4,2},{6,0},{8,14},{10,12},{12,10},{14,8},{1,7},{3,5},... | collective-permute-start | bytes 393224 | tf_op jit(solution)/shard_map/ppermute | solution.py:198
  63.3 1.3 %collective-permute-start.6 = (bf16[2,512,64]{1,2,0:T(8,128)(2,1)S(1)}, bf16[2,512,64]{1,2,0:T(8,128)(2,1)S(1)}, u32[]{:S(2)}, u32[]{:S(2)}) collective-permute-start(bf16[2,512,64]{1,2,0:T(8,128)(2,1)S(1)} %copy.26), channel_id=1, source_target_pairs={{0,2},{2,0},{4,6},{6,4},{8,10},{10,8},{12,14},{14,12},{1,3},{3,1},... | collective-permute-start | bytes 393224 | tf_op jit(solution)/shard_map/ppermute | solution.py:198
  64.6 3.9 %collective-permute-done.2 = bf16[2,512,64]{1,2,0:T(8,128)(2,1)S(1)} collective-permute-done((bf16[2,512,64]{1,2,0:T(8,128)(2,1)S(1)}, bf16[2,512,64]{1,2,0:T(8,128)(2,1)S(1)}, u32[]{:S(2)}, u32[]{:S(2)}) %collective-permute-start.2) | collective-permute-done | bytes 131104 | tf_op jit(solution)/shard_map/ppermute | solution.py:198
  68.5 2.0 %collective-permute-done.3 = bf16[2,512,64]{1,2,0:T(8,128)(2,1)S(1)} collective-permute-done((bf16[2,512,64]{1,2,0:T(8,128)(2,1)S(1)}, bf16[2,512,64]{1,2,0:T(8,128)(2,1)S(1)}, u32[]{:S(2)}, u32[]{:S(2)}) %collective-permute-start.3) | collective-permute-done | bytes 131104 | tf_op jit(solution)/shard_map/ppermute | solution.py:198
  70.5 0.8 %collective-permute-done.5 = bf16[2,512,64]{1,2,0:T(8,128)(2,1)S(1)} collective-permute-done((bf16[2,512,64]{1,2,0:T(8,128)(2,1)S(1)}, bf16[2,512,64]{1,2,0:T(8,128)(2,1)S(1)}, u32[]{:S(2)}, u32[]{:S(2)}) %collective-permute-start.5) | collective-permute-done | bytes 131104 | tf_op jit(solution)/shard_map/ppermute | solution.py:198
  71.4 0.5 collective-permute-done.6
  71.9 0.6 gather_fusion.3
  72.7 1.3 %copy.29 = bf16[1,1,2,512,512]{4,3,2,1,0:T(8,128)(2,1)} copy(bf16[1,1,2,512,512]{3,4,2,1,0:T(8,128)(2,1)S(1)} %bitcast.39) | data formatting | bytes 2097152 | tf_op jit(solution)/shard_map/reshape | solution.py:245
  (60 shorter events, 3.5 us)
Async XLA Ops:
  0.0 11.0 %copy-start = (s32[2,4]{1,0:T(2,128)S(1)}, s32[2,4]{1,0:T(2,128)}, u32[]{:S(2)}) copy-start(s32[2,4]{1,0:T(2,128)} %param.12) | copy-start | bytes 100
  0.0 9.8 %copy-start.1 = (s32[8]{0:T(128)S(1)}, s32[8]{0:T(128)}, u32[]{:S(2)}) copy-start(s32[8]{0:T(128)} %constant.92.clone) | copy-start | bytes 100
  0.0 12.4 %copy-start.6 = (f32[4]{0:T(128)S(1)}, f32[4]{0:T(128)}, u32[]{:S(2)}) copy-start(f32[4]{0:T(128)} %param.11) | copy-start | bytes 52
  2.3 11.1 %copy-start.3 = (f32[128]{0:T(128)S(1)}, f32[128]{0:T(128)}, u32[]{:S(2)}) copy-start(f32[128]{0:T(128)} %constant.93.clone) | copy-start | bytes 1540
  2.3 11.9 %copy-start.4 = (f32[2,8]{1,0:T(2,128)S(1)}, f32[2,8]{1,0:T(2,128)}, u32[]{:S(2)}) copy-start(f32[2,8]{1,0:T(2,128)} %constant.94.clone) | copy-start | bytes 196
  2.3 33.2 %all-to-all-start = ((bf16[8,2,64,512]{3,2,1,0:T(8,128)(2,1)}), bf16[8,2,64,512]{3,2,1,0:T(8,128)(2,1)S(1)}, u32[]{:S(2)}, u32[]{:S(2)}) async-start(bf16[8,2,64,512]{3,2,1,0:T(8,128)(2,1)} %bitcast.37), calls=%async_computation | async-start | bytes 2097152 | tf_op jit(solution)/shard_map/all_to_all | solution.py:217
  14.3 8.4 %copy-start.2 = (f32[4,8]{1,0:T(4,128)S(1)}, f32[4,8]{1,0:T(4,128)}, u32[]{:S(2)}) copy-start(f32[4,8]{1,0:T(4,128)} %constant.95.clone) | copy-start | bytes 388
  45.7 1.7 %copy-start.5 = (s32[8]{0:T(128)S(1)}, s32[8]{0:T(128)}, u32[]{:S(2)}) copy-start(s32[8]{0:T(128)} %fusion.3) | copy-start | bytes 100
  46.1 10.4 %collective-permute-start = (bf16[2,512,64]{1,2,0:T(8,128)(2,1)S(1)}, bf16[2,512,64]{1,2,0:T(8,128)(2,1)S(1)}, u32[]{:S(2)}, u32[]{:S(2)}) collective-permute-start(bf16[2,512,64]{1,2,0:T(8,128)(2,1)S(1)} %copy.14), channel_id=1, source_target_pairs={{0,12},{2,14},{4,8},{6,10},{8,4},{10,6},{12,0},{14,2},{1,13},{3,15... | collective-permute-start | bytes 393224 | tf_op jit(solution)/shard_map/ppermute | solution.py:198
  48.0 15.2 %collective-permute-start.1 = (bf16[2,512,64]{1,2,0:T(8,128)(2,1)S(1)}, bf16[2,512,64]{1,2,0:T(8,128)(2,1)S(1)}, u32[]{:S(2)}, u32[]{:S(2)}) collective-permute-start(bf16[2,512,64]{1,2,0:T(8,128)(2,1)S(1)} %copy.16), channel_id=1, source_target_pairs={{0,14},{2,12},{4,10},{6,8},{8,6},{10,4},{12,2},{14,0},{1,15},{3,13... | collective-permute-start | bytes 393224 | tf_op jit(solution)/shard_map/ppermute | solution.py:198
  52.0 16.5 %collective-permute-start.2 = (bf16[2,512,64]{1,2,0:T(8,128)(2,1)S(1)}, bf16[2,512,64]{1,2,0:T(8,128)(2,1)S(1)}, u32[]{:S(2)}, u32[]{:S(2)}) collective-permute-start(bf16[2,512,64]{1,2,0:T(8,128)(2,1)S(1)} %copy.18), channel_id=1, source_target_pairs={{0,8},{2,10},{4,12},{6,14},{8,0},{10,2},{12,4},{14,6},{1,9},{3,11}... | collective-permute-start | bytes 393224 | tf_op jit(solution)/shard_map/ppermute | solution.py:198
  52.4 18.1 %collective-permute-start.3 = (bf16[2,512,64]{1,2,0:T(8,128)(2,1)S(1)}, bf16[2,512,64]{1,2,0:T(8,128)(2,1)S(1)}, u32[]{:S(2)}, u32[]{:S(2)}) collective-permute-start(bf16[2,512,64]{1,2,0:T(8,128)(2,1)S(1)} %copy.20), channel_id=1, source_target_pairs={{0,10},{2,8},{4,14},{6,12},{8,2},{10,0},{12,6},{14,4},{1,11},{3,9}... | collective-permute-start | bytes 393224 | tf_op jit(solution)/shard_map/ppermute | solution.py:198
  55.7 14.8 %collective-permute-start.4 = (bf16[2,512,64]{1,2,0:T(8,128)(2,1)S(1)}, bf16[2,512,64]{1,2,0:T(8,128)(2,1)S(1)}, u32[]{:S(2)}, u32[]{:S(2)}) collective-permute-start(bf16[2,512,64]{1,2,0:T(8,128)(2,1)S(1)} %copy.22), channel_id=1, source_target_pairs={{0,4},{2,6},{4,0},{6,2},{8,12},{10,14},{12,8},{14,10},{1,5},{3,7},... | collective-permute-start | bytes 393224 | tf_op jit(solution)/shard_map/ppermute | solution.py:198
  56.5 14.9 %collective-permute-start.5 = (bf16[2,512,64]{1,2,0:T(8,128)(2,1)S(1)}, bf16[2,512,64]{1,2,0:T(8,128)(2,1)S(1)}, u32[]{:S(2)}, u32[]{:S(2)}) collective-permute-start(bf16[2,512,64]{1,2,0:T(8,128)(2,1)S(1)} %copy.24), channel_id=1, source_target_pairs={{0,6},{2,4},{4,2},{6,0},{8,14},{10,12},{12,10},{14,8},{1,7},{3,5},... | collective-permute-start | bytes 393224 | tf_op jit(solution)/shard_map/ppermute | solution.py:198
  63.3 8.6 %collective-permute-start.6 = (bf16[2,512,64]{1,2,0:T(8,128)(2,1)S(1)}, bf16[2,512,64]{1,2,0:T(8,128)(2,1)S(1)}, u32[]{:S(2)}, u32[]{:S(2)}) collective-permute-start(bf16[2,512,64]{1,2,0:T(8,128)(2,1)S(1)} %copy.26), channel_id=1, source_target_pairs={{0,2},{2,0},{4,6},{6,4},{8,10},{10,8},{12,14},{14,12},{1,3},{3,1},... | collective-permute-start | bytes 393224 | tf_op jit(solution)/shard_map/ppermute | solution.py:198

commit v11 on v10

--- a/solution.py
+++ b/solution.py
@@ -59,6 +59,33 @@
 
 
 LANES = 128
+
+
+TILE = 256
+
+
+def toeplitz_tiles(matrix):
+    count = matrix.shape[0] // TILE
+    tiles = []
+    for gap in range(-(count - 1), count):
+        i = max(0, -gap)
+        j = i + gap
+        tiles.append(matrix[i * TILE:(i + 1) * TILE, j * TILE:(j + 1) * TILE])
+    tiles = np.stack(tiles)
+    for i in range(count):
+        for j in range(count):
+            assert np.array_equal(matrix[i * TILE:(i + 1) * TILE, j * TILE:(j + 1) * TILE], tiles[j - i + count - 1])
+    return tiles
+
+
+def kernel_tables(width):
+    one = toeplitz_tiles(odd_values(width))
+    order = split_order(2 * width)
+    two = odd_values(2 * width)[order][:, order]
+    assert np.array_equal(two[:width, :width], two[width:, width:])
+    quads = np.stack([toeplitz_tiles(two[:width, :width]), toeplitz_tiles(two[:width, width:]),
+                      toeplitz_tiles(two[width:, :width])])
+    return jnp.asarray(one), jnp.asarray(quads)
 
 
 def merge_kernel(slot_ref, x_ref, t1c, t1s, f1c, f1s, t2c, t2s, f2c, f2s, k1_hbm, k2_hbm, o_ref,
@@ -95,13 +122,20 @@
             first_v[pair, pl.ds(rows, rows), out_cols] = im_sum.astype(first_v.dtype)
 
     load_one.wait()
+    count = half // TILE
+    per_piece = local // TILE
     for s in range(4):
-        total = None
-        for b in range(beam_count):
-            part = x_ref[s * beam_count + b].reshape(2 * rows, local)
-            term = jnp.dot(part, k1_v[pl.ds(b * local, local), :], preferred_element_type=jnp.float32)
-            total = term if total is None else total + term
-        odd1_v[s] = total
+        parts = []
+        for i in range(count):
+            b, k = divmod(i, per_piece)
+            piece = x_ref[s * beam_count + b, :, :, pl.ds(k * TILE, TILE)]
+            parts.append(piece.reshape(2 * rows, TILE))
+        for j in range(count):
+            total = None
+            for i in range(count):
+                term = jnp.dot(parts[i], k1_v[j - i + count - 1], preferred_element_type=jnp.float32)
+                total = term if total is None else total + term
+            odd1_v[s, :, pl.ds(j * TILE, TILE)] = total
 
     for pair in range(2):
         for u in range(wide):
@@ -119,7 +153,21 @@
 
     load_two.wait()
     for pair in range(2):
-        odd2_v[pair] = jnp.dot(first_v[pair], k2_v[...], preferred_element_type=jnp.float32)
+        evens = [first_v[pair, :, pl.ds(i * TILE, TILE)] for i in range(count)]
+        odds = [first_v[pair, :, pl.ds(half + i * TILE, TILE)] for i in range(count)]
+        for j in range(count):
+            even_out = None
+            odd_out = None
+            for i in range(count):
+                gap = j - i + count - 1
+                term_e = jnp.dot(evens[i], k2_v[0, gap], preferred_element_type=jnp.float32)
+                term_e += jnp.dot(odds[i], k2_v[2, gap], preferred_element_type=jnp.float32)
+                term_o = jnp.dot(evens[i], k2_v[1, gap], preferred_element_type=jnp.float32)
+                term_o += jnp.dot(odds[i], k2_v[0, gap], preferred_element_type=jnp.float32)
+                even_out = term_e if even_out is None else even_out + term_e
+                odd_out = term_o if odd_out is None else odd_out + term_o
+            odd2_v[pair, :, pl.ds(j * TILE, TILE)] = even_out
+            odd2_v[pair, :, pl.ds(half + j * TILE, TILE)] = odd_out
 
     for t in range(4):
         for u in range(wide):
@@ -142,7 +190,7 @@
 
 def merge_call(slots, x, tables, k1, k2, interpret=False):
     members, _, rows, local = x.shape
-    width = k1.shape[0]
+    width = local * members // 4
     vmem = pl.BlockSpec(memory_space=pltpu.VMEM)
     hbm = pl.BlockSpec(memory_space=pl.ANY)
     smem = pl.BlockSpec(memory_space=pltpu.SMEM)
@@ -152,8 +200,8 @@
         in_specs=[smem] + [vmem] * 9 + [hbm, hbm],
         out_specs=vmem,
         scratch_shapes=[
-            pltpu.VMEM((width, width), jnp.bfloat16),
-            pltpu.VMEM((2 * width, 2 * width), jnp.bfloat16),
+            pltpu.VMEM(k1.shape, jnp.bfloat16),
+            pltpu.VMEM(k2.shape, jnp.bfloat16),
             pltpu.VMEM((2, 2 * rows, 2 * width), jnp.bfloat16),
             pltpu.VMEM((4, 2 * rows, width), jnp.float32),
             pltpu.VMEM((2, 2 * rows, 2 * width), jnp.float32),
@@ -235,8 +283,7 @@
         slots,
         gathered,
         merge_tables(shifts, ratios, B),
-        jnp.asarray(odd_values(B)),
-        jnp.asarray(odd_values(2 * B)[order][:, order]),
+        *kernel_tables(B),
     )
     if direct:
         ordered = merged.transpose(0, 2, 4, 1, 3).reshape(blocks, 2, sector_width, own_rows)

time: 74.3 us -> 74.3 us (level)
  Pallas kernels: 10.2 us -> 8.9 us
  local copies, waits for them, and re-layouts: 9.11 us -> 10.3 us
    pallas_call x1, Pallas kernels: 10.2 us -> 8.9 us  [merge_call(): pl.pallas_call(merge_kernel, out_shape=jax.ShapeDtypeStruct((width // LAN...]
    unnamed x21 -> x23, local copies, waits for them, and re-layouts: 0.1 us -> 1.28 us
where the time goes in v11:
time: 74.3 us; the launch traced here: 74.1 us
  starting transfers between devices  23.4 us (31%)
  other arithmetic  19.5 us (26%)
  waiting for transfers between devices  11.5 us (15%)
  local copies, waits for them, and re-layouts  10.3 us (14%)
  Pallas kernels  8.9 us (12%)
    ppermute x7, starting transfers between devices, swap_ordered(): moved.append(lax.ppermute(ordered[at], axes, pairs))  16 us
    pallas_call x1, Pallas kernels, merge_call(): pl.pallas_call(merge_kernel, out_shape=jax.ShapeDtypeStruct((width // LAN...  8.9 us
    sin x1, other arithmetic, merge_tables(): jnp.sin(rough_two)  8.6 us
    sin x1, other arithmetic, merge_tables(): jnp.sin(rough_one)  8.42 us
    all_to_all x1, starting transfers between devices, body(): gathered = lax.all_to_all(pieces, ('sub4', 'beam'), 0, 0, tiled=True)  7.41 us
    ppermute x7, waiting for transfers between devices, swap_ordered(): moved.append(lax.ppermute(ordered[at], axes, pairs))  7.29 us
    all_to_all x1, waiting for transfers between devices, body(): gathered = lax.all_to_all(pieces, ('sub4', 'beam'), 0, 0, tiled=True)  4.24 us
    another operation x1, local copies, waits for them, and re-layouts, body(): images[0].reshape(2, members, own_rows, local_beams).transpose(1, 0, 2, 3)  2.31 us
  transfers between devices with their start and end apart: 8, of which 5 were waited for; matrix products, arithmetic and copies ran while one was open for 32% of the time, Pallas kernels for 0%

profile of v11, /device:TPU:0, one launch (start us, length us, event | category | flops | bytes accessed | tf_op | source)
XLA Modules:
  0.0 74.1 jit_solution(1358941639885231934)
XLA Ops:
  0.0 2.3 %copy.31 = bf16[2,8,64,512]{3,2,0,1:T(8,128)(2,1)} copy(bf16[2,8,64,512]{3,2,1,0:T(8,128)(2,1)} %bitcast.48) | data formatting | bytes 2097152 | tf_op jit(solution)/shard_map/reshape;squeeze | solution.py:264
  2.3 7.4 %all-to-all-start = ((bf16[8,2,64,512]{3,2,1,0:T(8,128)(2,1)}), bf16[8,2,64,512]{3,2,1,0:T(8,128)(2,1)S(1)}, u32[]{:S(2)}, u32[]{:S(2)}) async-start(bf16[8,2,64,512]{3,2,1,0:T(8,128)(2,1)} %bitcast.37), calls=%async_computation | async-start | bytes 2097152 | tf_op jit(solution)/shard_map/all_to_all | solution.py:265
  9.8 0.6 gather_fusion
  10.4 0.6 fusion.3
  11.0 0.6 gather_fusion.1
  11.6 0.7 iota_reduce_fusion
  12.6 0.6 gather_fusion.2
  13.7 0.5 multiply_sine_fusion.2
  14.2 8.4 %multiply_sine_fusion.1 = (f32[4,2,8,64,1]{4,3,2,1,0:T(8,128)}, f32[4,2,8,64,1]{4,3,2,1,0:T(8,128)S(1)}) fusion(f32[2,8]{1,0:T(2,128)S(1)} %copy-done.5, f32[4,64]{1,0:T(4,128)S(1)} %broadcast_multiply_fusion), kind=kLoop, calls=%fused_computation.6 | loop fusion | flops 4096 | bytes 33856 | tf_op jit(solution)/shard_map/sin | solution.py:231
  22.7 8.6 %multiply_sine_fusion = (f32[2,4,8,64,1]{4,3,2,1,0:T(8,128)}, f32[2,4,8,64,1]{4,3,2,1,0:T(8,128)}) fusion(f32[4,8]{1,0:T(4,128)S(1)} %copy-done.3, f32[2,64]{1,0:T(2,128)S(1)} %broadcast_multiply_fusion.1), kind=kLoop, calls=%fused_computation.4 | loop fusion | flops 4096 | bytes 33408 | tf_op jit(solution)/shard_map/sin | solution.py:232
  31.3 4.2 %all-to-all-done.x_ref = bf16[8,2,64,512]{3,2,1,0:T(8,128)(2,1)S(1)} async-done(((bf16[8,2,64,512]{3,2,1,0:T(8,128)(2,1)}), bf16[8,2,64,512]{3,2,1,0:T(8,128)(2,1)S(1)}, u32[]{:S(2)}, u32[]{:S(2)}) %all-to-all-start) | async-done | bytes 1048608 | tf_op jit(solution)/shard_map/all_to_all | solution.py:265
  35.5 1.2 %copy-done.1 = bf16[7,256,256]{2,1,0:T(8,128)(2,1)S(1)} copy-done((bf16[7,256,256]{2,1,0:T(8,128)(2,1)S(1)}, bf16[7,256,256]{2,1,0:T(8,128)(2,1)}, u32[]{:S(2)}) %copy-start.1) | copy-done | bytes 917528
  36.7 8.9 %shard_map.100 = bf16[8,4,2,64,128]{4,3,2,1,0:T(8,128)(2,1)S(1)} custom-call(s32[8]{0:T(128)S(1)} %gather_fusion.2, bf16[8,2,64,512]{3,2,1,0:T(8,128)(2,1)S(1)} %all-to-all-done.x_ref, f32[4,2,8,64,1]{4,3,2,1,0:T(8,128)S(1)} %get-tuple-element.18.t1c, f32[4,2,8,64,1]{4,3,2,1,0:T(8,128)} %get-tuple-element.17.t1s, f32[4,64,128]{2,1,0:T(8,128)S(1)} %get-tuple-element.20.f1c, ...), custom_call_target="tpu_custom_call" | custom-call | tf_op jit(solution)/shard_map/pallas_call | solution.py:197
  46.0 1.2 %collective-permute-start = (bf16[2,512,64]{1,2,0:T(8,128)(2,1)S(1)}, bf16[2,512,64]{1,2,0:T(8,128)(2,1)S(1)}, u32[]{:S(2)}, u32[]{:S(2)}) collective-permute-start(bf16[2,512,64]{1,2,0:T(8,128)(2,1)S(1)} %copy.14), channel_id=1, source_target_pairs={{0,12},{2,14},{4,8},{6,10},{8,4},{10,6},{12,0},{14,2},{1,13},{3,15... | collective-permute-start | bytes 393224 | tf_op jit(solution)/shard_map/ppermute | solution.py:246
  48.0 3.6 %collective-permute-start.1 = (bf16[2,512,64]{1,2,0:T(8,128)(2,1)S(1)}, bf16[2,512,64]{1,2,0:T(8,128)(2,1)S(1)}, u32[]{:S(2)}, u32[]{:S(2)}) collective-permute-start(bf16[2,512,64]{1,2,0:T(8,128)(2,1)S(1)} %copy.16), channel_id=1, source_target_pairs={{0,14},{2,12},{4,10},{6,8},{8,6},{10,4},{12,2},{14,0},{1,15},{3,13... | collective-permute-start | bytes 393224 | tf_op jit(solution)/shard_map/ppermute | solution.py:246
  52.3 3.0 %collective-permute-start.3 = (bf16[2,512,64]{1,2,0:T(8,128)(2,1)S(1)}, bf16[2,512,64]{1,2,0:T(8,128)(2,1)S(1)}, u32[]{:S(2)}, u32[]{:S(2)}) collective-permute-start(bf16[2,512,64]{1,2,0:T(8,128)(2,1)S(1)} %copy.20), channel_id=1, source_target_pairs={{0,10},{2,8},{4,14},{6,12},{8,2},{10,0},{12,6},{14,4},{1,11},{3,9}... | collective-permute-start | bytes 393224 | tf_op jit(solution)/shard_map/ppermute | solution.py:246
  56.4 6.8 %collective-permute-start.5 = (bf16[2,512,64]{1,2,0:T(8,128)(2,1)S(1)}, bf16[2,512,64]{1,2,0:T(8,128)(2,1)S(1)}, u32[]{:S(2)}, u32[]{:S(2)}) collective-permute-start(bf16[2,512,64]{1,2,0:T(8,128)(2,1)S(1)} %copy.24), channel_id=1, source_target_pairs={{0,6},{2,4},{4,2},{6,0},{8,14},{10,12},{12,10},{14,8},{1,7},{3,5},... | collective-permute-start | bytes 393224 | tf_op jit(solution)/shard_map/ppermute | solution.py:246
  63.3 1.2 %collective-permute-start.6 = (bf16[2,512,64]{1,2,0:T(8,128)(2,1)S(1)}, bf16[2,512,64]{1,2,0:T(8,128)(2,1)S(1)}, u32[]{:S(2)}, u32[]{:S(2)}) collective-permute-start(bf16[2,512,64]{1,2,0:T(8,128)(2,1)S(1)} %copy.26), channel_id=1, source_target_pairs={{0,2},{2,0},{4,6},{6,4},{8,10},{10,8},{12,14},{14,12},{1,3},{3,1},... | collective-permute-start | bytes 393224 | tf_op jit(solution)/shard_map/ppermute | solution.py:246
  64.5 3.9 %collective-permute-done.2 = bf16[2,512,64]{1,2,0:T(8,128)(2,1)S(1)} collective-permute-done((bf16[2,512,64]{1,2,0:T(8,128)(2,1)S(1)}, bf16[2,512,64]{1,2,0:T(8,128)(2,1)S(1)}, u32[]{:S(2)}, u32[]{:S(2)}) %collective-permute-start.2) | collective-permute-done | bytes 131104 | tf_op jit(solution)/shard_map/ppermute | solution.py:246
  68.4 2.0 %collective-permute-done.3 = bf16[2,512,64]{1,2,0:T(8,128)(2,1)S(1)} collective-permute-done((bf16[2,512,64]{1,2,0:T(8,128)(2,1)S(1)}, bf16[2,512,64]{1,2,0:T(8,128)(2,1)S(1)}, u32[]{:S(2)}, u32[]{:S(2)}) %collective-permute-start.3) | collective-permute-done | bytes 131104 | tf_op jit(solution)/shard_map/ppermute | solution.py:246
  70.5 0.9 %collective-permute-done.5 = bf16[2,512,64]{1,2,0:T(8,128)(2,1)S(1)} collective-permute-done((bf16[2,512,64]{1,2,0:T(8,128)(2,1)S(1)}, bf16[2,512,64]{1,2,0:T(8,128)(2,1)S(1)}, u32[]{:S(2)}, u32[]{:S(2)}) %collective-permute-start.5) | collective-permute-done | bytes 131104 | tf_op jit(solution)/shard_map/ppermute | solution.py:246
  71.3 0.5 collective-permute-done.6
  71.9 0.6 gather_fusion.3
  72.7 1.3 %copy.29 = bf16[1,1,2,512,512]{4,3,2,1,0:T(8,128)(2,1)} copy(bf16[1,1,2,512,512]{3,4,2,1,0:T(8,128)(2,1)S(1)} %bitcast.39) | data formatting | bytes 2097152 | tf_op jit(solution)/shard_map/reshape | solution.py:292
  (62 shorter events, 3.9 us)
Async XLA Ops:
  0.0 11.0 %copy-start = (s32[2,4]{1,0:T(2,128)S(1)}, s32[2,4]{1,0:T(2,128)}, u32[]{:S(2)}) copy-start(s32[2,4]{1,0:T(2,128)} %param.12) | copy-start | bytes 100
  0.0 9.8 %copy-start.2 = (s32[8]{0:T(128)S(1)}, s32[8]{0:T(128)}, u32[]{:S(2)}) copy-start(s32[8]{0:T(128)} %constant.92.clone) | copy-start | bytes 100
  0.0 12.4 %copy-start.7 = (f32[4]{0:T(128)S(1)}, f32[4]{0:T(128)}, u32[]{:S(2)}) copy-start(f32[4]{0:T(128)} %param.11) | copy-start | bytes 52
  2.3 11.0 %copy-start.4 = (f32[128]{0:T(128)S(1)}, f32[128]{0:T(128)}, u32[]{:S(2)}) copy-start(f32[128]{0:T(128)} %constant.93.clone) | copy-start | bytes 1540
  2.3 11.9 %copy-start.5 = (f32[2,8]{1,0:T(2,128)S(1)}, f32[2,8]{1,0:T(2,128)}, u32[]{:S(2)}) copy-start(f32[2,8]{1,0:T(2,128)} %constant.94.clone) | copy-start | bytes 196
  2.3 33.2 %all-to-all-start = ((bf16[8,2,64,512]{3,2,1,0:T(8,128)(2,1)}), bf16[8,2,64,512]{3,2,1,0:T(8,128)(2,1)S(1)}, u32[]{:S(2)}, u32[]{:S(2)}) async-start(bf16[8,2,64,512]{3,2,1,0:T(8,128)(2,1)} %bitcast.37), calls=%async_computation | async-start | bytes 2097152 | tf_op jit(solution)/shard_map/all_to_all | solution.py:265
  14.2 8.4 %copy-start.3 = (f32[4,8]{1,0:T(4,128)S(1)}, f32[4,8]{1,0:T(4,128)}, u32[]{:S(2)}) copy-start(f32[4,8]{1,0:T(4,128)} %constant.95.clone) | copy-start | bytes 388
  35.5 1.2 %copy-start.1 = (bf16[7,256,256]{2,1,0:T(8,128)(2,1)S(1)}, bf16[7,256,256]{2,1,0:T(8,128)(2,1)}, u32[]{:S(2)}) copy-start(bf16[7,256,256]{2,1,0:T(8,128)(2,1)} %constant.96.clone.k1_hbm) | copy-start | bytes 2752516
  45.6 1.7 %copy-start.6 = (s32[8]{0:T(128)S(1)}, s32[8]{0:T(128)}, u32[]{:S(2)}) copy-start(s32[8]{0:T(128)} %fusion.3) | copy-start | bytes 100
  46.0 10.4 %collective-permute-start = (bf16[2,512,64]{1,2,0:T(8,128)(2,1)S(1)}, bf16[2,512,64]{1,2,0:T(8,128)(2,1)S(1)}, u32[]{:S(2)}, u32[]{:S(2)}) collective-permute-start(bf16[2,512,64]{1,2,0:T(8,128)(2,1)S(1)} %copy.14), channel_id=1, source_target_pairs={{0,12},{2,14},{4,8},{6,10},{8,4},{10,6},{12,0},{14,2},{1,13},{3,15... | collective-permute-start | bytes 393224 | tf_op jit(solution)/shard_map/ppermute | solution.py:246
  48.0 15.3 %collective-permute-start.1 = (bf16[2,512,64]{1,2,0:T(8,128)(2,1)S(1)}, bf16[2,512,64]{1,2,0:T(8,128)(2,1)S(1)}, u32[]{:S(2)}, u32[]{:S(2)}) collective-permute-start(bf16[2,512,64]{1,2,0:T(8,128)(2,1)S(1)} %copy.16), channel_id=1, source_target_pairs={{0,14},{2,12},{4,10},{6,8},{8,6},{10,4},{12,2},{14,0},{1,15},{3,13... | collective-permute-start | bytes 393224 | tf_op jit(solution)/shard_map/ppermute | solution.py:246
  51.8 16.5 %collective-permute-start.2 = (bf16[2,512,64]{1,2,0:T(8,128)(2,1)S(1)}, bf16[2,512,64]{1,2,0:T(8,128)(2,1)S(1)}, u32[]{:S(2)}, u32[]{:S(2)}) collective-permute-start(bf16[2,512,64]{1,2,0:T(8,128)(2,1)S(1)} %copy.18), channel_id=1, source_target_pairs={{0,8},{2,10},{4,12},{6,14},{8,0},{10,2},{12,4},{14,6},{1,9},{3,11}... | collective-permute-start | bytes 393224 | tf_op jit(solution)/shard_map/ppermute | solution.py:246
  52.3 18.2 %collective-permute-start.3 = (bf16[2,512,64]{1,2,0:T(8,128)(2,1)S(1)}, bf16[2,512,64]{1,2,0:T(8,128)(2,1)S(1)}, u32[]{:S(2)}, u32[]{:S(2)}) collective-permute-start(bf16[2,512,64]{1,2,0:T(8,128)(2,1)S(1)} %copy.20), channel_id=1, source_target_pairs={{0,10},{2,8},{4,14},{6,12},{8,2},{10,0},{12,6},{14,4},{1,11},{3,9}... | collective-permute-start | bytes 393224 | tf_op jit(solution)/shard_map/ppermute | solution.py:246
  55.6 14.8 %collective-permute-start.4 = (bf16[2,512,64]{1,2,0:T(8,128)(2,1)S(1)}, bf16[2,512,64]{1,2,0:T(8,128)(2,1)S(1)}, u32[]{:S(2)}, u32[]{:S(2)}) collective-permute-start(bf16[2,512,64]{1,2,0:T(8,128)(2,1)S(1)} %copy.22), channel_id=1, source_target_pairs={{0,4},{2,6},{4,0},{6,2},{8,12},{10,14},{12,8},{14,10},{1,5},{3,7},... | collective-permute-start | bytes 393224 | tf_op jit(solution)/shard_map/ppermute | solution.py:246
  56.4 14.9 %collective-permute-start.5 = (bf16[2,512,64]{1,2,0:T(8,128)(2,1)S(1)}, bf16[2,512,64]{1,2,0:T(8,128)(2,1)S(1)}, u32[]{:S(2)}, u32[]{:S(2)}) collective-permute-start(bf16[2,512,64]{1,2,0:T(8,128)(2,1)S(1)} %copy.24), channel_id=1, source_target_pairs={{0,6},{2,4},{4,2},{6,0},{8,14},{10,12},{12,10},{14,8},{1,7},{3,5},... | collective-permute-start | bytes 393224 | tf_op jit(solution)/shard_map/ppermute | solution.py:246
  63.3 8.6 %collective-permute-start.6 = (bf16[2,512,64]{1,2,0:T(8,128)(2,1)S(1)}, bf16[2,512,64]{1,2,0:T(8,128)(2,1)S(1)}, u32[]{:S(2)}, u32[]{:S(2)}) collective-permute-start(bf16[2,512,64]{1,2,0:T(8,128)(2,1)S(1)} %copy.26), channel_id=1, source_target_pairs={{0,2},{2,0},{4,6},{6,4},{8,10},{10,8},{12,14},{14,12},{1,3},{3,1},... | collective-permute-start | bytes 393224 | tf_op jit(solution)/shard_map/ppermute | solution.py:246

commit v12 on v11

--- a/solution.py
+++ b/solution.py
@@ -124,18 +124,17 @@
     load_one.wait()
     count = half // TILE
     per_piece = local // TILE
-    for s in range(4):
-        parts = []
+    parts = []
+    for i in range(count):
+        b, k = divmod(i, per_piece)
+        stacked = [x_ref[s * beam_count + b, :, :, pl.ds(k * TILE, TILE)] for s in range(4)]
+        parts.append(jnp.concatenate(stacked, axis=0).reshape(8 * rows, TILE))
+    for j in range(count):
+        total = None
         for i in range(count):
-            b, k = divmod(i, per_piece)
-            piece = x_ref[s * beam_count + b, :, :, pl.ds(k * TILE, TILE)]
-            parts.append(piece.reshape(2 * rows, TILE))
-        for j in range(count):
-            total = None
-            for i in range(count):
-                term = jnp.dot(parts[i], k1_v[j - i + count - 1], preferred_element_type=jnp.float32)
-                total = term if total is None else total + term
-            odd1_v[s, :, pl.ds(j * TILE, TILE)] = total
+            term = jnp.dot(parts[i], k1_v[j - i + count - 1], preferred_element_type=jnp.float32)
+            total = term if total is None else total + term
+        odd1_v[:, :, pl.ds(j * TILE, TILE)] = total.reshape(4, 2 * rows, TILE)
 
     for pair in range(2):
         for u in range(wide):
@@ -152,22 +151,21 @@
             first_v[pair, pl.ds(rows, rows), out_cols] = im_sum.astype(first_v.dtype)
 
     load_two.wait()
-    for pair in range(2):
-        evens = [first_v[pair, :, pl.ds(i * TILE, TILE)] for i in range(count)]
-        odds = [first_v[pair, :, pl.ds(half + i * TILE, TILE)] for i in range(count)]
-        for j in range(count):
-            even_out = None
-            odd_out = None
-            for i in range(count):
-                gap = j - i + count - 1
-                term_e = jnp.dot(evens[i], k2_v[0, gap], preferred_element_type=jnp.float32)
-                term_e += jnp.dot(odds[i], k2_v[2, gap], preferred_element_type=jnp.float32)
-                term_o = jnp.dot(evens[i], k2_v[1, gap], preferred_element_type=jnp.float32)
-                term_o += jnp.dot(odds[i], k2_v[0, gap], preferred_element_type=jnp.float32)
-                even_out = term_e if even_out is None else even_out + term_e
-                odd_out = term_o if odd_out is None else odd_out + term_o
-            odd2_v[pair, :, pl.ds(j * TILE, TILE)] = even_out
-            odd2_v[pair, :, pl.ds(half + j * TILE, TILE)] = odd_out
+    evens = [first_v[:, :, pl.ds(i * TILE, TILE)].reshape(4 * rows, TILE) for i in range(count)]
+    odds = [first_v[:, :, pl.ds(half + i * TILE, TILE)].reshape(4 * rows, TILE) for i in range(count)]
+    for j in range(count):
+        even_out = None
+        odd_out = None
+        for i in range(count):
+            gap = j - i + count - 1
+            term_e = jnp.dot(evens[i], k2_v[0, gap], preferred_element_type=jnp.float32)
+            term_e += jnp.dot(odds[i], k2_v[2, gap], preferred_element_type=jnp.float32)
+            term_o = jnp.dot(evens[i], k2_v[1, gap], preferred_element_type=jnp.float32)
+            term_o += jnp.dot(odds[i], k2_v[0, gap], preferred_element_type=jnp.float32)
+            even_out = term_e if even_out is None else even_out + term_e
+            odd_out = term_o if odd_out is None else odd_out + term_o
+        odd2_v[:, :, pl.ds(j * TILE, TILE)] = even_out.reshape(2, 2 * rows, TILE)
+        odd2_v[:, :, pl.ds(half + j * TILE, TILE)] = odd_out.reshape(2, 2 * rows, TILE)
 
     for t in range(4):
         for u in range(wide):

time: 74.3 us -> 74.1 us (level)
  no operation moved by 1% of the time
where the time goes in v12:
time: 74.1 us; the launch traced here: 73.9 us
  starting transfers between devices  23.5 us (32%)
  other arithmetic  19.5 us (26%)
  waiting for transfers between devices  11.5 us (16%)
  local copies, waits for them, and re-layouts  10.3 us (14%)
  Pallas kernels  8.76 us (12%)
    ppermute x7, starting transfers between devices, swap_ordered(): moved.append(lax.ppermute(ordered[at], axes, pairs))  16 us
    pallas_call x1, Pallas kernels, merge_call(): pl.pallas_call(merge_kernel, out_shape=jax.ShapeDtypeStruct((width // LAN...  8.76 us
    sin x1, other arithmetic, merge_tables(): jnp.sin(rough_two)  8.6 us
    sin x1, other arithmetic, merge_tables(): jnp.sin(rough_one)  8.42 us
    all_to_all x1, starting transfers between devices, body(): gathered = lax.all_to_all(pieces, ('sub4', 'beam'), 0, 0, tiled=True)  7.41 us
    ppermute x7, waiting for transfers between devices, swap_ordered(): moved.append(lax.ppermute(ordered[at], axes, pairs))  7.26 us
    all_to_all x1, waiting for transfers between devices, body(): gathered = lax.all_to_all(pieces, ('sub4', 'beam'), 0, 0, tiled=True)  4.24 us
    another operation x1, local copies, waits for them, and re-layouts, body(): images[0].reshape(2, members, own_rows, local_beams).transpose(1, 0, 2, 3)  2.31 us
  transfers between devices with their start and end apart: 8, of which 5 were waited for; matrix products, arithmetic and copies ran while one was open for 32% of the time, Pallas kernels for 0%

profile of v12, /device:TPU:0, one launch (start us, length us, event | category | flops | bytes accessed | tf_op | source)
XLA Modules:
  0.0 73.9 jit_solution(7437972960063644767)
XLA Ops:
  0.0 2.3 %copy.31 = bf16[2,8,64,512]{3,2,0,1:T(8,128)(2,1)} copy(bf16[2,8,64,512]{3,2,1,0:T(8,128)(2,1)} %bitcast.48) | data formatting | bytes 2097152 | tf_op jit(solution)/shard_map/reshape;squeeze | solution.py:262
  2.3 7.4 %all-to-all-start = ((bf16[8,2,64,512]{3,2,1,0:T(8,128)(2,1)}), bf16[8,2,64,512]{3,2,1,0:T(8,128)(2,1)S(1)}, u32[]{:S(2)}, u32[]{:S(2)}) async-start(bf16[8,2,64,512]{3,2,1,0:T(8,128)(2,1)} %bitcast.37), calls=%async_computation | async-start | bytes 2097152 | tf_op jit(solution)/shard_map/all_to_all | solution.py:263
  9.8 0.6 gather_fusion
  10.4 0.6 fusion.3
  11.0 0.6 gather_fusion.1
  11.6 0.7 iota_reduce_fusion
  12.6 0.6 gather_fusion.2
  13.7 0.5 multiply_sine_fusion.2
  14.2 8.4 %multiply_sine_fusion.1 = (f32[4,2,8,64,1]{4,3,2,1,0:T(8,128)}, f32[4,2,8,64,1]{4,3,2,1,0:T(8,128)S(1)}) fusion(f32[2,8]{1,0:T(2,128)S(1)} %copy-done.5, f32[4,64]{1,0:T(4,128)S(1)} %broadcast_multiply_fusion), kind=kLoop, calls=%fused_computation.6 | loop fusion | flops 4096 | bytes 33856 | tf_op jit(solution)/shard_map/sin | solution.py:229
  22.7 8.6 %multiply_sine_fusion = (f32[2,4,8,64,1]{4,3,2,1,0:T(8,128)}, f32[2,4,8,64,1]{4,3,2,1,0:T(8,128)}) fusion(f32[4,8]{1,0:T(4,128)S(1)} %copy-done.3, f32[2,64]{1,0:T(2,128)S(1)} %broadcast_multiply_fusion.1), kind=kLoop, calls=%fused_computation.4 | loop fusion | flops 4096 | bytes 33408 | tf_op jit(solution)/shard_map/sin | solution.py:230
  31.3 4.2 %all-to-all-done.x_ref = bf16[8,2,64,512]{3,2,1,0:T(8,128)(2,1)S(1)} async-done(((bf16[8,2,64,512]{3,2,1,0:T(8,128)(2,1)}), bf16[8,2,64,512]{3,2,1,0:T(8,128)(2,1)S(1)}, u32[]{:S(2)}, u32[]{:S(2)}) %all-to-all-start) | async-done | bytes 1048608 | tf_op jit(solution)/shard_map/all_to_all | solution.py:263
  35.5 1.2 %copy-done.1 = bf16[7,256,256]{2,1,0:T(8,128)(2,1)S(1)} copy-done((bf16[7,256,256]{2,1,0:T(8,128)(2,1)S(1)}, bf16[7,256,256]{2,1,0:T(8,128)(2,1)}, u32[]{:S(2)}) %copy-start.1) | copy-done | bytes 917528
  36.7 8.8 %shard_map.100 = bf16[8,4,2,64,128]{4,3,2,1,0:T(8,128)(2,1)S(1)} custom-call(s32[8]{0:T(128)S(1)} %gather_fusion.2, bf16[8,2,64,512]{3,2,1,0:T(8,128)(2,1)S(1)} %all-to-all-done.x_ref, f32[4,2,8,64,1]{4,3,2,1,0:T(8,128)S(1)} %get-tuple-element.18.t1c, f32[4,2,8,64,1]{4,3,2,1,0:T(8,128)} %get-tuple-element.17.t1s, f32[4,64,128]{2,1,0:T(8,128)S(1)} %get-tuple-element.20.f1c, ...), custom_call_target="tpu_custom_call" | custom-call | tf_op jit(solution)/shard_map/pallas_call | solution.py:195
  45.9 1.3 %collective-permute-start = (bf16[2,512,64]{1,2,0:T(8,128)(2,1)S(1)}, bf16[2,512,64]{1,2,0:T(8,128)(2,1)S(1)}, u32[]{:S(2)}, u32[]{:S(2)}) collective-permute-start(bf16[2,512,64]{1,2,0:T(8,128)(2,1)S(1)} %copy.14), channel_id=1, source_target_pairs={{0,12},{2,14},{4,8},{6,10},{8,4},{10,6},{12,0},{14,2},{1,13},{3,15... | collective-permute-start | bytes 393224 | tf_op jit(solution)/shard_map/ppermute | solution.py:244
  47.8 3.6 %collective-permute-start.1 = (bf16[2,512,64]{1,2,0:T(8,128)(2,1)S(1)}, bf16[2,512,64]{1,2,0:T(8,128)(2,1)S(1)}, u32[]{:S(2)}, u32[]{:S(2)}) collective-permute-start(bf16[2,512,64]{1,2,0:T(8,128)(2,1)S(1)} %copy.16), channel_id=1, source_target_pairs={{0,14},{2,12},{4,10},{6,8},{8,6},{10,4},{12,2},{14,0},{1,15},{3,13... | collective-permute-start | bytes 393224 | tf_op jit(solution)/shard_map/ppermute | solution.py:244
  52.1 3.0 %collective-permute-start.3 = (bf16[2,512,64]{1,2,0:T(8,128)(2,1)S(1)}, bf16[2,512,64]{1,2,0:T(8,128)(2,1)S(1)}, u32[]{:S(2)}, u32[]{:S(2)}) collective-permute-start(bf16[2,512,64]{1,2,0:T(8,128)(2,1)S(1)} %copy.20), channel_id=1, source_target_pairs={{0,10},{2,8},{4,14},{6,12},{8,2},{10,0},{12,6},{14,4},{1,11},{3,9}... | collective-permute-start | bytes 393224 | tf_op jit(solution)/shard_map/ppermute | solution.py:244
  56.3 6.8 %collective-permute-start.5 = (bf16[2,512,64]{1,2,0:T(8,128)(2,1)S(1)}, bf16[2,512,64]{1,2,0:T(8,128)(2,1)S(1)}, u32[]{:S(2)}, u32[]{:S(2)}) collective-permute-start(bf16[2,512,64]{1,2,0:T(8,128)(2,1)S(1)} %copy.24), channel_id=1, source_target_pairs={{0,6},{2,4},{4,2},{6,0},{8,14},{10,12},{12,10},{14,8},{1,7},{3,5},... | collective-permute-start | bytes 393224 | tf_op jit(solution)/shard_map/ppermute | solution.py:244
  63.1 1.3 %collective-permute-start.6 = (bf16[2,512,64]{1,2,0:T(8,128)(2,1)S(1)}, bf16[2,512,64]{1,2,0:T(8,128)(2,1)S(1)}, u32[]{:S(2)}, u32[]{:S(2)}) collective-permute-start(bf16[2,512,64]{1,2,0:T(8,128)(2,1)S(1)} %copy.26), channel_id=1, source_target_pairs={{0,2},{2,0},{4,6},{6,4},{8,10},{10,8},{12,14},{14,12},{1,3},{3,1},... | collective-permute-start | bytes 393224 | tf_op jit(solution)/shard_map/ppermute | solution.py:244
  64.4 3.9 %collective-permute-done.2 = bf16[2,512,64]{1,2,0:T(8,128)(2,1)S(1)} collective-permute-done((bf16[2,512,64]{1,2,0:T(8,128)(2,1)S(1)}, bf16[2,512,64]{1,2,0:T(8,128)(2,1)S(1)}, u32[]{:S(2)}, u32[]{:S(2)}) %collective-permute-start.2) | collective-permute-done | bytes 131104 | tf_op jit(solution)/shard_map/ppermute | solution.py:244
  68.3 2.0 %collective-permute-done.3 = bf16[2,512,64]{1,2,0:T(8,128)(2,1)S(1)} collective-permute-done((bf16[2,512,64]{1,2,0:T(8,128)(2,1)S(1)}, bf16[2,512,64]{1,2,0:T(8,128)(2,1)S(1)}, u32[]{:S(2)}, u32[]{:S(2)}) %collective-permute-start.3) | collective-permute-done | bytes 131104 | tf_op jit(solution)/shard_map/ppermute | solution.py:244
  70.3 0.9 %collective-permute-done.5 = bf16[2,512,64]{1,2,0:T(8,128)(2,1)S(1)} collective-permute-done((bf16[2,512,64]{1,2,0:T(8,128)(2,1)S(1)}, bf16[2,512,64]{1,2,0:T(8,128)(2,1)S(1)}, u32[]{:S(2)}, u32[]{:S(2)}) %collective-permute-start.5) | collective-permute-done | bytes 131104 | tf_op jit(solution)/shard_map/ppermute | solution.py:244
  71.2 0.5 collective-permute-done.6
  71.7 0.6 gather_fusion.3
  72.6 1.3 %copy.29 = bf16[1,1,2,512,512]{4,3,2,1,0:T(8,128)(2,1)} copy(bf16[1,1,2,512,512]{3,4,2,1,0:T(8,128)(2,1)S(1)} %bitcast.39) | data formatting | bytes 2097152 | tf_op jit(solution)/shard_map/reshape | solution.py:290
  (62 shorter events, 3.9 us)
Async XLA Ops:
  0.0 11.0 %copy-start = (s32[2,4]{1,0:T(2,128)S(1)}, s32[2,4]{1,0:T(2,128)}, u32[]{:S(2)}) copy-start(s32[2,4]{1,0:T(2,128)} %param.12) | copy-start | bytes 100
  0.0 9.8 %copy-start.2 = (s32[8]{0:T(128)S(1)}, s32[8]{0:T(128)}, u32[]{:S(2)}) copy-start(s32[8]{0:T(128)} %constant.92.clone) | copy-start | bytes 100
  0.0 12.4 %copy-start.7 = (f32[4]{0:T(128)S(1)}, f32[4]{0:T(128)}, u32[]{:S(2)}) copy-start(f32[4]{0:T(128)} %param.11) | copy-start | bytes 52
  2.3 11.0 %copy-start.4 = (f32[128]{0:T(128)S(1)}, f32[128]{0:T(128)}, u32[]{:S(2)}) copy-start(f32[128]{0:T(128)} %constant.93.clone) | copy-start | bytes 1540
  2.3 11.9 %copy-start.5 = (f32[2,8]{1,0:T(2,128)S(1)}, f32[2,8]{1,0:T(2,128)}, u32[]{:S(2)}) copy-start(f32[2,8]{1,0:T(2,128)} %constant.94.clone) | copy-start | bytes 196
  2.3 33.2 %all-to-all-start = ((bf16[8,2,64,512]{3,2,1,0:T(8,128)(2,1)}), bf16[8,2,64,512]{3,2,1,0:T(8,128)(2,1)S(1)}, u32[]{:S(2)}, u32[]{:S(2)}) async-start(bf16[8,2,64,512]{3,2,1,0:T(8,128)(2,1)} %bitcast.37), calls=%async_computation | async-start | bytes 2097152 | tf_op jit(solution)/shard_map/all_to_all | solution.py:263
  14.2 8.4 %copy-start.3 = (f32[4,8]{1,0:T(4,128)S(1)}, f32[4,8]{1,0:T(4,128)}, u32[]{:S(2)}) copy-start(f32[4,8]{1,0:T(4,128)} %constant.95.clone) | copy-start | bytes 388
  35.5 1.2 %copy-start.1 = (bf16[7,256,256]{2,1,0:T(8,128)(2,1)S(1)}, bf16[7,256,256]{2,1,0:T(8,128)(2,1)}, u32[]{:S(2)}) copy-start(bf16[7,256,256]{2,1,0:T(8,128)(2,1)} %constant.96.clone.k1_hbm) | copy-start | bytes 2752516
  45.4 1.7 %copy-start.6 = (s32[8]{0:T(128)S(1)}, s32[8]{0:T(128)}, u32[]{:S(2)}) copy-start(s32[8]{0:T(128)} %fusion.3) | copy-start | bytes 100
  45.9 10.4 %collective-permute-start = (bf16[2,512,64]{1,2,0:T(8,128)(2,1)S(1)}, bf16[2,512,64]{1,2,0:T(8,128)(2,1)S(1)}, u32[]{:S(2)}, u32[]{:S(2)}) collective-permute-start(bf16[2,512,64]{1,2,0:T(8,128)(2,1)S(1)} %copy.14), channel_id=1, source_target_pairs={{0,12},{2,14},{4,8},{6,10},{8,4},{10,6},{12,0},{14,2},{1,13},{3,15... | collective-permute-start | bytes 393224 | tf_op jit(solution)/shard_map/ppermute | solution.py:244
  47.8 15.3 %collective-permute-start.1 = (bf16[2,512,64]{1,2,0:T(8,128)(2,1)S(1)}, bf16[2,512,64]{1,2,0:T(8,128)(2,1)S(1)}, u32[]{:S(2)}, u32[]{:S(2)}) collective-permute-start(bf16[2,512,64]{1,2,0:T(8,128)(2,1)S(1)} %copy.16), channel_id=1, source_target_pairs={{0,14},{2,12},{4,10},{6,8},{8,6},{10,4},{12,2},{14,0},{1,15},{3,13... | collective-permute-start | bytes 393224 | tf_op jit(solution)/shard_map/ppermute | solution.py:244
  51.7 16.5 %collective-permute-start.2 = (bf16[2,512,64]{1,2,0:T(8,128)(2,1)S(1)}, bf16[2,512,64]{1,2,0:T(8,128)(2,1)S(1)}, u32[]{:S(2)}, u32[]{:S(2)}) collective-permute-start(bf16[2,512,64]{1,2,0:T(8,128)(2,1)S(1)} %copy.18), channel_id=1, source_target_pairs={{0,8},{2,10},{4,12},{6,14},{8,0},{10,2},{12,4},{14,6},{1,9},{3,11}... | collective-permute-start | bytes 393224 | tf_op jit(solution)/shard_map/ppermute | solution.py:244
  52.1 18.1 %collective-permute-start.3 = (bf16[2,512,64]{1,2,0:T(8,128)(2,1)S(1)}, bf16[2,512,64]{1,2,0:T(8,128)(2,1)S(1)}, u32[]{:S(2)}, u32[]{:S(2)}) collective-permute-start(bf16[2,512,64]{1,2,0:T(8,128)(2,1)S(1)} %copy.20), channel_id=1, source_target_pairs={{0,10},{2,8},{4,14},{6,12},{8,2},{10,0},{12,6},{14,4},{1,11},{3,9}... | collective-permute-start | bytes 393224 | tf_op jit(solution)/shard_map/ppermute | solution.py:244
  55.5 14.8 %collective-permute-start.4 = (bf16[2,512,64]{1,2,0:T(8,128)(2,1)S(1)}, bf16[2,512,64]{1,2,0:T(8,128)(2,1)S(1)}, u32[]{:S(2)}, u32[]{:S(2)}) collective-permute-start(bf16[2,512,64]{1,2,0:T(8,128)(2,1)S(1)} %copy.22), channel_id=1, source_target_pairs={{0,4},{2,6},{4,0},{6,2},{8,12},{10,14},{12,8},{14,10},{1,5},{3,7},... | collective-permute-start | bytes 393224 | tf_op jit(solution)/shard_map/ppermute | solution.py:244
  56.3 14.9 %collective-permute-start.5 = (bf16[2,512,64]{1,2,0:T(8,128)(2,1)S(1)}, bf16[2,512,64]{1,2,0:T(8,128)(2,1)S(1)}, u32[]{:S(2)}, u32[]{:S(2)}) collective-permute-start(bf16[2,512,64]{1,2,0:T(8,128)(2,1)S(1)} %copy.24), channel_id=1, source_target_pairs={{0,6},{2,4},{4,2},{6,0},{8,14},{10,12},{12,10},{14,8},{1,7},{3,5},... | collective-permute-start | bytes 393224 | tf_op jit(solution)/shard_map/ppermute | solution.py:244
  63.1 8.6 %collective-permute-start.6 = (bf16[2,512,64]{1,2,0:T(8,128)(2,1)S(1)}, bf16[2,512,64]{1,2,0:T(8,128)(2,1)S(1)}, u32[]{:S(2)}, u32[]{:S(2)}) collective-permute-start(bf16[2,512,64]{1,2,0:T(8,128)(2,1)S(1)} %copy.26), channel_id=1, source_target_pairs={{0,2},{2,0},{4,6},{6,4},{8,10},{10,8},{12,14},{14,12},{1,3},{3,1},... | collective-permute-start | bytes 393224 | tf_op jit(solution)/shard_map/ppermute | solution.py:244

commit v13 on v12

--- a/solution.py
+++ b/solution.py
@@ -85,18 +85,18 @@
     assert np.array_equal(two[:width, :width], two[width:, width:])
     quads = np.stack([toeplitz_tiles(two[:width, :width]), toeplitz_tiles(two[:width, width:]),
                       toeplitz_tiles(two[width:, :width])])
-    return jnp.asarray(one), jnp.asarray(quads)
-
-
-def merge_kernel(slot_ref, x_ref, t1c, t1s, f1c, f1s, t2c, t2s, f2c, f2s, k1_hbm, k2_hbm, o_ref,
+    return jnp.asarray(np.concatenate([one[None], quads]))
+
+
+def merge_kernel(slot_ref, x_ref, t1c, t1s, f1c, f1s, t2c, t2s, f2c, f2s, k_hbm, o_ref,
                  k1_v, k2_v, first_v, odd1_v, odd2_v, sems):
     members, _, rows, local = x_ref.shape
     beam_count = members // 4
     blocks = local // LANES
     wide = beam_count * blocks
     half = wide * LANES
-    load_one = pltpu.make_async_copy(k1_hbm, k1_v, sems.at[0])
-    load_two = pltpu.make_async_copy(k2_hbm, k2_v, sems.at[1])
+    load_one = pltpu.make_async_copy(k_hbm.at[0], k1_v, sems.at[0])
+    load_two = pltpu.make_async_copy(k_hbm.at[pl.ds(1, 3)], k2_v, sems.at[1])
     load_one.start()
     load_two.start()
 
@@ -186,7 +186,7 @@
             o_ref[slot, t, 1] = im_sum.astype(o_ref.dtype)
 
 
-def merge_call(slots, x, tables, k1, k2, interpret=False):
+def merge_call(slots, x, tables, kernels, interpret=False):
     members, _, rows, local = x.shape
     width = local * members // 4
     vmem = pl.BlockSpec(memory_space=pltpu.VMEM)
@@ -195,11 +195,11 @@
     return pl.pallas_call(
         merge_kernel,
         out_shape=jax.ShapeDtypeStruct((width // LANES, 4, 2, rows, LANES), jnp.bfloat16),
-        in_specs=[smem] + [vmem] * 9 + [hbm, hbm],
+        in_specs=[smem] + [vmem] * 9 + [hbm],
         out_specs=vmem,
         scratch_shapes=[
-            pltpu.VMEM(k1.shape, jnp.bfloat16),
-            pltpu.VMEM(k2.shape, jnp.bfloat16),
+            pltpu.VMEM(kernels.shape[1:], jnp.bfloat16),
+            pltpu.VMEM((3,) + kernels.shape[1:], jnp.bfloat16),
             pltpu.VMEM((2, 2 * rows, 2 * width), jnp.bfloat16),
             pltpu.VMEM((4, 2 * rows, width), jnp.float32),
             pltpu.VMEM((2, 2 * rows, 2 * width), jnp.float32),
@@ -207,7 +207,7 @@
         ],
         compiler_params=pltpu.CompilerParams(vmem_limit_bytes=48 * 1024 * 1024),
         interpret=interpret,
-    )(slots, x, *tables, k1, k2)
+    )(slots, x, *tables, kernels)
 
 
 def merge_tables(shifts, ratios, width):
@@ -281,7 +281,7 @@
         slots,
         gathered,
         merge_tables(shifts, ratios, B),
-        *kernel_tables(B),
+        kernel_tables(B),
     )
     if direct:
         ordered = merged.transpose(0, 2, 4, 1, 3).reshape(blocks, 2, sector_width, own_rows)

time: 74.1 us -> 72.9 us (0.984)
  local copies, waits for them, and re-layouts: 10.3 us -> 9.11 us
    unnamed x23 -> x21, local copies, waits for them, and re-layouts: 1.28 us -> 0.1 us
  transfers between devices with their start and end apart: 8 -> 8, of which waited for: 5 -> 5; matrix products, arithmetic and copies ran while one was open for 32% -> 33% of each run, Pallas kernels for 0% -> 0%
where the time goes in v13:
time: 72.9 us; the launch traced here: 72.7 us
  starting transfers between devices  23.5 us (32%)
  other arithmetic  19.6 us (27%)
  waiting for transfers between devices  11.5 us (16%)
  local copies, waits for them, and re-layouts  9.11 us (12%)
  Pallas kernels  8.76 us (12%)
    ppermute x7, starting transfers between devices, swap_ordered(): moved.append(lax.ppermute(ordered[at], axes, pairs))  16.1 us
    pallas_call x1, Pallas kernels, merge_call(): pl.pallas_call(merge_kernel, out_shape=jax.ShapeDtypeStruct((width // LAN...  8.76 us
    sin x1, other arithmetic, merge_tables(): jnp.sin(rough_two)  8.59 us
    sin x1, other arithmetic, merge_tables(): jnp.sin(rough_one)  8.42 us
    all_to_all x1, starting transfers between devices, body(): gathered = lax.all_to_all(pieces, ('sub4', 'beam'), 0, 0, tiled=True)  7.41 us
    ppermute x7, waiting for transfers between devices, swap_ordered(): moved.append(lax.ppermute(ordered[at], axes, pairs))  7.24 us
    all_to_all x1, waiting for transfers between devices, body(): gathered = lax.all_to_all(pieces, ('sub4', 'beam'), 0, 0, tiled=True)  4.21 us
    another operation x1, local copies, waits for them, and re-layouts, body(): images[0].reshape(2, members, own_rows, local_beams).transpose(1, 0, 2, 3)  2.31 us
  transfers between devices with their start and end apart: 8, of which 5 were waited for; matrix products, arithmetic and copies ran while one was open for 33% of the time, Pallas kernels for 0%

profile of v13, /device:TPU:0, one launch (start us, length us, event | category | flops | bytes accessed | tf_op | source)
XLA Modules:
  0.0 72.7 jit_solution(15736874926010413142)
XLA Ops:
  0.0 2.3 %copy.30 = bf16[2,8,64,512]{3,2,0,1:T(8,128)(2,1)} copy(bf16[2,8,64,512]{3,2,1,0:T(8,128)(2,1)} %bitcast.48) | data formatting | bytes 2097152 | tf_op jit(solution)/shard_map/reshape;squeeze | solution.py:262
  2.3 7.4 %all-to-all-start = ((bf16[8,2,64,512]{3,2,1,0:T(8,128)(2,1)}), bf16[8,2,64,512]{3,2,1,0:T(8,128)(2,1)S(1)}, u32[]{:S(2)}, u32[]{:S(2)}) async-start(bf16[8,2,64,512]{3,2,1,0:T(8,128)(2,1)} %bitcast.37), calls=%async_computation | async-start | bytes 2097152 | tf_op jit(solution)/shard_map/all_to_all | solution.py:263
  9.8 0.6 gather_fusion
  10.4 0.6 fusion.3
  11.1 0.6 gather_fusion.1
  11.6 0.8 %iota_reduce_fusion = (pred[8]{0:T(512)(128)(4,1)}, s32[8]{0:T(128)S(1)}) fusion(s32[8,4]{1,0:T(8,128)S(1)} %gather_fusion.1, s32[8]{0:T(128)S(1)} %and_select_fusion.1), kind=kLoop, calls=%fused_computation.26 | loop fusion | flops 200 | bytes 200 | tf_op jit(solution)/shard_map/body/reduce | solution.py:274
  12.6 0.6 gather_fusion.2
  13.4 0.3 multiply_sine_fusion.3
  13.7 0.5 multiply_sine_fusion.2
  14.3 8.4 %multiply_sine_fusion.1 = (f32[4,2,8,64,1]{4,3,2,1,0:T(8,128)}, f32[4,2,8,64,1]{4,3,2,1,0:T(8,128)S(1)}) fusion(f32[2,8]{1,0:T(2,128)S(1)} %copy-done.4, f32[4,64]{1,0:T(4,128)S(1)} %broadcast_multiply_fusion), kind=kLoop, calls=%fused_computation.6 | loop fusion | flops 4096 | bytes 33856 | tf_op jit(solution)/shard_map/sin | solution.py:229
  22.7 8.6 %multiply_sine_fusion = (f32[2,4,8,64,1]{4,3,2,1,0:T(8,128)}, f32[2,4,8,64,1]{4,3,2,1,0:T(8,128)}) fusion(f32[4,8]{1,0:T(4,128)S(1)} %copy-done.2, f32[2,64]{1,0:T(2,128)S(1)} %broadcast_multiply_fusion.1), kind=kLoop, calls=%fused_computation.4 | loop fusion | flops 4096 | bytes 33408 | tf_op jit(solution)/shard_map/sin | solution.py:230
  31.3 4.2 %all-to-all-done.x_ref = bf16[8,2,64,512]{3,2,1,0:T(8,128)(2,1)S(1)} async-done(((bf16[8,2,64,512]{3,2,1,0:T(8,128)(2,1)}), bf16[8,2,64,512]{3,2,1,0:T(8,128)(2,1)S(1)}, u32[]{:S(2)}, u32[]{:S(2)}) %all-to-all-start) | async-done | bytes 1048608 | tf_op jit(solution)/shard_map/all_to_all | solution.py:263
  35.5 8.8 %shard_map.91 = bf16[8,4,2,64,128]{4,3,2,1,0:T(8,128)(2,1)S(1)} custom-call(s32[8]{0:T(128)S(1)} %gather_fusion.2, bf16[8,2,64,512]{3,2,1,0:T(8,128)(2,1)S(1)} %all-to-all-done.x_ref, f32[4,2,8,64,1]{4,3,2,1,0:T(8,128)S(1)} %get-tuple-element.18.t1c, f32[4,2,8,64,1]{4,3,2,1,0:T(8,128)} %get-tuple-element.17.t1s, f32[4,64,128]{2,1,0:T(8,128)S(1)} %get-tuple-element.20.f1c, ...), custom_call_target="tpu_custom_call" | custom-call | tf_op jit(solution)/shard_map/pallas_call | solution.py:195
  44.7 1.2 %collective-permute-start = (bf16[2,512,64]{1,2,0:T(8,128)(2,1)S(1)}, bf16[2,512,64]{1,2,0:T(8,128)(2,1)S(1)}, u32[]{:S(2)}, u32[]{:S(2)}) collective-permute-start(bf16[2,512,64]{1,2,0:T(8,128)(2,1)S(1)} %copy.13), channel_id=1, source_target_pairs={{0,12},{2,14},{4,8},{6,10},{8,4},{10,6},{12,0},{14,2},{1,13},{3,15... | collective-permute-start | bytes 393224 | tf_op jit(solution)/shard_map/ppermute | solution.py:244
  46.6 3.6 %collective-permute-start.1 = (bf16[2,512,64]{1,2,0:T(8,128)(2,1)S(1)}, bf16[2,512,64]{1,2,0:T(8,128)(2,1)S(1)}, u32[]{:S(2)}, u32[]{:S(2)}) collective-permute-start(bf16[2,512,64]{1,2,0:T(8,128)(2,1)S(1)} %copy.15), channel_id=1, source_target_pairs={{0,14},{2,12},{4,10},{6,8},{8,6},{10,4},{12,2},{14,0},{1,15},{3,13... | collective-permute-start | bytes 393224 | tf_op jit(solution)/shard_map/ppermute | solution.py:244
  50.9 3.0 %collective-permute-start.3 = (bf16[2,512,64]{1,2,0:T(8,128)(2,1)S(1)}, bf16[2,512,64]{1,2,0:T(8,128)(2,1)S(1)}, u32[]{:S(2)}, u32[]{:S(2)}) collective-permute-start(bf16[2,512,64]{1,2,0:T(8,128)(2,1)S(1)} %copy.19), channel_id=1, source_target_pairs={{0,10},{2,8},{4,14},{6,12},{8,2},{10,0},{12,6},{14,4},{1,11},{3,9}... | collective-permute-start | bytes 393224 | tf_op jit(solution)/shard_map/ppermute | solution.py:244
  55.1 6.8 %collective-permute-start.5 = (bf16[2,512,64]{1,2,0:T(8,128)(2,1)S(1)}, bf16[2,512,64]{1,2,0:T(8,128)(2,1)S(1)}, u32[]{:S(2)}, u32[]{:S(2)}) collective-permute-start(bf16[2,512,64]{1,2,0:T(8,128)(2,1)S(1)} %copy.23), channel_id=1, source_target_pairs={{0,6},{2,4},{4,2},{6,0},{8,14},{10,12},{12,10},{14,8},{1,7},{3,5},... | collective-permute-start | bytes 393224 | tf_op jit(solution)/shard_map/ppermute | solution.py:244
  61.9 1.3 %collective-permute-start.6 = (bf16[2,512,64]{1,2,0:T(8,128)(2,1)S(1)}, bf16[2,512,64]{1,2,0:T(8,128)(2,1)S(1)}, u32[]{:S(2)}, u32[]{:S(2)}) collective-permute-start(bf16[2,512,64]{1,2,0:T(8,128)(2,1)S(1)} %copy.25), channel_id=1, source_target_pairs={{0,2},{2,0},{4,6},{6,4},{8,10},{10,8},{12,14},{14,12},{1,3},{3,1},... | collective-permute-start | bytes 393224 | tf_op jit(solution)/shard_map/ppermute | solution.py:244
  63.2 3.9 %collective-permute-done.2 = bf16[2,512,64]{1,2,0:T(8,128)(2,1)S(1)} collective-permute-done((bf16[2,512,64]{1,2,0:T(8,128)(2,1)S(1)}, bf16[2,512,64]{1,2,0:T(8,128)(2,1)S(1)}, u32[]{:S(2)}, u32[]{:S(2)}) %collective-permute-start.2) | collective-permute-done | bytes 131104 | tf_op jit(solution)/shard_map/ppermute | solution.py:244
  67.1 2.0 %collective-permute-done.3 = bf16[2,512,64]{1,2,0:T(8,128)(2,1)S(1)} collective-permute-done((bf16[2,512,64]{1,2,0:T(8,128)(2,1)S(1)}, bf16[2,512,64]{1,2,0:T(8,128)(2,1)S(1)}, u32[]{:S(2)}, u32[]{:S(2)}) %collective-permute-start.3) | collective-permute-done | bytes 131104 | tf_op jit(solution)/shard_map/ppermute | solution.py:244
  69.1 0.9 %collective-permute-done.5 = bf16[2,512,64]{1,2,0:T(8,128)(2,1)S(1)} collective-permute-done((bf16[2,512,64]{1,2,0:T(8,128)(2,1)S(1)}, bf16[2,512,64]{1,2,0:T(8,128)(2,1)S(1)}, u32[]{:S(2)}, u32[]{:S(2)}) %collective-permute-start.5) | collective-permute-done | bytes 131104 | tf_op jit(solution)/shard_map/ppermute | solution.py:244
  70.0 0.5 collective-permute-done.6
  70.5 0.6 gather_fusion.3
  71.4 1.3 %copy.28 = bf16[1,1,2,512,512]{4,3,2,1,0:T(8,128)(2,1)} copy(bf16[1,1,2,512,512]{3,4,2,1,0:T(8,128)(2,1)S(1)} %bitcast.39) | data formatting | bytes 2097152 | tf_op jit(solution)/shard_map/reshape | solution.py:290
  (60 shorter events, 3.5 us)
Async XLA Ops:
  0.0 11.0 %copy-start = (s32[2,4]{1,0:T(2,128)S(1)}, s32[2,4]{1,0:T(2,128)}, u32[]{:S(2)}) copy-start(s32[2,4]{1,0:T(2,128)} %param.11) | copy-start | bytes 100
  0.0 9.8 %copy-start.1 = (s32[8]{0:T(128)S(1)}, s32[8]{0:T(128)}, u32[]{:S(2)}) copy-start(s32[8]{0:T(128)} %constant.90.clone) | copy-start | bytes 100
  0.0 12.4 %copy-start.6 = (f32[4]{0:T(128)S(1)}, f32[4]{0:T(128)}, u32[]{:S(2)}) copy-start(f32[4]{0:T(128)} %param.10) | copy-start | bytes 52
  2.3 11.1 %copy-start.3 = (f32[128]{0:T(128)S(1)}, f32[128]{0:T(128)}, u32[]{:S(2)}) copy-start(f32[128]{0:T(128)} %constant.91.clone) | copy-start | bytes 1540
  2.3 11.9 %copy-start.4 = (f32[2,8]{1,0:T(2,128)S(1)}, f32[2,8]{1,0:T(2,128)}, u32[]{:S(2)}) copy-start(f32[2,8]{1,0:T(2,128)} %constant.92.clone) | copy-start | bytes 196
  2.3 33.2 %all-to-all-start = ((bf16[8,2,64,512]{3,2,1,0:T(8,128)(2,1)}), bf16[8,2,64,512]{3,2,1,0:T(8,128)(2,1)S(1)}, u32[]{:S(2)}, u32[]{:S(2)}) async-start(bf16[8,2,64,512]{3,2,1,0:T(8,128)(2,1)} %bitcast.37), calls=%async_computation | async-start | bytes 2097152 | tf_op jit(solution)/shard_map/all_to_all | solution.py:263
  14.3 8.4 %copy-start.2 = (f32[4,8]{1,0:T(4,128)S(1)}, f32[4,8]{1,0:T(4,128)}, u32[]{:S(2)}) copy-start(f32[4,8]{1,0:T(4,128)} %constant.93.clone) | copy-start | bytes 388
  44.3 1.7 %copy-start.5 = (s32[8]{0:T(128)S(1)}, s32[8]{0:T(128)}, u32[]{:S(2)}) copy-start(s32[8]{0:T(128)} %fusion.3) | copy-start | bytes 100
  44.7 10.4 %collective-permute-start = (bf16[2,512,64]{1,2,0:T(8,128)(2,1)S(1)}, bf16[2,512,64]{1,2,0:T(8,128)(2,1)S(1)}, u32[]{:S(2)}, u32[]{:S(2)}) collective-permute-start(bf16[2,512,64]{1,2,0:T(8,128)(2,1)S(1)} %copy.13), channel_id=1, source_target_pairs={{0,12},{2,14},{4,8},{6,10},{8,4},{10,6},{12,0},{14,2},{1,13},{3,15... | collective-permute-start | bytes 393224 | tf_op jit(solution)/shard_map/ppermute | solution.py:244
  46.6 15.3 %collective-permute-start.1 = (bf16[2,512,64]{1,2,0:T(8,128)(2,1)S(1)}, bf16[2,512,64]{1,2,0:T(8,128)(2,1)S(1)}, u32[]{:S(2)}, u32[]{:S(2)}) collective-permute-start(bf16[2,512,64]{1,2,0:T(8,128)(2,1)S(1)} %copy.15), channel_id=1, source_target_pairs={{0,14},{2,12},{4,10},{6,8},{8,6},{10,4},{12,2},{14,0},{1,15},{3,13... | collective-permute-start | bytes 393224 | tf_op jit(solution)/shard_map/ppermute | solution.py:244
  50.5 16.6 %collective-permute-start.2 = (bf16[2,512,64]{1,2,0:T(8,128)(2,1)S(1)}, bf16[2,512,64]{1,2,0:T(8,128)(2,1)S(1)}, u32[]{:S(2)}, u32[]{:S(2)}) collective-permute-start(bf16[2,512,64]{1,2,0:T(8,128)(2,1)S(1)} %copy.17), channel_id=1, source_target_pairs={{0,8},{2,10},{4,12},{6,14},{8,0},{10,2},{12,4},{14,6},{1,9},{3,11}... | collective-permute-start | bytes 393224 | tf_op jit(solution)/shard_map/ppermute | solution.py:244
  50.9 18.2 %collective-permute-start.3 = (bf16[2,512,64]{1,2,0:T(8,128)(2,1)S(1)}, bf16[2,512,64]{1,2,0:T(8,128)(2,1)S(1)}, u32[]{:S(2)}, u32[]{:S(2)}) collective-permute-start(bf16[2,512,64]{1,2,0:T(8,128)(2,1)S(1)} %copy.19), channel_id=1, source_target_pairs={{0,10},{2,8},{4,14},{6,12},{8,2},{10,0},{12,6},{14,4},{1,11},{3,9}... | collective-permute-start | bytes 393224 | tf_op jit(solution)/shard_map/ppermute | solution.py:244
  54.3 14.8 %collective-permute-start.4 = (bf16[2,512,64]{1,2,0:T(8,128)(2,1)S(1)}, bf16[2,512,64]{1,2,0:T(8,128)(2,1)S(1)}, u32[]{:S(2)}, u32[]{:S(2)}) collective-permute-start(bf16[2,512,64]{1,2,0:T(8,128)(2,1)S(1)} %copy.21), channel_id=1, source_target_pairs={{0,4},{2,6},{4,0},{6,2},{8,12},{10,14},{12,8},{14,10},{1,5},{3,7},... | collective-permute-start | bytes 393224 | tf_op jit(solution)/shard_map/ppermute | solution.py:244
  55.1 14.9 %collective-permute-start.5 = (bf16[2,512,64]{1,2,0:T(8,128)(2,1)S(1)}, bf16[2,512,64]{1,2,0:T(8,128)(2,1)S(1)}, u32[]{:S(2)}, u32[]{:S(2)}) collective-permute-start(bf16[2,512,64]{1,2,0:T(8,128)(2,1)S(1)} %copy.23), channel_id=1, source_target_pairs={{0,6},{2,4},{4,2},{6,0},{8,14},{10,12},{12,10},{14,8},{1,7},{3,5},... | collective-permute-start | bytes 393224 | tf_op jit(solution)/shard_map/ppermute | solution.py:244
  61.9 8.6 %collective-permute-start.6 = (bf16[2,512,64]{1,2,0:T(8,128)(2,1)S(1)}, bf16[2,512,64]{1,2,0:T(8,128)(2,1)S(1)}, u32[]{:S(2)}, u32[]{:S(2)}) collective-permute-start(bf16[2,512,64]{1,2,0:T(8,128)(2,1)S(1)} %copy.25), channel_id=1, source_target_pairs={{0,2},{2,0},{4,6},{6,4},{8,10},{10,8},{12,14},{14,12},{1,3},{3,1},... | collective-permute-start | bytes 393224 | tf_op jit(solution)/shard_map/ppermute | solution.py:244
